TPU v7x, 32 devices: a whole 2x2x4 slice. The times are simulated.
32 devices in a mesh: snp: 8 (over z, y), ind: 4 (over x, core).
Axes of the slice: x: 2, y: 2, z: 4, core: 2. Of those that a mesh axis runs over, the one named last changes fastest.
Arguments:
- beta_hat: float32 [64, 8192], P('ind', 'snp'), may hold values from -8 to 8
- ld_band: float32 [8192, 1024], P('snp'), as said below
- band_start: int32 [64], P('snp'), may hold values from -480 to 7648, as said below
- heritability: float32 [64], P('ind'), may hold values from 0.2 to 0.6
- genotypes: bfloat16 [4096, 8192], P('ind', 'snp'), may hold values from 0 to 2, as said below
Outputs:
- weights: float32 [64, 8192], P('ind', 'snp')
- scores: float32 [64, 4096], P(None, ('ind', 'snp'))
Inputs may be any that keep to these rules, and one draw needn't show every extreme that they name: ld_band is a symmetric matrix R in band form: entry k of row i is R[i, band_start[i // 128] + k]; R[i, i] = 1; R[i, j] = 0 when |i - j| > 416 or j lies outside the SNPs; the off-diagonal magnitudes of a row sum to 2.5 at most. `band_start`: block b's window starts at 128 * b - 416 - k with k from 0 to 64; the first block has k = 64 and the last block k = 0. `genotypes`: dosages are 0, 1 or 2.
All inputs are finite; a program needn't handle non-finite values.
Results may differ from a plain program's by a relative error of at most 0.0021.
Values may be sent and summed in bfloat16 or wider, within the bound.
No kernel may reach another device: no remote copies, remote signals or barrier semaphores. Data moves between devices by JAX's collectives and lax.ppermute only.
A program may use at most 64 MiB of HBM per device.

v0:
```python
import jax
import jax.numpy as jnp
from jax import lax
from jax.sharding import PartitionSpec as P

BLK = 128
ITERS = 2
M_GENOME = 1100000
N_GWAS = 1000000


def padded_2(block, sides, width):
    for axis, dim in sides:
        count = lax.axis_size(axis)
        forward = [(i, i + 1) for i in range(count - 1)]
        backward = [(target, source) for source, target in forward]
        low = lax.ppermute(
            lax.slice_in_dim(block, block.shape[dim] - width, None, axis=dim), axis, forward
        )
        high = lax.ppermute(lax.slice_in_dim(block, 0, width, axis=dim), axis, backward)
        block = jnp.concatenate([low, block, high], axis=dim)
    return block


def apply_operator(vector, ld_band, band_start, ridge_shift):
    band_cols = ld_band.shape[1]
    halo_cols = band_cols - BLK
    padded = padded_2(vector, (("snp", 1),), halo_cols)
    local_rows = vector.shape[1]
    offsets = band_start - lax.axis_index("snp") * local_rows + halo_cols
    windows = jax.vmap(lambda row_begin: lax.dynamic_slice_in_dim(padded, row_begin, band_cols, 1))(
        offsets
    )
    blocks = ld_band.reshape(band_start.shape[0], BLK, band_cols)
    product = jnp.einsum("btk,brk->tbr", windows, blocks, precision=lax.Precision.HIGHEST)
    return product.reshape(vector.shape) + ridge_shift[:, None] * vector


def paired_sums(residual, product):
    return lax.psum(
        (jnp.sum(residual * residual, axis=1), jnp.sum(residual * product, axis=1)), "snp"
    )


def local(beta_hat, ld_band, band_start, heritability, genotypes):
    ridge_shift = M_GENOME / N_GWAS / heritability
    weights = jnp.zeros_like(beta_hat)
    residual = beta_hat
    product = apply_operator(residual, ld_band, band_start, ridge_shift)
    norm_now, mixed = paired_sums(residual, product)
    step_size = norm_now / mixed
    direction = residual
    along = product
    for turn_index in range(ITERS):
        weights = weights + step_size[:, None] * direction
        residual = residual - step_size[:, None] * along
        if turn_index + 1 < ITERS:
            product = apply_operator(residual, ld_band, band_start, ridge_shift)
            norm_next, mixed = paired_sums(residual, product)
            ratio_new = norm_next / norm_now
            step_size = norm_next / (mixed - ratio_new * norm_next / step_size)
            direction = residual + ratio_new[:, None] * direction
            along = product + ratio_new[:, None] * along
            norm_now = norm_next
    rounded = weights.astype(jnp.bfloat16)
    partial_scores = lax.dot_general(
        lax.all_gather(rounded, "ind", axis=0, tiled=True),
        genotypes,
        (((1,), (1,)), ((), ())),
        preferred_element_type=jnp.float32,
    )
    complete = lax.psum(partial_scores, "snp")
    count = complete.shape[1] * lax.axis_size("ind")
    summed = lax.psum(jnp.sum(complete, axis=1), "ind")
    average = summed / count
    centred = complete - average[:, None]
    variance = lax.psum(jnp.sum(centred * centred, axis=1), "ind") / count
    share_cols = complete.shape[1] // lax.axis_size("snp")
    own_part = lax.dynamic_slice_in_dim(centred, lax.axis_index("snp") * share_cols, share_cols, 1)
    scores = own_part * lax.rsqrt(variance + 1e-05)[:, None]
    return (weights, scores)


def solution(mesh):
    placed = (P("ind", "snp"), P("snp", None), P("snp"), P("ind"), P("ind", "snp"))
    return jax.shard_map(
        local,
        mesh=mesh,
        in_specs=placed,
        out_specs=(P("ind", "snp"), P(None, ("ind", "snp"))),
        check_vma=False,
    )
```

profile of v0, /device:TPU:0, one launch (start us, length us, event | category | flops | bytes accessed | tf_op | source)
XLA Modules:
  0.0 196.7 jit_solution(16912710394377717429)
XLA Ops:
  7.2 1.0 fusion.5
  8.2 4.9 %collective-permute-start = (f32[16,896]{1,0:T(8,128)S(1)}, f32[16,896]{1,0:T(8,128)S(1)}, u32[]{:S(2)}, u32[]{:S(2)}) collective-permute-start(f32[16,896]{1,0:T(8,128)S(1)} %get-tuple-element.50), channel_id=1, source_target_pairs={{0,4},{4,8},{8,12},{12,16},{16,20},{20,24},{24,28},{1,5},{5,9},{9,... | collective-permute-start | bytes 172040 | tf_op jit(solution)/shard_map/ppermute | solution.py:17
  13.1 1.3 collective-permute-start.1
  14.4 0.7 broadcast_divide_fusion
  15.1 0.7 fusion.2
  15.8 3.4 %collective-permute-done.1 = f32[16,896]{1,0:T(8,128)S(1)} collective-permute-done((f32[16,896]{1,0:T(8,128)S(1)}, f32[16,896]{1,0:T(8,128)S(1)}, u32[]{:S(2)}, u32[]{:S(2)}) %collective-permute-start.1) | collective-permute-done | bytes 57376 | tf_op jit(solution)/shard_map/ppermute | solution.py:20
  19.2 0.9 pad_maximum_fusion
  20.1 10.6 %while.2 = (s32[]{:T(128)}, f32[16,2816]{1,0:T(8,128)S(1)}, s32[8,2]{0,1:T(2,128)S(1)}, f32[8,16,1024]{2,1,0:T(8,128)S(1)}, s32[]{:T(128)}) while((s32[]{:T(128)}, f32[16,2816]{1,0:T(8,128)S(1)}, s32[8,2]{0,1:T(2,128)S(1)}, f32[8,16,1024]{2,1,0:T(8,128)S(1)}, s32[]{:T(128)}) %tuple.38), condition=%wide.while_cond, body=%wide.while_body.sunk | while | flops 2 | bytes 131169 | solution.py:31
  20.7 0.7 bitcast_dynamic-update-slice_fusion.4
  22.0 0.7 bitcast_dynamic-update-slice_fusion.4
  22.8 0.5 slice.46
  23.4 0.7 bitcast_dynamic-update-slice_fusion.4
  24.2 0.5 slice.46
  24.7 0.7 bitcast_dynamic-update-slice_fusion.4
  25.5 0.5 slice.46
  26.0 0.7 bitcast_dynamic-update-slice_fusion.4
  26.8 0.5 slice.46
  27.3 0.7 bitcast_dynamic-update-slice_fusion.4
  28.1 0.5 slice.46
  28.7 0.7 bitcast_dynamic-update-slice_fusion.4
  29.5 0.5 slice.46
  30.0 0.7 bitcast_dynamic-update-slice_fusion.4
  30.7 5.3 %convolution_bitcast_fusion.1 = f32[8,2,8,128]{3,2,1,0:T(8,128)S(1)} fusion(f32[8,16,1024]{2,1,0:T(8,128)S(1)} %get-tuple-element.9, f32[8,128,1024]{2,1,0:T(8,128)} %bitcast.41), kind=kOutput, calls=%fused_computation.5 | convolution fusion | flops 201326592 | bytes 4784128 | tf_op jit(solution)/shard_map/btk,brk->tbr/dot_general | solution.py:35
  36.2 19.8 %all-reduce.2 = (f32[16]{0:T(128)S(1)}, f32[16]{0:T(128)S(1)}) all-reduce(f32[16]{0:T(128)S(1)} %get-tuple-element.21, f32[16]{0:T(128)S(1)} %get-tuple-element.20), channel_id=1, replica_groups=mesh['snp'=8,'ind'=4] {'snp'}, use_global_device_ids=true, to_apply=%region_1.0 | all-reduce | flops 32 | bytes 256 | tf_op jit(solution)/shard_map/psum | solution.py:40
  56.2 1.6 collective-permute-start.2
  57.8 1.3 collective-permute-start.3
  59.6 4.3 %collective-permute-done.3 = f32[16,896]{1,0:T(8,128)S(1)} collective-permute-done((f32[16,896]{1,0:T(8,128)S(1)}, f32[16,896]{1,0:T(8,128)S(1)}, u32[]{:S(2)}, u32[]{:S(2)}) %collective-permute-start.3) | collective-permute-done | bytes 57376 | tf_op jit(solution)/shard_map/ppermute | solution.py:20
  63.9 10.6 %while.3 = (s32[]{:T(128)}, f32[16,2816]{1,0:T(8,128)S(1)}, s32[8,2]{0,1:T(2,128)S(1)}, f32[8,16,1024]{2,1,0:T(8,128)S(1)}, s32[]{:T(128)}) while((s32[]{:T(128)}, f32[16,2816]{1,0:T(8,128)S(1)}, s32[8,2]{0,1:T(2,128)S(1)}, f32[8,16,1024]{2,1,0:T(8,128)S(1)}, s32[]{:T(128)}) %tuple.46), condition=%wide.while_cond.1, body=%wide.while_body.1.sunk | while | flops 2 | bytes 131169 | solution.py:31
  64.5 0.7 bitcast_dynamic-update-slice_fusion.5
  65.3 0.5 slice.47
  65.8 0.7 bitcast_dynamic-update-slice_fusion.5
  67.2 0.7 bitcast_dynamic-update-slice_fusion.5
  68.5 0.7 bitcast_dynamic-update-slice_fusion.5
  69.8 0.7 bitcast_dynamic-update-slice_fusion.5
  71.1 0.7 bitcast_dynamic-update-slice_fusion.5
  72.5 0.7 bitcast_dynamic-update-slice_fusion.5
  73.8 0.7 bitcast_dynamic-update-slice_fusion.5
  74.5 5.3 %convolution_bitcast_fusion = f32[8,2,8,128]{3,2,1,0:T(8,128)S(1)} fusion(f32[8,16,1024]{2,1,0:T(8,128)S(1)} %get-tuple-element.17, f32[8,128,1024]{2,1,0:T(8,128)} %bitcast.42), kind=kOutput, calls=%fused_computation.4 | convolution fusion | flops 201326592 | bytes 4784128 | tf_op jit(solution)/shard_map/btk,brk->tbr/dot_general | solution.py:35
  80.0 18.6 %all-reduce.1 = (f32[16]{0:T(128)S(1)}, f32[16]{0:T(128)S(1)}) all-reduce(f32[16]{0:T(128)S(1)} %get-tuple-element.19, f32[16]{0:T(128)S(1)} %get-tuple-element.18), channel_id=1, replica_groups=mesh['snp'=8,'ind'=4] {'snp'}, use_global_device_ids=true, to_apply=%region_5.0 | all-reduce | flops 32 | bytes 256 | tf_op jit(solution)/shard_map/psum | solution.py:40
  98.6 0.7 fusion.3
  99.3 5.4 %all_gather.3 = bf16[64,1024]{1,0:T(8,128)(2,1)S(1)} all-gather(bf16[16,1024]{1,0:T(8,128)(2,1)S(1)} %get-tuple-element.44), channel_id=1, replica_groups=mesh['snp'=8,'ind'=4] {'ind'}, dimensions={0}, use_global_device_ids=true | all-gather | bytes 163840 | tf_op jit(solution)/shard_map/all_gather | solution.py:67
  104.7 1.5 fusion.6
  106.2 68.5 %all-reduce.5.cloned.1.call-done = f32[64,1024]{1,0:T(8,128)} async-done(((f32[64,1024]{1,0:T(8,128)}), f32[64,1024]{1,0:T(8,128)}) %all-reduce.5.cloned.1.call-update) | async-done | bytes 262160 | tf_op jit(solution)/shard_map/psum | solution.py:72
  174.7 1.1 reduce_sum.58
  175.8 5.7 %psum.54 = f32[64]{0:T(128)S(1)} all-reduce(f32[64]{0:T(128)S(1)} %reduce_sum.58), channel_id=1, replica_groups=mesh['snp'=8,'ind'=4] {'ind'}, use_global_device_ids=true, to_apply=%region_10.0 | all-reduce | flops 64 | bytes 512 | tf_op jit(solution)/shard_map/psum | solution.py:74
  181.4 1.1 multiply_reduce_fusion
  182.6 6.6 %psum.55 = f32[64]{0:T(128)S(1)} all-reduce(f32[64]{0:T(128)S(1)} %get-tuple-element.42), channel_id=1, replica_groups=mesh['snp'=8,'ind'=4] {'ind'}, use_global_device_ids=true, to_apply=%region_12.0 | all-reduce | flops 64 | bytes 512 | tf_op jit(solution)/shard_map/psum | solution.py:77
  189.2 0.7 dynamic-slice_multiply_fusion
  (45 shorter events, 7.1 us)
Async XLA Ops:
  7.2 97.5 %copy-start = (bf16[1024,1024]{1,0:T(8,128)(2,1)S(1)}, bf16[1024,1024]{1,0:T(8,128)(2,1)}, u32[]{:S(2)}) copy-start(bf16[1024,1024]{1,0:T(8,128)(2,1)} %param.9) | copy-start | bytes 6291460
  7.2 28.8 %copy-start.1 = (f32[16,1024]{1,0:T(8,128)S(1)}, f32[16,1024]{1,0:T(8,128)}, u32[]{:S(2)}) copy-start(f32[16,1024]{1,0:T(8,128)} %param.5) | copy-start | bytes 196612
  7.2 167.5 %all-reduce.5.cloned.1.call-start = ((), (), s32[]{:S(2)}) async-start(), calls=%async_computation | async-start | bytes 524288 | tf_op jit(solution)/shard_map/psum | solution.py:72
  8.2 7.5 %collective-permute-start = (f32[16,896]{1,0:T(8,128)S(1)}, f32[16,896]{1,0:T(8,128)S(1)}, u32[]{:S(2)}, u32[]{:S(2)}) collective-permute-start(f32[16,896]{1,0:T(8,128)S(1)} %get-tuple-element.50), channel_id=1, source_target_pairs={{0,4},{4,8},{8,12},{12,16},{16,20},{20,24},{24,28},{1,5},{5,9},{9,... | collective-permute-start | bytes 172040 | tf_op jit(solution)/shard_map/ppermute | solution.py:17
  13.1 6.1 %collective-permute-start.1 = (f32[16,896]{1,0:T(8,128)S(1)}, f32[16,896]{1,0:T(8,128)S(1)}, u32[]{:S(2)}, u32[]{:S(2)}) collective-permute-start(f32[16,896]{1,0:T(8,128)S(1)} %get-tuple-element.51), channel_id=1, source_target_pairs={{4,0},{8,4},{12,8},{16,12},{20,16},{24,20},{28,24},{5,1},{9,5},{13... | collective-permute-start | bytes 172040 | tf_op jit(solution)/shard_map/ppermute | solution.py:20
  56.2 3.4 %collective-permute-start.2 = (f32[16,896]{1,0:T(8,128)S(1)}, f32[16,896]{1,0:T(8,128)S(1)}, u32[]{:S(2)}, u32[]{:S(2)}) collective-permute-start(f32[16,896]{1,0:T(8,128)S(1)} %get-tuple-element.48), channel_id=1, source_target_pairs={{0,4},{4,8},{8,12},{12,16},{16,20},{20,24},{24,28},{1,5},{5,9},{9,... | collective-permute-start | bytes 172040 | tf_op jit(solution)/shard_map/ppermute | solution.py:17
  57.8 6.1 %collective-permute-start.3 = (f32[16,896]{1,0:T(8,128)S(1)}, f32[16,896]{1,0:T(8,128)S(1)}, u32[]{:S(2)}, u32[]{:S(2)}) collective-permute-start(f32[16,896]{1,0:T(8,128)S(1)} %get-tuple-element.49), channel_id=1, source_target_pairs={{4,0},{8,4},{12,8},{16,12},{20,16},{24,20},{28,24},{5,1},{9,5},{13... | collective-permute-start | bytes 172040 | tf_op jit(solution)/shard_map/ppermute | solution.py:20
Sparse Core Ops, SparseCore 0:
  106.3 68.3 all-reduce.4
where the time goes:
time: 197 us
  waiting for transfers between devices  76.7 us (39%)
  blocking collectives  56.1 us (28%)
  local copies, waits for them, and re-layouts  22.3 us (11%)
  between operations  14.1 us (7%)
  matrix products  12 us (6%)
  starting transfers between devices  9.11 us (5%)
  other arithmetic  6.34 us (3%)
    psum x1, waiting for transfers between devices, local(): complete = lax.psum(partial_scores, 'snp')  68.5 us
    psum x2, blocking collectives, paired_sums(): lax.psum((jnp.sum(residual * residual, axis=1), jnp.sum(residual * produc...  38.4 us
    gather x48, local copies, waits for them, and re-layouts  21.1 us
    dot_general x2, matrix products, apply_operator(): jnp.einsum('btk,brk->tbr', windows, blocks, precision=lax.Precision.HIGHEST)  10.6 us
    ppermute x2, waiting for transfers between devices, padded_2(): lax.ppermute(lax.slice_in_dim(block, 0, width, axis=dim), axis, backward)  7.69 us
    psum x1, blocking collectives, local(): variance = lax.psum(jnp.sum(centred * centred, axis=1), 'ind') / count  6.6 us
    ppermute x2, starting transfers between devices, padded_2(): lax.ppermute(lax.slice_in_dim(block, block.shape[dim] - width, None, axis...  6.49 us
    psum x1, blocking collectives, local(): summed = lax.psum(jnp.sum(complete, axis=1), 'ind')  5.67 us
  transfers between devices with their start and end apart: 5, of which 4 were waited for; matrix products, arithmetic and copies ran while one was open for 1% of the time, Pallas kernels for 0%

commit v1 on v0

v1 whole, which is shorter than its diff:
```python
import jax
import jax.numpy as jnp
from jax import lax
from jax.sharding import PartitionSpec as P

BLK = 128
ITERS = 2
M_GENOME = 1100000
N_GWAS = 1000000
REACH = 416
SHIFT_BITS = 7


def all_sum(x, axes, count):
    sent = jnp.broadcast_to(x[None], (count,) + x.shape)
    return jnp.sum(lax.all_to_all(sent, axes, 0, 0, tiled=True), axis=0)


def with_halo(block, width):
    count = lax.axis_size("snp")
    forward = [(i, i + 1) for i in range(count - 1)]
    backward = [(target, source) for source, target in forward]
    low = lax.ppermute(block[:, block.shape[1] - width :], "snp", forward)
    high = lax.ppermute(block[:, :width], "snp", backward)
    return jnp.concatenate([low, block, high], axis=1)


def apply_operator(vector, ld_band, shifts, ridge_shift, halo):
    band_cols = ld_band.shape[1]
    blocks_here = ld_band.shape[0] // BLK
    span = band_cols + (1 << SHIFT_BITS) - 1
    padded = with_halo(vector, halo)
    need = (blocks_here - 1) * BLK + span
    padded = jnp.pad(padded, ((0, 0), (0, max(0, need - padded.shape[1]))))
    wide = jnp.stack([padded[:, b * BLK : b * BLK + span] for b in range(blocks_here)])
    for bit in range(SHIFT_BITS):
        step = 1 << bit
        take = ((shifts >> bit) & 1)[:, None, None] == 1
        wide = jnp.where(take, wide[:, :, step:], wide[:, :, :-step])
    windows = wide[:, :, :band_cols]
    blocks = ld_band.reshape(blocks_here, BLK, band_cols)
    product = jnp.einsum("btk,brk->tbr", windows, blocks, precision=lax.Precision.HIGHEST)
    return product.reshape(vector.shape) + ridge_shift[:, None] * vector


def local(beta_hat, ld_band, band_start, heritability, genotypes):
    n_snp = lax.axis_size("snp")
    n_ind = lax.axis_size("ind")
    n_all = n_snp * n_ind
    me_ind = lax.axis_index("ind")
    traits_here, rows_here = beta_hat.shape
    traits = traits_here * n_ind
    halo = ld_band.shape[1] - BLK - REACH
    offsets = band_start - lax.axis_index("snp") * rows_here + halo
    shifts = offsets - jnp.arange(band_start.shape[0], dtype=jnp.int32) * BLK

    ridge_shift = M_GENOME / N_GWAS / heritability
    colsum = jnp.sum(genotypes.astype(jnp.float32), axis=0)
    colsum = all_sum(colsum, "ind", n_ind)
    beta_all = lax.all_gather(beta_hat, "ind", axis=0, tiled=True)

    image = apply_operator(beta_hat, ld_band, shifts, ridge_shift, halo)
    image_all = lax.all_gather(image, "ind", axis=0, tiled=True)
    image2 = apply_operator(image, ld_band, shifts, ridge_shift, halo)

    moments = jnp.stack(
        [
            jnp.sum(beta_hat * beta_hat, axis=1),
            jnp.sum(beta_hat * image, axis=1),
            jnp.sum(image * image, axis=1),
            jnp.sum(image * image2, axis=1),
        ]
    )
    placed = jnp.zeros((4, traits), jnp.float32)
    placed = lax.dynamic_update_slice_in_dim(placed, moments, me_ind * traits_here, 1)
    m0, m1, m2, m3 = all_sum(placed, ("ind", "snp"), n_all)

    alpha1 = m0 / m1
    norm1 = alpha1 * alpha1 * m2 - m0
    ratio = norm1 / m0
    grow = 1.0 + ratio
    curv = grow * grow * m1 - 2.0 * grow * alpha1 * m2 + alpha1 * alpha1 * m3
    alpha2 = norm1 / curv
    residual = beta_all - alpha1[:, None] * image_all
    direction = residual + ratio[:, None] * beta_all
    weights_all = alpha1[:, None] * beta_all + alpha2[:, None] * direction
    weights = lax.dynamic_slice_in_dim(weights_all, me_ind * traits_here, traits_here, 0)

    rounded = weights_all.astype(jnp.bfloat16)
    partial = lax.dot_general(
        rounded, genotypes, (((1,), (1,)), ((), ())), preferred_element_type=jnp.float32
    )
    mean_part = jnp.sum(rounded.astype(jnp.float32) * colsum[None, :], axis=1)
    inds_here = genotypes.shape[0]
    share = inds_here // n_snp
    chunks = partial.reshape(traits, n_snp, share).transpose(1, 0, 2).reshape(n_snp, traits * share)
    extra = jnp.broadcast_to(jnp.pad(mean_part, (0, 128 - traits % 128 if traits % 128 else 0))[None], (n_snp, -(-traits // 128) * 128))
    sent = jnp.concatenate([chunks, extra], axis=1).reshape(n_snp, -1, 128)
    got = jnp.sum(lax.all_to_all(sent, "snp", 0, 0, tiled=True), axis=0).reshape(-1)
    complete = got[: traits * share].reshape(traits, share)
    count = inds_here * n_ind
    average = got[traits * share : traits * share + traits] / count
    centred = complete - average[:, None]
    variance = all_sum(jnp.sum(centred * centred, axis=1), ("ind", "snp"), n_all) / count
    scores = centred * lax.rsqrt(variance + 1e-05)[:, None]
    return (weights, scores)


def solution(mesh):
    placed = (P("ind", "snp"), P("snp", None), P("snp"), P("ind"), P("ind", "snp"))
    return jax.shard_map(
        local,
        mesh=mesh,
        in_specs=placed,
        out_specs=(P("ind", "snp"), P(None, ("ind", "snp"))),
        check_vma=False,
    )
```

time: 197 us -> 94.3 us (0.48)
  waiting for transfers between devices: 76.7 us -> 12.3 us
  blocking collectives: 56.1 us -> 27.4 us
  starting transfers between devices: 9.11 us -> 24.5 us
  local copies, waits for them, and re-layouts: 22.3 us -> 8.63 us
  between operations: 14.1 us -> 1 us
  other arithmetic: 6.34 us -> 11.5 us
  matrix products: 12 us -> 8.08 us
    psum x1 -> x0, waiting for transfers between devices: 68.5 us -> none  [local(): complete = lax.psum(partial_scores, 'snp')]
    psum x4 -> x0, blocking collectives: 50.7 us -> none  [the longest x2 38.4 us: paired_sums(): lax.psum((jnp.sum(residual * residual, axis=1), jnp.sum(residual * produc...]
    gather x48 -> x0, local copies, waits for them, and re-layouts: 21.1 us -> none
    all_to_all x0 -> x1, blocking collectives: none -> 15.1 us  [local(): lax.all_to_all(sent, 'snp', 0, 0, tiled=True)]
    all_to_all x0 -> x3, starting transfers between devices: none -> 12.5 us  [all_sum(): return jnp.sum(lax.all_to_all(sent, axes, 0, 0, tiled=True), axis=0)]
    all_to_all x0 -> x3, waiting for transfers between devices: none -> 7.48 us  [all_sum(): return jnp.sum(lax.all_to_all(sent, axes, 0, 0, tiled=True), axis=0)]
    all_gather x1 -> x2, blocking collectives: 5.4 us -> 12.4 us  [the longest x1 6.23 us: local(): beta_all = lax.all_gather(beta_hat, 'ind', axis=0, tiled=True)]
    unnamed x6 -> x17, local copies, waits for them, and re-layouts: 0.1 us -> 4.03 us
  transfers between devices with their start and end apart: 5 -> 7, of which waited for: 4 -> 3; matrix products, arithmetic and copies ran while one was open for 1% -> 16% of each run, Pallas kernels for 0% -> 0%
where the time goes in v1:
time: 94.3 us; the launch traced here: 93.5 us
  blocking collectives  27.4 us (29%)
  starting transfers between devices  24.5 us (26%)
  waiting for transfers between devices  12.3 us (13%)
  other arithmetic  11.5 us (12%)
  local copies, waits for them, and re-layouts  8.63 us (9%)
  matrix products  8.08 us (9%)
  between operations  1 us (1%)
    all_to_all x1, blocking collectives, local(): lax.all_to_all(sent, 'snp', 0, 0, tiled=True)  15.1 us
    all_to_all x3, starting transfers between devices, all_sum(): return jnp.sum(lax.all_to_all(sent, axes, 0, 0, tiled=True), axis=0)  12.5 us
    ppermute x2, starting transfers between devices, with_halo(): low = lax.ppermute(block[:, block.shape[1] - width:], 'snp', forward)  9.44 us
    all_to_all x3, waiting for transfers between devices, all_sum(): return jnp.sum(lax.all_to_all(sent, axes, 0, 0, tiled=True), axis=0)  7.48 us
    dot_general x2, matrix products, apply_operator(): jnp.einsum('btk,brk->tbr', windows, blocks, precision=lax.Precision.HIGHEST)  7.32 us
    all_gather x1, blocking collectives, local(): beta_all = lax.all_gather(beta_hat, 'ind', axis=0, tiled=True)  6.23 us
    all_gather x1, blocking collectives, local(): image_all = lax.all_gather(image, 'ind', axis=0, tiled=True)  6.14 us
    ppermute x2, waiting for transfers between devices, with_halo(): high = lax.ppermute(block[:, :width], 'snp', backward)  4.84 us
  transfers between devices with their start and end apart: 7, of which 3 were waited for; matrix products, arithmetic and copies ran while one was open for 16% of the time, Pallas kernels for 0%

profile of v1, /device:TPU:0, one launch (start us, length us, event | category | flops | bytes accessed | tf_op | source)
XLA Modules:
  0.0 93.5 jit_solution(7003058788836734256)
XLA Ops:
  0.6 0.9 fusion.46
  1.5 4.9 %collective-permute-start = (f32[16,480]{1,0:T(8,128)S(1)}, f32[16,480]{1,0:T(8,128)S(1)}, u32[]{:S(2)}, u32[]{:S(2)}) collective-permute-start(f32[16,480]{1,0:T(8,128)S(1)} %get-tuple-element.16), channel_id=1, source_target_pairs={{0,4},{4,8},{8,12},{12,16},{16,20},{20,24},{24,28},{1,5},{5,9},{9,... | collective-permute-start | bytes 92168 | tf_op jit(solution)/shard_map/ppermute | solution.py:23
  6.4 1.3 %collective-permute-start.1 = (f32[16,480]{1,0:T(8,128)S(1)}, f32[16,480]{1,0:T(8,128)S(1)}, u32[]{:S(2)}, u32[]{:S(2)}) collective-permute-start(f32[16,480]{1,0:T(8,128)S(1)} %get-tuple-element.15), channel_id=1, source_target_pairs={{4,0},{8,4},{12,8},{16,12},{20,16},{24,20},{28,24},{5,1},{9,5},{13... | collective-permute-start | bytes 92168 | tf_op jit(solution)/shard_map/ppermute | solution.py:24
  7.7 2.0 %convert_reduce_fusion = f32[1024]{0:T(1024)S(1)} fusion(bf16[1024,1024]{1,0:T(8,128)(2,1)} %param.9), kind=kLoop, calls=%fused_computation | loop fusion | flops 2096128 | bytes 2101248 | tf_op jit(solution)/shard_map/reduce_sum | solution.py:58
  9.6 0.6 broadcast_in_dim.136
  10.3 3.3 %all-to-all-start.1 = ((f32[4,1,1024]{2,1,0:T(1,128)}), f32[4,1,1024]{2,1,0:T(1,128)S(1)}, u32[]{:S(2)}, u32[]{:S(2)}) async-start(f32[4,1,1024]{2,1,0:T(1,128)} %broadcast_in_dim.136), calls=%async_computation.1 | async-start | bytes 32768 | tf_op jit(solution)/shard_map/all_to_all | solution.py:16
  13.5 0.7 and_compare_fusion.6
  14.2 0.7 broadcast_divide_fusion
  14.9 0.8 constant_dynamic-update-slice_fusion.1
  15.7 0.9 fusion.21
  16.6 0.9 fusion.18
  17.5 0.9 fusion.36
  18.4 0.9 %concatenate.30 = f32[16,1984]{1,0:T(8,128)S(1)} concatenate(f32[16,480]{1,0:T(8,128)S(1)} %collective-permute-done, f32[16,1024]{1,0:T(8,128)} %param.5, f32[16,480]{1,0:T(8,128)S(1)} %collective-permute-done.1), dimensions={1} | concatenate | bytes 253952 | tf_op jit(solution)/shard_map/concatenate | solution.py:25
  19.7 0.2 slice_select_fusion.11
  19.9 0.2 slice_select_fusion.10
  20.2 0.2 slice_select_fusion.9
  20.4 0.2 slice_select_fusion.8
  20.6 0.2 slice_select_fusion.7
  20.9 0.2 slice_select_fusion.6
  21.1 1.0 %copy-done = f32[1024,1024]{1,0:T(8,128)S(1)} copy-done((f32[1024,1024]{1,0:T(8,128)S(1)}, f32[1024,1024]{1,0:T(8,128)}, u32[]{:S(2)}) %copy-start) | copy-done | bytes 4194328
  22.1 3.7 %convolution_bitcast_fusion.2 = f32[8,2,8,128]{3,2,1,0:T(8,128)S(1)} fusion(f32[8,128,1024]{2,1,0:T(8,128)S(1)} %bitcast.133, f32[8,16,1088]{2,1,0:T(8,128)S(1)} %slice_select_fusion.6, pred[8]{0:T(512)(128)(4,1)S(1)} %get-tuple-element.11), kind=kOutput, calls=%fused_computation.3 | convolution fusion | flops 201457664 | bytes 5308928 | tf_op jit(solution)/shard_map/btk,brk->tbr/dot_general | solution.py:42
  25.9 4.5 %collective-permute-start.2 = (f32[16,480]{1,0:T(8,128)S(1)}, f32[16,480]{1,0:T(8,128)S(1)}, u32[]{:S(2)}, u32[]{:S(2)}) collective-permute-start(f32[16,480]{1,0:T(8,128)S(1)} %get-tuple-element.14), channel_id=1, source_target_pairs={{0,4},{4,8},{8,12},{12,16},{16,20},{20,24},{24,28},{1,5},{5,9},{9,... | collective-permute-start | bytes 92168 | tf_op jit(solution)/shard_map/ppermute | solution.py:23
  30.5 6.2 %all_gather.6 = f32[64,1024]{1,0:T(8,128)S(1)} all-gather(f32[16,1024]{1,0:T(8,128)S(1)} %copy-done.3), channel_id=1, replica_groups=mesh['snp'=8,'ind'=4] {'ind'}, dimensions={0}, use_global_device_ids=true | all-gather | bytes 327680 | tf_op jit(solution)/shard_map/all_gather | solution.py:60
  36.8 1.3 %collective-permute-start.3 = (f32[16,480]{1,0:T(8,128)S(1)}, f32[16,480]{1,0:T(8,128)S(1)}, u32[]{:S(2)}, u32[]{:S(2)}) collective-permute-start(f32[16,480]{1,0:T(8,128)S(1)} %get-tuple-element.13), channel_id=1, source_target_pairs={{4,0},{8,4},{12,8},{16,12},{20,16},{24,20},{28,24},{5,1},{9,5},{13... | collective-permute-start | bytes 92168 | tf_op jit(solution)/shard_map/ppermute | solution.py:24
  38.1 4.8 %collective-permute-done.3 = f32[16,480]{1,0:T(8,128)S(1)} collective-permute-done((f32[16,480]{1,0:T(8,128)S(1)}, f32[16,480]{1,0:T(8,128)S(1)}, u32[]{:S(2)}, u32[]{:S(2)}) %collective-permute-start.3) | collective-permute-done | bytes 30752 | tf_op jit(solution)/shard_map/ppermute | solution.py:24
  43.6 0.2 slice_select_fusion.5
  43.8 0.2 slice_select_fusion.4
  44.0 0.2 slice_select_fusion.3
  44.3 0.2 slice_select_fusion.2
  44.5 0.2 slice_select_fusion.1
  44.7 0.2 slice_select_fusion
  45.0 1.0 %copy-done.1 = f32[1024,1024]{1,0:T(8,128)S(1)} copy-done((f32[1024,1024]{1,0:T(8,128)S(1)}, f32[1024,1024]{1,0:T(8,128)}, u32[]{:S(2)}) %copy-start.1) | copy-done | bytes 4194328
  46.0 3.7 %convolution_bitcast_fusion.1 = f32[8,2,8,128]{3,2,1,0:T(8,128)S(1)} fusion(f32[8,128,1024]{2,1,0:T(8,128)S(1)} %bitcast.134, f32[8,16,1088]{2,1,0:T(8,128)S(1)} %slice_select_fusion, pred[8]{0:T(512)(128)(4,1)S(1)} %get-tuple-element.11), kind=kOutput, calls=%fused_computation.2 | convolution fusion | flops 201457664 | bytes 5308928 | tf_op jit(solution)/shard_map/btk,brk->tbr/dot_general | solution.py:42
  49.6 0.2 multiply_reduce_fusion.3
  50.0 0.7 reshape.139
  50.8 6.4 %all-to-all-start = ((f32[32,1,256]{2,1,0:T(1,128)}), f32[32,1,256]{2,1,0:T(1,128)S(1)}, u32[]{:S(2)}, u32[]{:S(2)}) async-start(f32[32,1,256]{2,1,0:T(1,128)} %reshape.139), calls=%async_computation | async-start | bytes 65536 | tf_op jit(solution)/shard_map/all_to_all | solution.py:16
  57.1 6.1 %all_gather.7 = f32[64,1024]{1,0:T(8,128)S(1)} all-gather(f32[16,1024]{1,0:T(8,128)S(1)} %bitcast_add_fusion.1), channel_id=1, replica_groups=mesh['snp'=8,'ind'=4] {'ind'}, dimensions={0}, use_global_device_ids=true | all-gather | bytes 327680 | tf_op jit(solution)/shard_map/all_gather | solution.py:63
  63.3 1.0 %all-to-all-done = f32[32,1,256]{2,1,0:T(1,128)S(1)} async-done(((f32[32,1,256]{2,1,0:T(1,128)}), f32[32,1,256]{2,1,0:T(1,128)S(1)}, u32[]{:S(2)}, u32[]{:S(2)}) %all-to-all-start) | async-done | bytes 32800 | tf_op jit(solution)/shard_map/all_to_all | solution.py:16
  64.3 0.5 broadcast.122
  64.8 0.7 reduce.2
  65.7 0.3 multiply_reduce_fusion
  66.0 0.8 convolution_bitcast_fusion
  66.9 15.1 %all_to_all.22 = f32[8,65,128]{2,1,0:T(8,128)S(1)} all-to-all(f32[8,65,128]{2,1,0:T(8,128)S(1)} %copy.21), channel_id=1, replica_groups=mesh['snp'=8,'ind'=4] {'snp'}, dimensions={0} | all-to-all | bytes 532480 | tf_op jit(solution)/shard_map/all_to_all | solution.py:99
  82.2 0.6 broadcast_in_dim.138
  82.8 2.9 %all-to-all-start.3 = ((f32[32,1,64]{2,1,0:T(1,128)}), f32[32,1,64]{2,1,0:T(1,128)S(1)}, u32[]{:S(2)}, u32[]{:S(2)}) async-start(f32[32,1,64]{2,1,0:T(1,128)} %broadcast_in_dim.138), calls=%async_computation.3 | async-start | bytes 32768 | tf_op jit(solution)/shard_map/all_to_all | solution.py:16
  85.7 0.6 constant_dynamic-slice_fusion
  86.3 6.4 %all-to-all-done.3 = f32[32,1,64]{2,1,0:T(1,128)S(1)} async-done(((f32[32,1,64]{2,1,0:T(1,128)}), f32[32,1,64]{2,1,0:T(1,128)S(1)}, u32[]{:S(2)}, u32[]{:S(2)}) %all-to-all-start.3) | async-done | bytes 8224 | tf_op jit(solution)/shard_map/all_to_all | solution.py:16
  92.8 0.7 fusion.40
  (45 shorter events, 1.8 us)
Async XLA Ops:
  1.5 14.2 %collective-permute-start = (f32[16,480]{1,0:T(8,128)S(1)}, f32[16,480]{1,0:T(8,128)S(1)}, u32[]{:S(2)}, u32[]{:S(2)}) collective-permute-start(f32[16,480]{1,0:T(8,128)S(1)} %get-tuple-element.16), channel_id=1, source_target_pairs={{0,4},{4,8},{8,12},{12,16},{16,20},{20,24},{24,28},{1,5},{5,9},{9,... | collective-permute-start | bytes 92168 | tf_op jit(solution)/shard_map/ppermute | solution.py:23
  6.4 12.0 %collective-permute-start.1 = (f32[16,480]{1,0:T(8,128)S(1)}, f32[16,480]{1,0:T(8,128)S(1)}, u32[]{:S(2)}, u32[]{:S(2)}) collective-permute-start(f32[16,480]{1,0:T(8,128)S(1)} %get-tuple-element.15), channel_id=1, source_target_pairs={{4,0},{8,4},{12,8},{16,12},{20,16},{24,20},{28,24},{5,1},{9,5},{13... | collective-permute-start | bytes 92168 | tf_op jit(solution)/shard_map/ppermute | solution.py:24
  10.3 26.5 %all-to-all-start.1 = ((f32[4,1,1024]{2,1,0:T(1,128)}), f32[4,1,1024]{2,1,0:T(1,128)S(1)}, u32[]{:S(2)}, u32[]{:S(2)}) async-start(f32[4,1,1024]{2,1,0:T(1,128)} %broadcast_in_dim.136), calls=%async_computation.1 | async-start | bytes 32768 | tf_op jit(solution)/shard_map/all_to_all | solution.py:16
  19.9 2.2 %copy-start = (f32[1024,1024]{1,0:T(8,128)S(1)}, f32[1024,1024]{1,0:T(8,128)}, u32[]{:S(2)}) copy-start(f32[1024,1024]{1,0:T(8,128)} %param.6) | copy-start | bytes 12582916
  20.6 5.1 %copy-start.3 = (f32[16,1024]{1,0:T(8,128)S(1)}, f32[16,1024]{1,0:T(8,128)}, u32[]{:S(2)}) copy-start(f32[16,1024]{1,0:T(8,128)} %param.5) | copy-start | bytes 196612
  25.9 12.1 %collective-permute-start.2 = (f32[16,480]{1,0:T(8,128)S(1)}, f32[16,480]{1,0:T(8,128)S(1)}, u32[]{:S(2)}, u32[]{:S(2)}) collective-permute-start(f32[16,480]{1,0:T(8,128)S(1)} %get-tuple-element.14), channel_id=1, source_target_pairs={{0,4},{4,8},{8,12},{12,16},{16,20},{20,24},{24,28},{1,5},{5,9},{9,... | collective-permute-start | bytes 92168 | tf_op jit(solution)/shard_map/ppermute | solution.py:23
  36.8 6.2 %collective-permute-start.3 = (f32[16,480]{1,0:T(8,128)S(1)}, f32[16,480]{1,0:T(8,128)S(1)}, u32[]{:S(2)}, u32[]{:S(2)}) collective-permute-start(f32[16,480]{1,0:T(8,128)S(1)} %get-tuple-element.13), channel_id=1, source_target_pairs={{4,0},{8,4},{12,8},{16,12},{20,16},{24,20},{28,24},{5,1},{9,5},{13... | collective-permute-start | bytes 92168 | tf_op jit(solution)/shard_map/ppermute | solution.py:24
  43.8 2.2 %copy-start.1 = (f32[1024,1024]{1,0:T(8,128)S(1)}, f32[1024,1024]{1,0:T(8,128)}, u32[]{:S(2)}) copy-start(f32[1024,1024]{1,0:T(8,128)} %param.6) | copy-start | bytes 12582916
  44.7 21.3 %copy-start.2 = (bf16[1024,1024]{1,0:T(8,128)(2,1)S(1)}, bf16[1024,1024]{1,0:T(8,128)(2,1)}, u32[]{:S(2)}) copy-start(bf16[1024,1024]{1,0:T(8,128)(2,1)} %param.9) | copy-start | bytes 6291460
  50.8 13.6 %all-to-all-start = ((f32[32,1,256]{2,1,0:T(1,128)}), f32[32,1,256]{2,1,0:T(1,128)S(1)}, u32[]{:S(2)}, u32[]{:S(2)}) async-start(f32[32,1,256]{2,1,0:T(1,128)} %reshape.139), calls=%async_computation | async-start | bytes 65536 | tf_op jit(solution)/shard_map/all_to_all | solution.py:16
  82.8 9.9 %all-to-all-start.3 = ((f32[32,1,64]{2,1,0:T(1,128)}), f32[32,1,64]{2,1,0:T(1,128)S(1)}, u32[]{:S(2)}, u32[]{:S(2)}) async-start(f32[32,1,64]{2,1,0:T(1,128)} %broadcast_in_dim.138), calls=%async_computation.3 | async-start | bytes 32768 | tf_op jit(solution)/shard_map/all_to_all | solution.py:16

commit v2 on v1

--- a/solution.py
+++ b/solution.py
@@ -16,20 +16,8 @@
     return jnp.sum(lax.all_to_all(sent, axes, 0, 0, tiled=True), axis=0)
 
 
-def with_halo(block, width):
-    count = lax.axis_size("snp")
-    forward = [(i, i + 1) for i in range(count - 1)]
-    backward = [(target, source) for source, target in forward]
-    low = lax.ppermute(block[:, block.shape[1] - width :], "snp", forward)
-    high = lax.ppermute(block[:, :width], "snp", backward)
-    return jnp.concatenate([low, block, high], axis=1)
-
-
-def apply_operator(vector, ld_band, shifts, ridge_shift, halo):
-    band_cols = ld_band.shape[1]
-    blocks_here = ld_band.shape[0] // BLK
+def windows_of(padded, shifts, band_cols, blocks_here):
     span = band_cols + (1 << SHIFT_BITS) - 1
-    padded = with_halo(vector, halo)
     need = (blocks_here - 1) * BLK + span
     padded = jnp.pad(padded, ((0, 0), (0, max(0, need - padded.shape[1]))))
     wide = jnp.stack([padded[:, b * BLK : b * BLK + span] for b in range(blocks_here)])
@@ -37,10 +25,45 @@
         step = 1 << bit
         take = ((shifts >> bit) & 1)[:, None, None] == 1
         wide = jnp.where(take, wide[:, :, step:], wide[:, :, :-step])
-    windows = wide[:, :, :band_cols]
+    return wide[:, :, :band_cols]
+
+
+def apply_operator(extended, vector, ld_band, shifts, ridge_shift):
+    band_cols = ld_band.shape[1]
+    blocks_here = ld_band.shape[0] // BLK
+    windows = windows_of(extended, shifts, band_cols, blocks_here)
     blocks = ld_band.reshape(blocks_here, BLK, band_cols)
     product = jnp.einsum("btk,brk->tbr", windows, blocks, precision=lax.Precision.HIGHEST)
     return product.reshape(vector.shape) + ridge_shift[:, None] * vector
+
+
+def spread_operator(vector, ld_band, shifts, ridge_shift, halo):
+    band_cols = ld_band.shape[1]
+    blocks_here = ld_band.shape[0] // BLK
+    traits, rows = vector.shape
+    span = band_cols + (1 << SHIFT_BITS) - 1
+    blocks = ld_band.reshape(blocks_here, BLK, band_cols)
+    pieces = jnp.einsum(
+        "tbr,brk->btk", vector.reshape(traits, blocks_here, BLK), blocks,
+        precision=lax.Precision.HIGHEST,
+    )
+    wide = jnp.pad(pieces, ((0, 0), (0, 0), (0, span - band_cols)))
+    for bit in range(SHIFT_BITS):
+        step = 1 << bit
+        take = ((shifts >> bit) & 1)[:, None, None] == 1
+        moved = jnp.pad(wide, ((0, 0), (0, 0), (step, 0)))[:, :, :span]
+        wide = jnp.where(take, moved, wide)
+    width = max((blocks_here - 1) * BLK + span, rows + 2 * halo)
+    own = sum(
+        jnp.pad(wide[b], ((0, 0), (b * BLK, width - b * BLK - span))) for b in range(blocks_here)
+    )[:, : rows + 2 * halo]
+    own = own + jnp.pad(ridge_shift[:, None] * vector, ((0, 0), (halo, halo)))
+    count = lax.axis_size("snp")
+    forward = [(i, i + 1) for i in range(count - 1)]
+    backward = [(target, source) for source, target in forward]
+    from_left = lax.ppermute(own[:, rows:], "snp", forward)
+    from_right = lax.ppermute(own[:, : 2 * halo], "snp", backward)
+    return own + jnp.pad(from_left, ((0, 0), (0, rows))) + jnp.pad(from_right, ((0, 0), (rows, 0)))
 
 
 def local(beta_hat, ld_band, band_start, heritability, genotypes):
@@ -59,9 +82,10 @@
     colsum = all_sum(colsum, "ind", n_ind)
     beta_all = lax.all_gather(beta_hat, "ind", axis=0, tiled=True)
 
-    image = apply_operator(beta_hat, ld_band, shifts, ridge_shift, halo)
+    extended = spread_operator(beta_hat, ld_band, shifts, ridge_shift, halo)
+    image = extended[:, halo : halo + rows_here]
     image_all = lax.all_gather(image, "ind", axis=0, tiled=True)
-    image2 = apply_operator(image, ld_band, shifts, ridge_shift, halo)
+    image2 = apply_operator(extended, image, ld_band, shifts, ridge_shift)
 
     moments = jnp.stack(
         [

time: 94.3 us -> 75.2 us (0.80)
  starting transfers between devices: 24.5 us -> 19.4 us
  other arithmetic: 11.5 us -> 6.47 us
  waiting for transfers between devices: 12.3 us -> 7.48 us
  local copies, waits for them, and re-layouts: 8.63 us -> 4.68 us
    ppermute x4 -> x2, starting transfers between devices: 12 us -> 6.19 us  [the longest x1 4.9 us: spread_operator(): from_left = lax.ppermute(own[:, rows:], 'snp', forward)]
    ppermute x4 -> x2, waiting for transfers between devices: 4.85 us -> 0.01 us  [the longest x1 0.01 us: spread_operator(): from_left = lax.ppermute(own[:, rows:], 'snp', forward)]
    dot_general x0 -> x1, matrix products: none -> 3.87 us  [spread_operator(): jnp.einsum('tbr,brk->btk', vector.reshape(traits, blocks_here, BLK), bloc...]
    dot_general x2 -> x1, matrix products: 7.32 us -> 3.66 us  [apply_operator(): jnp.einsum('btk,brk->tbr', windows, blocks, precision=lax.Precision.HIGHEST)]
    unnamed x9 -> x0, other arithmetic: 3.18 us -> none
    unnamed x17 -> x18, local copies, waits for them, and re-layouts: 4.03 us -> 1.97 us
    reduce_sum x1, other arithmetic: 1.96 us -> 0.37 us  [local(): colsum = jnp.sum(genotypes.astype(jnp.float32), axis=0)]
    concatenate x3 -> x0, local copies, waits for them, and re-layouts: 1.05 us -> none  [with_halo(): return jnp.concatenate([low, block, high], axis=1)]
  transfers between devices with their start and end apart: 7 -> 5, of which waited for: 3 -> 2; matrix products, arithmetic and copies ran while one was open for 16% -> 2% of each run, Pallas kernels for 0% -> 0%
where the time goes in v2:
time: 75.2 us; the launch traced here: 74.8 us
  blocking collectives  27.4 us (36%)
  starting transfers between devices  19.4 us (26%)
  matrix products  8.29 us (11%)
  waiting for transfers between devices  7.48 us (10%)
  other arithmetic  6.47 us (9%)
  local copies, waits for them, and re-layouts  4.68 us (6%)
  between operations  1.02 us (1%)
    all_to_all x1, blocking collectives, local(): lax.all_to_all(sent, 'snp', 0, 0, tiled=True)  15.1 us
    all_to_all x3, starting transfers between devices, all_sum(): return jnp.sum(lax.all_to_all(sent, axes, 0, 0, tiled=True), axis=0)  13.2 us
    all_to_all x3, waiting for transfers between devices, all_sum(): return jnp.sum(lax.all_to_all(sent, axes, 0, 0, tiled=True), axis=0)  7.48 us
    all_gather x1, blocking collectives, local(): beta_all = lax.all_gather(beta_hat, 'ind', axis=0, tiled=True)  6.23 us
    all_gather x1, blocking collectives, local(): image_all = lax.all_gather(image, 'ind', axis=0, tiled=True)  6.14 us
    ppermute x1, starting transfers between devices, spread_operator(): from_left = lax.ppermute(own[:, rows:], 'snp', forward)  4.9 us
    dot_general x1, matrix products, spread_operator(): jnp.einsum('tbr,brk->btk', vector.reshape(traits, blocks_here, BLK), bloc...  3.87 us
    dot_general x1, matrix products, apply_operator(): jnp.einsum('btk,brk->tbr', windows, blocks, precision=lax.Precision.HIGHEST)  3.66 us
  transfers between devices with their start and end apart: 5, of which 2 were waited for; matrix products, arithmetic and copies ran while one was open for 2% of the time, Pallas kernels for 0%

profile of v2, /device:TPU:0, one launch (start us, length us, event | category | flops | bytes accessed | tf_op | source)
XLA Modules:
  0.0 74.8 jit_solution(6264992410320001044)
XLA Ops:
  0.6 0.7 and_compare_fusion.6
  1.3 3.9 %fusion.20 = f32[8,16,1024]{2,1,0:T(8,128)S(1)} fusion(f32[8,128,1024]{2,1,0:T(8,128)} %bitcast.119, f32[16,1024]{1,0:T(8,128)} %param.5), kind=kOutput, calls=%fused_computation.64 | convolution fusion | flops 201326592 | bytes 4784128 | tf_op jit(solution)/shard_map/tbr,brk->btk/dot_general | solution.py:46
  5.2 0.2 slice_select_fusion.6
  5.5 0.0 copy-start.3
  5.5 0.0 copy-start.2
  5.5 0.2 fusion
  5.7 0.0 copy-start.1
  5.7 0.2 fusion.1
  6.0 0.2 fusion.2
  6.2 0.2 fusion.3
  6.4 0.2 fusion.4
  6.7 0.2 fusion.5
  7.0 0.1 broadcast_multiply_fusion
  7.1 0.1 fusion.8
  7.2 4.9 %collective-permute-start = (f32[16,960]{1,0:T(8,128)S(1)}, f32[16,960]{1,0:T(8,128)S(1)}, u32[]{:S(2)}, u32[]{:S(2)}) collective-permute-start(f32[16,960]{1,0:T(8,128)S(1)} %get-tuple-element.22), channel_id=1, source_target_pairs={{0,4},{4,8},{8,12},{12,16},{16,20},{20,24},{24,28},{1,5},{5,9},{9,... | collective-permute-start | bytes 184328 | tf_op jit(solution)/shard_map/ppermute | solution.py:64
  12.1 1.3 %collective-permute-start.1 = (f32[16,960]{1,0:T(8,128)S(1)}, f32[16,960]{1,0:T(8,128)S(1)}, u32[]{:S(2)}, u32[]{:S(2)}) collective-permute-start(f32[16,960]{1,0:T(8,128)S(1)} %get-tuple-element.23), channel_id=1, source_target_pairs={{4,0},{8,4},{12,8},{16,12},{20,16},{24,20},{28,24},{5,1},{9,5},{13... | collective-permute-start | bytes 184328 | tf_op jit(solution)/shard_map/ppermute | solution.py:65
  13.4 0.4 convert_reduce_fusion
  13.8 0.6 broadcast_in_dim.160
  14.4 3.3 %all-to-all-start.1 = ((f32[4,1,1024]{2,1,0:T(1,128)}), f32[4,1,1024]{2,1,0:T(1,128)S(1)}, u32[]{:S(2)}, u32[]{:S(2)}) async-start(f32[4,1,1024]{2,1,0:T(1,128)} %broadcast_in_dim.160), calls=%async_computation.1 | async-start | bytes 32768 | tf_op jit(solution)/shard_map/all_to_all | solution.py:16
  17.6 6.2 %all_gather.6 = f32[64,1024]{1,0:T(8,128)S(1)} all-gather(f32[16,1024]{1,0:T(8,128)S(1)} %copy-done.2), channel_id=1, replica_groups=mesh['snp'=8,'ind'=4] {'ind'}, dimensions={0}, use_global_device_ids=true | all-gather | bytes 327680 | tf_op jit(solution)/shard_map/all_gather | solution.py:83
  24.1 0.2 slice_select_fusion.5
  24.3 0.0 copy-start
  24.3 0.2 slice_select_fusion.4
  24.5 0.2 slice_select_fusion.3
  24.8 0.2 slice_select_fusion.2
  25.0 0.2 slice_select_fusion.1
  25.2 0.2 slice_select_fusion
  25.5 1.0 %copy-done = f32[1024,1024]{1,0:T(8,128)S(1)} copy-done((f32[1024,1024]{1,0:T(8,128)S(1)}, f32[1024,1024]{1,0:T(8,128)}, u32[]{:S(2)}) %copy-start) | copy-done | bytes 4194328
  26.5 3.7 %convolution_bitcast_fusion.1 = f32[8,2,8,128]{3,2,1,0:T(8,128)S(1)} fusion(f32[8,128,1024]{2,1,0:T(8,128)S(1)} %bitcast.120, f32[8,16,1088]{2,1,0:T(8,128)S(1)} %slice_select_fusion, pred[8]{0:T(512)(128)(4,1)S(1)} %get-tuple-element.11), kind=kOutput, calls=%fused_computation.2 | convolution fusion | flops 201457664 | bytes 5308928 | tf_op jit(solution)/shard_map/btk,brk->tbr/dot_general | solution.py:36
  30.1 0.2 multiply_reduce_fusion.2
  30.4 0.1 dynamic_update_slice.5
  30.6 0.7 reshape.139
  31.3 7.1 %all-to-all-start = ((f32[32,1,256]{2,1,0:T(1,128)}), f32[32,1,256]{2,1,0:T(1,128)S(1)}, u32[]{:S(2)}, u32[]{:S(2)}) async-start(f32[32,1,256]{2,1,0:T(1,128)} %reshape.139), calls=%async_computation | async-start | bytes 65536 | tf_op jit(solution)/shard_map/all_to_all | solution.py:16
  38.4 6.1 %all_gather.7 = f32[64,1024]{1,0:T(8,128)S(1)} all-gather(f32[16,1024]{1,0:T(8,128)S(1)} %get-tuple-element.21), channel_id=1, replica_groups=mesh['snp'=8,'ind'=4] {'ind'}, dimensions={0}, use_global_device_ids=true | all-gather | bytes 327680 | tf_op jit(solution)/shard_map/all_gather | solution.py:87
  44.6 1.0 %all-to-all-done = f32[32,1,256]{2,1,0:T(1,128)S(1)} async-done(((f32[32,1,256]{2,1,0:T(1,128)}), f32[32,1,256]{2,1,0:T(1,128)S(1)}, u32[]{:S(2)}, u32[]{:S(2)}) %all-to-all-start) | async-done | bytes 32800 | tf_op jit(solution)/shard_map/all_to_all | solution.py:16
  45.6 0.5 broadcast.158
  46.1 0.7 reduce.2
  46.9 0.1 reshape.140
  47.0 0.3 multiply_reduce_fusion
  47.3 0.8 %convolution_bitcast_fusion = f32[8,8,8,128]{3,1,2,0:T(8,128)S(1)} fusion(bf16[1024,1024]{1,0:T(8,128)(2,1)S(1)} %copy-done.1, f32[64,1024]{1,0:T(8,128)S(1)} %get-tuple-element.7), kind=kOutput, calls=%fused_computation.1 | convolution fusion | flops 134283264 | bytes 2621440 | tf_op jit(solution)/shard_map/dot_general | solution.py:114
  48.1 0.1 copy.21
  48.2 15.1 %all_to_all.22 = f32[8,65,128]{2,1,0:T(8,128)S(1)} all-to-all(f32[8,65,128]{2,1,0:T(8,128)S(1)} %copy.21), channel_id=1, replica_groups=mesh['snp'=8,'ind'=4] {'snp'}, dimensions={0} | all-to-all | bytes 532480 | tf_op jit(solution)/shard_map/all_to_all | solution.py:123
  63.3 0.2 multiply_reduce_fusion.4
  63.5 0.6 broadcast_in_dim.162
  64.1 2.9 %all-to-all-start.3 = ((f32[32,1,64]{2,1,0:T(1,128)}), f32[32,1,64]{2,1,0:T(1,128)S(1)}, u32[]{:S(2)}, u32[]{:S(2)}) async-start(f32[32,1,64]{2,1,0:T(1,128)} %broadcast_in_dim.162), calls=%async_computation.3 | async-start | bytes 32768 | tf_op jit(solution)/shard_map/all_to_all | solution.py:16
  67.0 0.6 constant_dynamic-slice_fusion
  67.6 6.4 %all-to-all-done.3 = f32[32,1,64]{2,1,0:T(1,128)S(1)} async-done(((f32[32,1,64]{2,1,0:T(1,128)}), f32[32,1,64]{2,1,0:T(1,128)S(1)}, u32[]{:S(2)}, u32[]{:S(2)}) %all-to-all-start.3) | async-done | bytes 8224 | tf_op jit(solution)/shard_map/all_to_all | solution.py:16
  74.1 0.7 fusion.24
  (33 shorter events, 0.5 us)
Async XLA Ops:
  5.5 1.5 %copy-start.3 = (f32[16]{0:T(128)S(1)}, f32[16]{0:T(128)}, u32[]{:S(2)}) copy-start(f32[16]{0:T(128)} %param.8) | copy-start | bytes 196
  5.5 1.5 %copy-start.2 = (f32[16,1024]{1,0:T(8,128)S(1)}, f32[16,1024]{1,0:T(8,128)}, u32[]{:S(2)}) copy-start(f32[16,1024]{1,0:T(8,128)} %param.5) | copy-start | bytes 196612
  5.7 7.7 %copy-start.1 = (bf16[1024,1024]{1,0:T(8,128)(2,1)S(1)}, bf16[1024,1024]{1,0:T(8,128)(2,1)}, u32[]{:S(2)}) copy-start(bf16[1024,1024]{1,0:T(8,128)(2,1)} %param.9) | copy-start | bytes 6291460
  7.2 16.7 %collective-permute-start = (f32[16,960]{1,0:T(8,128)S(1)}, f32[16,960]{1,0:T(8,128)S(1)}, u32[]{:S(2)}, u32[]{:S(2)}) collective-permute-start(f32[16,960]{1,0:T(8,128)S(1)} %get-tuple-element.22), channel_id=1, source_target_pairs={{0,4},{4,8},{8,12},{12,16},{16,20},{20,24},{24,28},{1,5},{5,9},{9,... | collective-permute-start | bytes 184328 | tf_op jit(solution)/shard_map/ppermute | solution.py:64
  12.1 11.8 %collective-permute-start.1 = (f32[16,960]{1,0:T(8,128)S(1)}, f32[16,960]{1,0:T(8,128)S(1)}, u32[]{:S(2)}, u32[]{:S(2)}) collective-permute-start(f32[16,960]{1,0:T(8,128)S(1)} %get-tuple-element.23), channel_id=1, source_target_pairs={{4,0},{8,4},{12,8},{16,12},{20,16},{24,20},{28,24},{5,1},{9,5},{13... | collective-permute-start | bytes 184328 | tf_op jit(solution)/shard_map/ppermute | solution.py:65
  14.4 9.5 %all-to-all-start.1 = ((f32[4,1,1024]{2,1,0:T(1,128)}), f32[4,1,1024]{2,1,0:T(1,128)S(1)}, u32[]{:S(2)}, u32[]{:S(2)}) async-start(f32[4,1,1024]{2,1,0:T(1,128)} %broadcast_in_dim.160), calls=%async_computation.1 | async-start | bytes 32768 | tf_op jit(solution)/shard_map/all_to_all | solution.py:16
  24.3 2.2 %copy-start = (f32[1024,1024]{1,0:T(8,128)S(1)}, f32[1024,1024]{1,0:T(8,128)}, u32[]{:S(2)}) copy-start(f32[1024,1024]{1,0:T(8,128)} %param.6) | copy-start | bytes 12582916
  31.3 14.3 %all-to-all-start = ((f32[32,1,256]{2,1,0:T(1,128)}), f32[32,1,256]{2,1,0:T(1,128)S(1)}, u32[]{:S(2)}, u32[]{:S(2)}) async-start(f32[32,1,256]{2,1,0:T(1,128)} %reshape.139), calls=%async_computation | async-start | bytes 65536 | tf_op jit(solution)/shard_map/all_to_all | solution.py:16
  64.1 9.9 %all-to-all-start.3 = ((f32[32,1,64]{2,1,0:T(1,128)}), f32[32,1,64]{2,1,0:T(1,128)S(1)}, u32[]{:S(2)}, u32[]{:S(2)}) async-start(f32[32,1,64]{2,1,0:T(1,128)} %broadcast_in_dim.162), calls=%async_computation.3 | async-start | bytes 32768 | tf_op jit(solution)/shard_map/all_to_all | solution.py:16

commit v3 on v2

--- a/solution.py
+++ b/solution.py
@@ -70,7 +70,6 @@
     n_snp = lax.axis_size("snp")
     n_ind = lax.axis_size("ind")
     n_all = n_snp * n_ind
-    me_ind = lax.axis_index("ind")
     traits_here, rows_here = beta_hat.shape
     traits = traits_here * n_ind
     halo = ld_band.shape[1] - BLK - REACH
@@ -78,13 +77,8 @@
     shifts = offsets - jnp.arange(band_start.shape[0], dtype=jnp.int32) * BLK
 
     ridge_shift = M_GENOME / N_GWAS / heritability
-    colsum = jnp.sum(genotypes.astype(jnp.float32), axis=0)
-    colsum = all_sum(colsum, "ind", n_ind)
-    beta_all = lax.all_gather(beta_hat, "ind", axis=0, tiled=True)
-
     extended = spread_operator(beta_hat, ld_band, shifts, ridge_shift, halo)
     image = extended[:, halo : halo + rows_here]
-    image_all = lax.all_gather(image, "ind", axis=0, tiled=True)
     image2 = apply_operator(extended, image, ld_band, shifts, ridge_shift)
 
     moments = jnp.stack(
@@ -95,9 +89,7 @@
             jnp.sum(image * image2, axis=1),
         ]
     )
-    placed = jnp.zeros((4, traits), jnp.float32)
-    placed = lax.dynamic_update_slice_in_dim(placed, moments, me_ind * traits_here, 1)
-    m0, m1, m2, m3 = all_sum(placed, ("ind", "snp"), n_all)
+    m0, m1, m2, m3 = all_sum(moments, "snp", n_snp)
 
     alpha1 = m0 / m1
     norm1 = alpha1 * alpha1 * m2 - m0
@@ -105,27 +97,30 @@
     grow = 1.0 + ratio
     curv = grow * grow * m1 - 2.0 * grow * alpha1 * m2 + alpha1 * alpha1 * m3
     alpha2 = norm1 / curv
-    residual = beta_all - alpha1[:, None] * image_all
-    direction = residual + ratio[:, None] * beta_all
-    weights_all = alpha1[:, None] * beta_all + alpha2[:, None] * direction
-    weights = lax.dynamic_slice_in_dim(weights_all, me_ind * traits_here, traits_here, 0)
+    residual = beta_hat - alpha1[:, None] * image
+    direction = residual + ratio[:, None] * beta_hat
+    weights = alpha1[:, None] * beta_hat + alpha2[:, None] * direction
 
-    rounded = weights_all.astype(jnp.bfloat16)
+    rounded = lax.all_gather(weights.astype(jnp.bfloat16), "ind", axis=0, tiled=True)
     partial = lax.dot_general(
         rounded, genotypes, (((1,), (1,)), ((), ())), preferred_element_type=jnp.float32
     )
-    mean_part = jnp.sum(rounded.astype(jnp.float32) * colsum[None, :], axis=1)
     inds_here = genotypes.shape[0]
     share = inds_here // n_snp
-    chunks = partial.reshape(traits, n_snp, share).transpose(1, 0, 2).reshape(n_snp, traits * share)
-    extra = jnp.broadcast_to(jnp.pad(mean_part, (0, 128 - traits % 128 if traits % 128 else 0))[None], (n_snp, -(-traits // 128) * 128))
-    sent = jnp.concatenate([chunks, extra], axis=1).reshape(n_snp, -1, 128)
-    got = jnp.sum(lax.all_to_all(sent, "snp", 0, 0, tiled=True), axis=0).reshape(-1)
-    complete = got[: traits * share].reshape(traits, share)
+    chunks = partial.reshape(traits, n_snp, share).transpose(1, 0, 2)
+    complete = jnp.sum(lax.all_to_all(chunks, "snp", 0, 0, tiled=True), axis=0)
     count = inds_here * n_ind
-    average = got[traits * share : traits * share + traits] / count
+    local_sum = jnp.sum(complete, axis=1)
+    local_centred = complete - (local_sum / share)[:, None]
+    local_square = jnp.sum(local_centred * local_centred, axis=1)
+    both = jnp.stack([local_sum, local_square])
+    sent = jnp.broadcast_to(both[None], (n_all,) + both.shape)
+    every = lax.all_to_all(sent, ("ind", "snp"), 0, 0, tiled=True)
+    average = jnp.sum(every[:, 0], axis=0) / count
+    spread = every[:, 0] / share - average[None, :]
+    squares = jnp.sum(every[:, 1], axis=0) + share * jnp.sum(spread * spread, axis=0)
+    variance = squares / count
     centred = complete - average[:, None]
-    variance = all_sum(jnp.sum(centred * centred, axis=1), ("ind", "snp"), n_all) / count
     scores = centred * lax.rsqrt(variance + 1e-05)[:, None]
     return (weights, scores)
 

time: 75.2 us -> 69.5 us (0.924)
  starting transfers between devices: 19.4 us -> 6.19 us
  blocking collectives: 27.4 us -> 40.2 us
  local copies, waits for them, and re-layouts: 4.68 us -> 1.94 us
  waiting for transfers between devices: 7.48 us -> 4.86 us
    all_to_all x1 -> x3, blocking collectives: 15.1 us -> 34.8 us  [the longest x1 12.1 us: local(): complete = jnp.sum(lax.all_to_all(chunks, 'snp', 0, 0, tiled=True), axis=0)]
    all_to_all x3 -> x0, starting transfers between devices: 13.2 us -> none  [all_sum(): return jnp.sum(lax.all_to_all(sent, axes, 0, 0, tiled=True), axis=0)]
    all_to_all x3 -> x0, waiting for transfers between devices: 7.48 us -> none  [all_sum(): return jnp.sum(lax.all_to_all(sent, axes, 0, 0, tiled=True), axis=0)]
    all_gather x2 -> x1, blocking collectives: 12.4 us -> 5.4 us  [local(): lax.all_gather(weights.astype(jnp.bfloat16), 'ind', axis=0, tiled=True)]
    ppermute x1, waiting for transfers between devices: 0.01 us -> 4.27 us  [spread_operator(): from_right = lax.ppermute(own[:, :2 * halo], 'snp', backward)]
    broadcast_in_dim x4 -> x1, local copies, waits for them, and re-layouts: 1.25 us -> 0.01 us  [all_sum(): sent = jnp.broadcast_to(x[None], (count,) + x.shape)]
    unnamed x18 -> x17, local copies, waits for them, and re-layouts: 1.97 us -> 1.29 us
  transfers between devices with their start and end apart: 5 -> 2, of which waited for: 2 -> 2; matrix products, arithmetic and copies ran while one was open for 2% -> 0% of each run, Pallas kernels for 0% -> 0%
where the time goes in v3:
time: 69.5 us; the launch traced here: 69.2 us
  blocking collectives  40.2 us (58%)
  matrix products  8.28 us (12%)
  other arithmetic  6.82 us (10%)
  starting transfers between devices  6.19 us (9%)
  waiting for transfers between devices  4.86 us (7%)
  local copies, waits for them, and re-layouts  1.94 us (3%)
  between operations  0.94 us (1%)
    all_to_all x1, blocking collectives, local(): complete = jnp.sum(lax.all_to_all(chunks, 'snp', 0, 0, tiled=True), axis=0)  12.1 us
    all_to_all x1, blocking collectives, all_sum(): return jnp.sum(lax.all_to_all(sent, axes, 0, 0, tiled=True), axis=0)  12.1 us
    all_to_all x1, blocking collectives, local(): every = lax.all_to_all(sent, ('ind', 'snp'), 0, 0, tiled=True)  10.5 us
    all_gather x1, blocking collectives, local(): lax.all_gather(weights.astype(jnp.bfloat16), 'ind', axis=0, tiled=True)  5.4 us
    ppermute x1, starting transfers between devices, spread_operator(): from_left = lax.ppermute(own[:, rows:], 'snp', forward)  4.9 us
    ppermute x1, waiting for transfers between devices, spread_operator(): from_right = lax.ppermute(own[:, :2 * halo], 'snp', backward)  4.27 us
    dot_general x1, matrix products, spread_operator(): jnp.einsum('tbr,brk->btk', vector.reshape(traits, blocks_here, BLK), bloc...  3.87 us
    dot_general x1, matrix products, apply_operator(): jnp.einsum('btk,brk->tbr', windows, blocks, precision=lax.Precision.HIGHEST)  3.66 us
  transfers between devices with their start and end apart: 2, of which 2 were waited for; matrix products, arithmetic and copies ran while one was open for 0% of the time, Pallas kernels for 0%

profile of v3, /device:TPU:0, one launch (start us, length us, event | category | flops | bytes accessed | tf_op | source)
XLA Modules:
  0.0 69.2 jit_solution(10162374669973409148)
XLA Ops:
  0.6 0.0 copy-start
  0.6 0.8 %and_compare_fusion.6 = (pred[8]{0:T(512)(128)(4,1)S(1)}, s32[8]{0:T(128)S(1)}) fusion(s32[8]{0:T(128)} %param.7, s32[]{:T(128)S(6)} %mul.147), kind=kLoop, calls=%fused_computation.92 | loop fusion | flops 56 | bytes 76 | tf_op jit(solution)/shard_map/eq | solution.py:53
  1.5 3.9 %fusion.20 = f32[8,16,1024]{2,1,0:T(8,128)S(1)} fusion(f32[8,128,1024]{2,1,0:T(8,128)} %bitcast.122, f32[16,1024]{1,0:T(8,128)} %param.5), kind=kOutput, calls=%fused_computation.61 | convolution fusion | flops 201326592 | bytes 4784128 | tf_op jit(solution)/shard_map/tbr,brk->btk/dot_general | solution.py:46
  5.4 0.2 slice_select_fusion.6
  5.6 0.0 copy-start.3
  5.6 0.0 copy-start.2
  5.7 0.2 fusion
  5.9 0.2 fusion.1
  6.1 0.2 fusion.2
  6.3 0.2 fusion.3
  6.6 0.2 fusion.4
  6.8 0.2 fusion.5
  7.1 0.0 copy-done.3
  7.1 0.0 copy-done.2
  7.1 0.1 broadcast_multiply_fusion
  7.2 0.1 fusion.8
  7.3 4.9 %collective-permute-start = (f32[16,960]{1,0:T(8,128)S(1)}, f32[16,960]{1,0:T(8,128)S(1)}, u32[]{:S(2)}, u32[]{:S(2)}) collective-permute-start(f32[16,960]{1,0:T(8,128)S(1)} %get-tuple-element.23), channel_id=1, source_target_pairs={{0,4},{4,8},{8,12},{12,16},{16,20},{20,24},{24,28},{1,5},{5,9},{9,... | collective-permute-start | bytes 184328 | tf_op jit(solution)/shard_map/ppermute | solution.py:64
  12.2 1.3 %collective-permute-start.1 = (f32[16,960]{1,0:T(8,128)S(1)}, f32[16,960]{1,0:T(8,128)S(1)}, u32[]{:S(2)}, u32[]{:S(2)}) collective-permute-start(f32[16,960]{1,0:T(8,128)S(1)} %get-tuple-element.24), channel_id=1, source_target_pairs={{4,0},{8,4},{12,8},{16,12},{20,16},{24,20},{28,24},{5,1},{9,5},{13... | collective-permute-start | bytes 184328 | tf_op jit(solution)/shard_map/ppermute | solution.py:65
  13.5 0.6 collective-permute-done
  14.1 4.3 %collective-permute-done.1 = f32[16,960]{1,0:T(8,128)S(1)} collective-permute-done((f32[16,960]{1,0:T(8,128)S(1)}, f32[16,960]{1,0:T(8,128)S(1)}, u32[]{:S(2)}, u32[]{:S(2)}) %collective-permute-start.1) | collective-permute-done | bytes 61472 | tf_op jit(solution)/shard_map/ppermute | solution.py:65
  18.5 0.2 slice_select_fusion.5
  18.8 0.0 copy-start.1
  18.8 0.2 slice_select_fusion.4
  19.0 0.2 slice_select_fusion.3
  19.2 0.2 slice_select_fusion.2
  19.5 0.2 slice_select_fusion.1
  19.7 0.2 slice_select_fusion
  19.9 1.0 %copy-done.1 = f32[1024,1024]{1,0:T(8,128)S(1)} copy-done((f32[1024,1024]{1,0:T(8,128)S(1)}, f32[1024,1024]{1,0:T(8,128)}, u32[]{:S(2)}) %copy-start.1) | copy-done | bytes 4194328
  21.0 3.7 %convolution_bitcast_fusion.1 = f32[8,2,8,128]{3,2,1,0:T(8,128)S(1)} fusion(f32[8,128,1024]{2,1,0:T(8,128)S(1)} %bitcast.123, f32[8,16,1088]{2,1,0:T(8,128)S(1)} %slice_select_fusion, pred[8]{0:T(512)(128)(4,1)S(1)} %get-tuple-element.13), kind=kOutput, calls=%fused_computation.1 | convolution fusion | flops 201457664 | bytes 5308928 | tf_op jit(solution)/shard_map/btk,brk->tbr/dot_general | solution.py:36
  24.6 0.2 multiply_reduce_fusion.1
  24.9 12.1 %all_to_all.15 = f32[8,4,16]{2,1,0:T(4,128)S(1)} all-to-all(f32[8,4,16]{2,1,0:T(4,128)S(1)} %broadcast_in_dim.144), channel_id=1, replica_groups=mesh['snp'=8,'ind'=4] {'snp'}, dimensions={0} | all-to-all | bytes 4096 | tf_op jit(solution)/shard_map/all_to_all | solution.py:16
  37.0 0.7 %fusion.28 = (bf16[16,1024]{1,0:T(8,128)(2,1)S(1)}, f32[16,1024]{1,0:T(8,128)}) fusion(f32[16,1024]{1,0:T(8,128)S(1)} %copy-done.2, f32[16]{0:T(128)S(1)} %get-tuple-element.11, f32[16,1984]{1,0:T(8,128)S(1)} %pad_add_fusion.6, f32[16]{0:T(128)S(1)} %get-tuple-element.10, f32[16]{0:T(128)S(1)} %get-tuple-element.12), kind=kLoop, calls=%fused_computation.98 | loop fusion | flops 131072 | bytes 229568 | tf_op jit(solution)/shard_map/convert_element_type | solution.py:104
  37.8 5.4 %all_gather.3 = bf16[64,1024]{1,0:T(8,128)(2,1)S(1)} all-gather(bf16[16,1024]{1,0:T(8,128)(2,1)S(1)} %get-tuple-element.8), channel_id=1, replica_groups=mesh['snp'=8,'ind'=4] {'ind'}, dimensions={0}, use_global_device_ids=true | all-gather | bytes 163840 | tf_op jit(solution)/shard_map/all_gather | solution.py:104
  43.2 0.0 copy-done
  43.2 0.8 %convolution_bitcast_fusion = f32[8,8,8,128]{3,2,1,0:T(8,128)S(1)} fusion(bf16[64,1024]{1,0:T(8,128)(2,1)S(1)} %all_gather.3, bf16[1024,1024]{1,0:T(8,128)(2,1)S(1)} %copy-done), kind=kOutput, calls=%fused_computation | convolution fusion | flops 134217728 | bytes 2490368 | tf_op jit(solution)/shard_map/dot_general | solution.py:105
  44.0 12.1 %all_to_all.16 = f32[8,64,128]{2,1,0:T(8,128)S(1)} all-to-all(f32[8,64,128]{2,1,0:T(8,128)S(1)} %bitcast.124), channel_id=1, replica_groups=mesh['snp'=8,'ind'=4] {'snp'}, dimensions={0} | all-to-all | bytes 524288 | tf_op jit(solution)/shard_map/all_to_all | solution.py:111
  56.1 0.1 fusion.27
  56.2 0.2 multiply_reduce_fusion.3
  56.4 0.1 reshape.120
  56.5 10.5 %all_to_all.17 = f32[32,1,128]{2,1,0:T(1,128)S(1)} all-to-all(f32[32,1,128]{2,1,0:T(1,128)S(1)} %reshape.120), channel_id=1, replica_groups=mesh['snp'=8,'ind'=4] {'ind','snp'}, dimensions={0} | all-to-all | bytes 32768 | tf_op jit(solution)/shard_map/all_to_all | solution.py:118
  67.1 0.5 broadcast.179
  67.6 0.7 reduce.3
  68.3 0.1 reshape.121
  68.5 0.7 %subtract_multiply_fusion = f32[64,128]{1,0:T(8,128)} fusion(f32[64,128]{1,0:T(8,128)S(1)} %get-tuple-element.3, f32[64]{0:T(128)S(1)} %add_rsqrt_fusion, f32[64]{0:T(128)S(1)} %broadcast_multiply_fusion.2), kind=kLoop, calls=%fused_computation.68 | loop fusion | flops 16384 | bytes 66048 | tf_op jit(solution)/shard_map/mul | solution.py:124
  (28 shorter events, 0.4 us)
Async XLA Ops:
  0.6 42.5 %copy-start = (bf16[1024,1024]{1,0:T(8,128)(2,1)S(1)}, bf16[1024,1024]{1,0:T(8,128)(2,1)}, u32[]{:S(2)}) copy-start(bf16[1024,1024]{1,0:T(8,128)(2,1)} %param.9) | copy-start | bytes 6291460
  5.6 1.5 %copy-start.3 = (f32[16]{0:T(128)S(1)}, f32[16]{0:T(128)}, u32[]{:S(2)}) copy-start(f32[16]{0:T(128)} %param.8) | copy-start | bytes 196
  5.6 1.5 %copy-start.2 = (f32[16,1024]{1,0:T(8,128)S(1)}, f32[16,1024]{1,0:T(8,128)}, u32[]{:S(2)}) copy-start(f32[16,1024]{1,0:T(8,128)} %param.5) | copy-start | bytes 196612
  7.3 6.8 %collective-permute-start = (f32[16,960]{1,0:T(8,128)S(1)}, f32[16,960]{1,0:T(8,128)S(1)}, u32[]{:S(2)}, u32[]{:S(2)}) collective-permute-start(f32[16,960]{1,0:T(8,128)S(1)} %get-tuple-element.23), channel_id=1, source_target_pairs={{0,4},{4,8},{8,12},{12,16},{16,20},{20,24},{24,28},{1,5},{5,9},{9,... | collective-permute-start | bytes 184328 | tf_op jit(solution)/shard_map/ppermute | solution.py:64
  12.2 6.2 %collective-permute-start.1 = (f32[16,960]{1,0:T(8,128)S(1)}, f32[16,960]{1,0:T(8,128)S(1)}, u32[]{:S(2)}, u32[]{:S(2)}) collective-permute-start(f32[16,960]{1,0:T(8,128)S(1)} %get-tuple-element.24), channel_id=1, source_target_pairs={{4,0},{8,4},{12,8},{16,12},{20,16},{24,20},{28,24},{5,1},{9,5},{13... | collective-permute-start | bytes 184328 | tf_op jit(solution)/shard_map/ppermute | solution.py:65
  18.8 2.2 %copy-start.1 = (f32[1024,1024]{1,0:T(8,128)S(1)}, f32[1024,1024]{1,0:T(8,128)}, u32[]{:S(2)}) copy-start(f32[1024,1024]{1,0:T(8,128)} %param.6) | copy-start | bytes 12582916

commit v4 on v3

--- a/solution.py
+++ b/solution.py
@@ -70,6 +70,7 @@
     n_snp = lax.axis_size("snp")
     n_ind = lax.axis_size("ind")
     n_all = n_snp * n_ind
+    me_ind = lax.axis_index("ind")
     traits_here, rows_here = beta_hat.shape
     traits = traits_here * n_ind
     halo = ld_band.shape[1] - BLK - REACH
@@ -79,6 +80,11 @@
     ridge_shift = M_GENOME / N_GWAS / heritability
     extended = spread_operator(beta_hat, ld_band, shifts, ridge_shift, halo)
     image = extended[:, halo : halo + rows_here]
+    pair = jnp.concatenate([beta_hat, image], axis=0)
+    arrived = [pair] + [
+        lax.ppermute(pair, "ind", [(j, (j + k) % n_ind) for j in range(n_ind)])
+        for k in range(1, n_ind)
+    ]
     image2 = apply_operator(extended, image, ld_band, shifts, ridge_shift)
 
     moments = jnp.stack(
@@ -89,7 +95,13 @@
             jnp.sum(image * image2, axis=1),
         ]
     )
-    m0, m1, m2, m3 = all_sum(moments, "snp", n_snp)
+    placed = jnp.zeros((4, traits), jnp.float32)
+    placed = lax.dynamic_update_slice_in_dim(placed, moments, me_ind * traits_here, 1)
+    m0, m1, m2, m3 = all_sum(placed, ("ind", "snp"), n_all)
+    slots = (me_ind - jnp.arange(n_ind)) % n_ind
+    ordered = jnp.take(jnp.stack(arrived), slots, axis=0)
+    beta_all = ordered[:, :traits_here].reshape(traits, rows_here)
+    image_all = ordered[:, traits_here:].reshape(traits, rows_here)
 
     alpha1 = m0 / m1
     norm1 = alpha1 * alpha1 * m2 - m0
@@ -97,11 +109,12 @@
     grow = 1.0 + ratio
     curv = grow * grow * m1 - 2.0 * grow * alpha1 * m2 + alpha1 * alpha1 * m3
     alpha2 = norm1 / curv
-    residual = beta_hat - alpha1[:, None] * image
-    direction = residual + ratio[:, None] * beta_hat
-    weights = alpha1[:, None] * beta_hat + alpha2[:, None] * direction
+    residual = beta_all - alpha1[:, None] * image_all
+    direction = residual + ratio[:, None] * beta_all
+    weights_all = alpha1[:, None] * beta_all + alpha2[:, None] * direction
+    weights = lax.dynamic_slice_in_dim(weights_all, me_ind * traits_here, traits_here, 0)
 
-    rounded = lax.all_gather(weights.astype(jnp.bfloat16), "ind", axis=0, tiled=True)
+    rounded = weights_all.astype(jnp.bfloat16)
     partial = lax.dot_general(
         rounded, genotypes, (((1,), (1,)), ((), ())), preferred_element_type=jnp.float32
     )

time: 69.5 us -> 70.8 us (1.019)
  blocking collectives: 40.2 us -> 0 us
  waiting for transfers between devices: 4.86 us -> 24.8 us
  starting transfers between devices: 6.19 us -> 22.9 us
  local copies, waits for them, and re-layouts: 1.94 us -> 4.71 us
  other arithmetic: 6.82 us -> 7.9 us
    all_to_all x3 -> x0, blocking collectives: 34.8 us -> none  [the longest x1 12.1 us: local(): complete = jnp.sum(lax.all_to_all(chunks, 'snp', 0, 0, tiled=True), axis=0)]
    all_to_all x0 -> x3, waiting for transfers between devices: none -> 20 us  [the longest x1 9.77 us: local(): complete = jnp.sum(lax.all_to_all(chunks, 'snp', 0, 0, tiled=True), axis=0)]
    all_to_all x0 -> x3, starting transfers between devices: none -> 13.4 us  [the longest x1 5.84 us: all_sum(): return jnp.sum(lax.all_to_all(sent, axes, 0, 0, tiled=True), axis=0)]
    all_gather x1 -> x0, blocking collectives: 5.4 us -> none  [local(): lax.all_gather(weights.astype(jnp.bfloat16), 'ind', axis=0, tiled=True)]
    ppermute x0 -> x3, starting transfers between devices: none -> 3.28 us  [local(): lax.ppermute(pair, 'ind', [(j, (j + k) % n_ind) for j in range(n_ind)])]
    unnamed x17 -> x19, local copies, waits for them, and re-layouts: 1.29 us -> 2.71 us
    add x0 -> x1, other arithmetic: none -> 0.72 us  [local(): weights_all = alpha1[:, None] * beta_all + alpha2[:, None] * direction]
  transfers between devices with their start and end apart: 2 -> 8, of which waited for: 2 -> 5; matrix products, arithmetic and copies ran while one was open for 0% -> 4% of each run, Pallas kernels for 0% -> 0%
where the time goes in v4:
time: 70.8 us; the launch traced here: 70.4 us
  waiting for transfers between devices  24.8 us (35%)
  starting transfers between devices  22.9 us (32%)
  matrix products  8.98 us (13%)
  other arithmetic  7.9 us (11%)
  local copies, waits for them, and re-layouts  4.71 us (7%)
  between operations  1.08 us (2%)
    all_to_all x1, waiting for transfers between devices, local(): complete = jnp.sum(lax.all_to_all(chunks, 'snp', 0, 0, tiled=True), axis=0)  9.77 us
    all_to_all x1, waiting for transfers between devices, local(): every = lax.all_to_all(sent, ('ind', 'snp'), 0, 0, tiled=True)  6.35 us
    all_to_all x1, starting transfers between devices, all_sum(): return jnp.sum(lax.all_to_all(sent, axes, 0, 0, tiled=True), axis=0)  5.84 us
    ppermute x1, starting transfers between devices, spread_operator(): from_left = lax.ppermute(own[:, rows:], 'snp', forward)  4.9 us
    all_to_all x1, starting transfers between devices, local(): complete = jnp.sum(lax.all_to_all(chunks, 'snp', 0, 0, tiled=True), axis=0)  4.49 us
    ppermute x1, waiting for transfers between devices, spread_operator(): from_right = lax.ppermute(own[:, :2 * halo], 'snp', backward)  4.27 us
    all_to_all x1, waiting for transfers between devices, all_sum(): return jnp.sum(lax.all_to_all(sent, axes, 0, 0, tiled=True), axis=0)  3.88 us
    dot_general x1, matrix products, spread_operator(): jnp.einsum('tbr,brk->btk', vector.reshape(traits, blocks_here, BLK), bloc...  3.87 us
  transfers between devices with their start and end apart: 8, of which 5 were waited for; matrix products, arithmetic and copies ran while one was open for 4% of the time, Pallas kernels for 0%

profile of v4, /device:TPU:0, one launch (start us, length us, event | category | flops | bytes accessed | tf_op | source)
XLA Modules:
  0.0 70.4 jit_solution(4853047738563047622)
XLA Ops:
  0.7 0.8 %and_compare_fusion.6 = (pred[8]{0:T(512)(128)(4,1)S(1)}, s32[8]{0:T(128)S(1)}) fusion(s32[8]{0:T(128)} %param.7, s32[]{:T(128)S(6)} %mul.200), kind=kLoop, calls=%fused_computation.116 | loop fusion | flops 56 | bytes 76 | tf_op jit(solution)/shard_map/eq | solution.py:53
  1.5 3.9 %fusion.20 = f32[8,16,1024]{2,1,0:T(8,128)S(1)} fusion(f32[8,128,1024]{2,1,0:T(8,128)} %bitcast.130, f32[16,1024]{1,0:T(8,128)} %param.5), kind=kOutput, calls=%fused_computation.65 | convolution fusion | flops 201326592 | bytes 4784128 | tf_op jit(solution)/shard_map/tbr,brk->btk/dot_general | solution.py:46
  5.4 0.2 slice_select_fusion.6
  5.7 0.2 fusion
  5.9 0.2 fusion.1
  6.1 0.2 fusion.2
  6.4 0.2 fusion.3
  6.6 0.2 fusion.4
  6.8 0.2 fusion.5
  7.2 0.1 fusion.8
  7.3 4.9 %collective-permute-start = (f32[16,960]{1,0:T(8,128)S(1)}, f32[16,960]{1,0:T(8,128)S(1)}, u32[]{:S(2)}, u32[]{:S(2)}) collective-permute-start(f32[16,960]{1,0:T(8,128)S(1)} %get-tuple-element.33), channel_id=1, source_target_pairs={{0,4},{4,8},{8,12},{12,16},{16,20},{20,24},{24,28},{1,5},{5,9},{9,... | collective-permute-start | bytes 184328 | tf_op jit(solution)/shard_map/ppermute | solution.py:64
  12.2 1.3 %collective-permute-start.1 = (f32[16,960]{1,0:T(8,128)S(1)}, f32[16,960]{1,0:T(8,128)S(1)}, u32[]{:S(2)}, u32[]{:S(2)}) collective-permute-start(f32[16,960]{1,0:T(8,128)S(1)} %get-tuple-element.34), channel_id=1, source_target_pairs={{4,0},{8,4},{12,8},{16,12},{20,16},{24,20},{28,24},{5,1},{9,5},{13... | collective-permute-start | bytes 184328 | tf_op jit(solution)/shard_map/ppermute | solution.py:65
  13.6 0.5 collective-permute-done
  14.1 4.3 %collective-permute-done.1 = f32[16,960]{1,0:T(8,128)S(1)} collective-permute-done((f32[16,960]{1,0:T(8,128)S(1)}, f32[16,960]{1,0:T(8,128)S(1)}, u32[]{:S(2)}, u32[]{:S(2)}) %collective-permute-start.1) | collective-permute-done | bytes 61472 | tf_op jit(solution)/shard_map/ppermute | solution.py:65
  18.5 0.2 slice_select_fusion.5
  18.8 0.2 slice_select_fusion.4
  19.0 0.2 slice_select_fusion.3
  19.2 0.2 slice_select_fusion.2
  19.5 0.2 slice_select_fusion.1
  19.7 0.2 slice_select_fusion
  19.9 1.0 %copy-done.1 = f32[1024,1024]{1,0:T(8,128)S(1)} copy-done((f32[1024,1024]{1,0:T(8,128)S(1)}, f32[1024,1024]{1,0:T(8,128)}, u32[]{:S(2)}) %copy-start.1) | copy-done | bytes 4194328
  21.0 3.7 %convolution_bitcast_fusion.1 = f32[8,2,8,128]{3,2,1,0:T(8,128)S(1)} fusion(f32[8,128,1024]{2,1,0:T(8,128)S(1)} %bitcast.131, f32[8,16,1088]{2,1,0:T(8,128)S(1)} %slice_select_fusion, pred[8]{0:T(512)(128)(4,1)S(1)} %get-tuple-element.17), kind=kOutput, calls=%fused_computation.2 | convolution fusion | flops 201457664 | bytes 5308928 | tf_op jit(solution)/shard_map/btk,brk->tbr/dot_general | solution.py:36
  24.6 0.2 multiply_reduce_fusion.1
  24.9 0.1 dynamic_update_slice.5
  25.1 0.7 %reshape.251 = f32[32,1,256]{2,1,0:T(1,128)} reshape(f32[32,4,64]{2,1,0:T(4,128)S(1)} %broadcast_in_dim.158) | data formatting | bytes 65536
  25.8 5.8 %all-to-all-start = ((f32[32,1,256]{2,1,0:T(1,128)}), f32[32,1,256]{2,1,0:T(1,128)S(1)}, u32[]{:S(2)}, u32[]{:S(2)}) async-start(f32[32,1,256]{2,1,0:T(1,128)} %reshape.251), calls=%async_computation | async-start | bytes 65536 | tf_op jit(solution)/shard_map/all_to_all | solution.py:16
  31.7 0.3 collective-permute-start.2
  32.0 1.6 %collective-permute-start.3 = (f32[32,1024]{1,0:T(8,128)S(1)}, f32[32,1024]{1,0:T(8,128)S(1)}, u32[]{:S(2)}, u32[]{:S(2)}) collective-permute-start(f32[32,1024]{1,0:T(8,128)S(1)} %get-tuple-element.32), channel_id=1, source_target_pairs={{0,2},{1,3},{2,0},{3,1},{4,6},{5,7},{6,4},{7,5},{8,10},{9,11},{10,... | collective-permute-start | bytes 393224 | tf_op jit(solution)/shard_map/ppermute | solution.py:85
  33.6 1.4 %collective-permute-start.4 = (f32[32,1024]{1,0:T(8,128)S(1)}, f32[32,1024]{1,0:T(8,128)S(1)}, u32[]{:S(2)}, u32[]{:S(2)}) collective-permute-start(f32[32,1024]{1,0:T(8,128)S(1)} %get-tuple-element.32), channel_id=1, source_target_pairs={{0,3},{1,0},{2,1},{3,2},{4,7},{5,4},{6,5},{7,6},{8,11},{9,8},{10,9... | collective-permute-start | bytes 393224 | tf_op jit(solution)/shard_map/ppermute | solution.py:85
  34.9 3.9 %all-to-all-done = f32[32,1,256]{2,1,0:T(1,128)S(1)} async-done(((f32[32,1,256]{2,1,0:T(1,128)}), f32[32,1,256]{2,1,0:T(1,128)S(1)}, u32[]{:S(2)}, u32[]{:S(2)}) %all-to-all-start) | async-done | bytes 32800 | tf_op jit(solution)/shard_map/all_to_all | solution.py:16
  38.8 0.6 broadcast.294
  39.4 0.7 reduce.19
  40.1 0.1 reshape.252
  40.7 0.6 gather_fusion
  41.3 0.1 broadcast_select_fusion
  41.4 0.2 add_convert_fusion
  41.6 1.5 %convolution_bitcast_fusion = f32[8,64,128]{2,1,0:T(8,128)} fusion(bf16[64,1024,1]{1,0,2:T(8,128)(2,1)S(1)} %bitcast.132, bf16[8,128,1024]{2,1,0:T(8,128)(2,1)S(1)} %bitcast.129), kind=kOutput, calls=%fused_computation.1 | convolution fusion | flops 134217728 | bytes 2490368 | tf_op jit(solution)/shard_map/dot_general | solution.py:118
  43.1 4.5 %all-to-all-start.1 = ((f32[8,64,128]{2,1,0:T(8,128)}), f32[8,64,128]{2,1,0:T(8,128)S(1)}, u32[]{:S(2)}, u32[]{:S(2)}) async-start(f32[8,64,128]{2,1,0:T(8,128)} %convolution_bitcast_fusion), calls=%async_computation.1 | async-start | bytes 524288 | tf_op jit(solution)/shard_map/all_to_all | solution.py:124
  47.8 9.8 %all-to-all-done.1 = f32[8,64,128]{2,1,0:T(8,128)S(1)} async-done(((f32[8,64,128]{2,1,0:T(8,128)}), f32[8,64,128]{2,1,0:T(8,128)S(1)}, u32[]{:S(2)}, u32[]{:S(2)}) %all-to-all-start.1) | async-done | bytes 262176 | tf_op jit(solution)/shard_map/all_to_all | solution.py:124
  57.6 0.1 fusion.36
  57.7 0.2 multiply_reduce_fusion.3
  57.9 0.7 reshape.253
  58.6 3.1 %all-to-all-start.2 = ((f32[32,1,128]{2,1,0:T(1,128)}), f32[32,1,128]{2,1,0:T(1,128)S(1)}, u32[]{:S(2)}, u32[]{:S(2)}) async-start(f32[32,1,128]{2,1,0:T(1,128)} %reshape.253), calls=%async_computation.2 | async-start | bytes 32768 | tf_op jit(solution)/shard_map/all_to_all | solution.py:131
  61.7 0.7 %fusion.26 = f32[16,1024]{1,0:T(8,128)} fusion(f32[64,1024]{1,0:T(8,128)S(1)} %bitcast.133, s32[]{:T(128)S(6)} %select_n.106, f32[64,1024]{1,0:T(8,128)S(1)} %bitcast.134, f32[16]{0:T(128)S(1)} %dynamic-slice.2, f32[16]{0:T(128)S(1)} %dynamic-slice.1, f32[16]{0:T(128)S(1)} %dynamic-slice), kind=kLoop, calls=%fused_computation.72 | loop fusion | flops 114688 | bytes 196804 | tf_op jit(solution)/shard_map/add | solution.py:114
  62.4 6.3 %all-to-all-done.2 = f32[32,1,128]{2,1,0:T(1,128)S(1)} async-done(((f32[32,1,128]{2,1,0:T(1,128)}), f32[32,1,128]{2,1,0:T(1,128)S(1)}, u32[]{:S(2)}, u32[]{:S(2)}) %all-to-all-start.2) | async-done | bytes 16416 | tf_op jit(solution)/shard_map/all_to_all | solution.py:131
  68.8 0.7 reduce.20
  69.4 0.1 reshape.254
  69.7 0.7 %subtract_multiply_fusion = f32[64,128]{1,0:T(8,128)} fusion(f32[64,128]{1,0:T(8,128)S(1)} %get-tuple-element.3, f32[64]{0:T(128)S(1)} %add_rsqrt_fusion, f32[64]{0:T(128)S(1)} %broadcast_multiply_fusion.2), kind=kLoop, calls=%fused_computation.76 | loop fusion | flops 16384 | bytes 66048 | tf_op jit(solution)/shard_map/mul | solution.py:137
  (54 shorter events, 1.2 us)
Async XLA Ops:
  0.6 41.0 %copy-start = (bf16[1024,1024]{1,0:T(8,128)(2,1)S(1)}, bf16[1024,1024]{1,0:T(8,128)(2,1)}, u32[]{:S(2)}) copy-start(bf16[1024,1024]{1,0:T(8,128)(2,1)} %param.9) | copy-start | bytes 6291460
  5.6 1.5 %copy-start.3 = (f32[16]{0:T(128)S(1)}, f32[16]{0:T(128)}, u32[]{:S(2)}) copy-start(f32[16]{0:T(128)} %param.8) | copy-start | bytes 196
  5.6 1.5 %copy-start.2 = (f32[16,1024]{1,0:T(8,128)S(1)}, f32[16,1024]{1,0:T(8,128)}, u32[]{:S(2)}) copy-start(f32[16,1024]{1,0:T(8,128)} %param.5) | copy-start | bytes 196612
  7.3 6.8 %collective-permute-start = (f32[16,960]{1,0:T(8,128)S(1)}, f32[16,960]{1,0:T(8,128)S(1)}, u32[]{:S(2)}, u32[]{:S(2)}) collective-permute-start(f32[16,960]{1,0:T(8,128)S(1)} %get-tuple-element.33), channel_id=1, source_target_pairs={{0,4},{4,8},{8,12},{12,16},{16,20},{20,24},{24,28},{1,5},{5,9},{9,... | collective-permute-start | bytes 184328 | tf_op jit(solution)/shard_map/ppermute | solution.py:64
  12.2 6.2 %collective-permute-start.1 = (f32[16,960]{1,0:T(8,128)S(1)}, f32[16,960]{1,0:T(8,128)S(1)}, u32[]{:S(2)}, u32[]{:S(2)}) collective-permute-start(f32[16,960]{1,0:T(8,128)S(1)} %get-tuple-element.34), channel_id=1, source_target_pairs={{4,0},{8,4},{12,8},{16,12},{20,16},{24,20},{28,24},{5,1},{9,5},{13... | collective-permute-start | bytes 184328 | tf_op jit(solution)/shard_map/ppermute | solution.py:65
  18.8 2.2 %copy-start.1 = (f32[1024,1024]{1,0:T(8,128)S(1)}, f32[1024,1024]{1,0:T(8,128)}, u32[]{:S(2)}) copy-start(f32[1024,1024]{1,0:T(8,128)} %param.6) | copy-start | bytes 12582916
  25.8 13.0 %all-to-all-start = ((f32[32,1,256]{2,1,0:T(1,128)}), f32[32,1,256]{2,1,0:T(1,128)S(1)}, u32[]{:S(2)}, u32[]{:S(2)}) async-start(f32[32,1,256]{2,1,0:T(1,128)} %reshape.251), calls=%async_computation | async-start | bytes 65536 | tf_op jit(solution)/shard_map/all_to_all | solution.py:16
  31.7 9.0 %collective-permute-start.2 = (f32[32,1024]{1,0:T(8,128)S(1)}, f32[32,1024]{1,0:T(8,128)S(1)}, u32[]{:S(2)}, u32[]{:S(2)}) collective-permute-start(f32[32,1024]{1,0:T(8,128)S(1)} %get-tuple-element.32), channel_id=1, source_target_pairs={{0,1},{1,2},{2,3},{3,0},{4,5},{5,6},{6,7},{7,4},{8,9},{9,10},{10,1... | collective-permute-start | bytes 393224 | tf_op jit(solution)/shard_map/ppermute | solution.py:85
  32.0 8.7 %collective-permute-start.3 = (f32[32,1024]{1,0:T(8,128)S(1)}, f32[32,1024]{1,0:T(8,128)S(1)}, u32[]{:S(2)}, u32[]{:S(2)}) collective-permute-start(f32[32,1024]{1,0:T(8,128)S(1)} %get-tuple-element.32), channel_id=1, source_target_pairs={{0,2},{1,3},{2,0},{3,1},{4,6},{5,7},{6,4},{7,5},{8,10},{9,11},{10,... | collective-permute-start | bytes 393224 | tf_op jit(solution)/shard_map/ppermute | solution.py:85
  33.6 7.1 %collective-permute-start.4 = (f32[32,1024]{1,0:T(8,128)S(1)}, f32[32,1024]{1,0:T(8,128)S(1)}, u32[]{:S(2)}, u32[]{:S(2)}) collective-permute-start(f32[32,1024]{1,0:T(8,128)S(1)} %get-tuple-element.32), channel_id=1, source_target_pairs={{0,3},{1,0},{2,1},{3,2},{4,7},{5,4},{6,5},{7,6},{8,11},{9,8},{10,9... | collective-permute-start | bytes 393224 | tf_op jit(solution)/shard_map/ppermute | solution.py:85
  43.1 14.5 %all-to-all-start.1 = ((f32[8,64,128]{2,1,0:T(8,128)}), f32[8,64,128]{2,1,0:T(8,128)S(1)}, u32[]{:S(2)}, u32[]{:S(2)}) async-start(f32[8,64,128]{2,1,0:T(8,128)} %convolution_bitcast_fusion), calls=%async_computation.1 | async-start | bytes 524288 | tf_op jit(solution)/shard_map/all_to_all | solution.py:124
  58.6 10.2 %all-to-all-start.2 = ((f32[32,1,128]{2,1,0:T(1,128)}), f32[32,1,128]{2,1,0:T(1,128)S(1)}, u32[]{:S(2)}, u32[]{:S(2)}) async-start(f32[32,1,128]{2,1,0:T(1,128)} %reshape.253), calls=%async_computation.2 | async-start | bytes 32768 | tf_op jit(solution)/shard_map/all_to_all | solution.py:131

commit v5 on v3

--- a/solution.py
+++ b/solution.py
@@ -33,7 +33,7 @@
     blocks_here = ld_band.shape[0] // BLK
     windows = windows_of(extended, shifts, band_cols, blocks_here)
     blocks = ld_band.reshape(blocks_here, BLK, band_cols)
-    product = jnp.einsum("btk,brk->tbr", windows, blocks, precision=lax.Precision.HIGHEST)
+    product = jnp.einsum("btk,brk->tbr", windows, blocks, precision=lax.Precision.HIGH)
     return product.reshape(vector.shape) + ridge_shift[:, None] * vector
 
 
@@ -45,7 +45,7 @@
     blocks = ld_band.reshape(blocks_here, BLK, band_cols)
     pieces = jnp.einsum(
         "tbr,brk->btk", vector.reshape(traits, blocks_here, BLK), blocks,
-        precision=lax.Precision.HIGHEST,
+        precision=lax.Precision.HIGH,
     )
     wide = jnp.pad(pieces, ((0, 0), (0, 0), (0, span - band_cols)))
     for bit in range(SHIFT_BITS):

time: 69.5 us -> 67.3 us (0.968)
  matrix products: 8.28 us -> 6.03 us
    dot_general x1, matrix products: 3.66 us -> 1.9 us  [apply_operator(): jnp.einsum('btk,brk->tbr', windows, blocks, precision=lax.Precision.HIGH)]
where the time goes in v5:
time: 67.3 us; the launch traced here: 66.9 us
  blocking collectives  40.2 us (60%)
  other arithmetic  6.82 us (10%)
  starting transfers between devices  6.19 us (9%)
  matrix products  6.03 us (9%)
  waiting for transfers between devices  4.86 us (7%)
  local copies, waits for them, and re-layouts  1.94 us (3%)
  between operations  0.94 us (1%)
    all_to_all x1, blocking collectives, local(): complete = jnp.sum(lax.all_to_all(chunks, 'snp', 0, 0, tiled=True), axis=0)  12.1 us
    all_to_all x1, blocking collectives, all_sum(): return jnp.sum(lax.all_to_all(sent, axes, 0, 0, tiled=True), axis=0)  12.1 us
    all_to_all x1, blocking collectives, local(): every = lax.all_to_all(sent, ('ind', 'snp'), 0, 0, tiled=True)  10.5 us
    all_gather x1, blocking collectives, local(): lax.all_gather(weights.astype(jnp.bfloat16), 'ind', axis=0, tiled=True)  5.4 us
    ppermute x1, starting transfers between devices, spread_operator(): from_left = lax.ppermute(own[:, rows:], 'snp', forward)  4.9 us
    ppermute x1, waiting for transfers between devices, spread_operator(): from_right = lax.ppermute(own[:, :2 * halo], 'snp', backward)  4.27 us
    dot_general x1, matrix products, spread_operator(): jnp.einsum('tbr,brk->btk', vector.reshape(traits, blocks_here, BLK), bloc...  3.38 us
    dot_general x1, matrix products, apply_operator(): jnp.einsum('btk,brk->tbr', windows, blocks, precision=lax.Precision.HIGH)  1.9 us
  transfers between devices with their start and end apart: 2, of which 2 were waited for; matrix products, arithmetic and copies ran while one was open for 0% of the time, Pallas kernels for 0%

profile of v5, /device:TPU:0, one launch (start us, length us, event | category | flops | bytes accessed | tf_op | source)
XLA Modules:
  0.0 66.9 jit_solution(5798754007484028554)
XLA Ops:
  0.6 0.0 copy-start
  0.6 0.8 %and_compare_fusion.6 = (pred[8]{0:T(512)(128)(4,1)S(1)}, s32[8]{0:T(128)S(1)}) fusion(s32[8]{0:T(128)} %param.7, s32[]{:T(128)S(6)} %mul.147), kind=kLoop, calls=%fused_computation.92 | loop fusion | flops 56 | bytes 76 | tf_op jit(solution)/shard_map/eq | solution.py:53
  1.5 3.4 %fusion.20 = f32[8,16,1024]{2,1,0:T(8,128)S(1)} fusion(f32[8,128,1024]{2,1,0:T(8,128)} %bitcast.122, f32[16,1024]{1,0:T(8,128)} %param.5), kind=kOutput, calls=%fused_computation.61 | convolution fusion | flops 100663296 | bytes 4784128 | tf_op jit(solution)/shard_map/tbr,brk->btk/dot_general | solution.py:46
  4.9 0.2 slice_select_fusion.6
  5.1 0.0 copy-start.3
  5.1 0.0 copy-start.2
  5.2 0.2 fusion
  5.4 0.2 fusion.1
  5.6 0.2 fusion.2
  5.8 0.2 fusion.3
  6.1 0.2 fusion.4
  6.3 0.2 fusion.5
  6.6 0.0 copy-done.3
  6.6 0.0 copy-done.2
  6.6 0.1 broadcast_multiply_fusion
  6.7 0.1 fusion.8
  6.8 4.9 %collective-permute-start = (f32[16,960]{1,0:T(8,128)S(1)}, f32[16,960]{1,0:T(8,128)S(1)}, u32[]{:S(2)}, u32[]{:S(2)}) collective-permute-start(f32[16,960]{1,0:T(8,128)S(1)} %get-tuple-element.23), channel_id=1, source_target_pairs={{0,4},{4,8},{8,12},{12,16},{16,20},{20,24},{24,28},{1,5},{5,9},{9,... | collective-permute-start | bytes 184328 | tf_op jit(solution)/shard_map/ppermute | solution.py:64
  11.7 1.3 %collective-permute-start.1 = (f32[16,960]{1,0:T(8,128)S(1)}, f32[16,960]{1,0:T(8,128)S(1)}, u32[]{:S(2)}, u32[]{:S(2)}) collective-permute-start(f32[16,960]{1,0:T(8,128)S(1)} %get-tuple-element.24), channel_id=1, source_target_pairs={{4,0},{8,4},{12,8},{16,12},{20,16},{24,20},{28,24},{5,1},{9,5},{13... | collective-permute-start | bytes 184328 | tf_op jit(solution)/shard_map/ppermute | solution.py:65
  13.0 0.6 collective-permute-done
  13.6 4.3 %collective-permute-done.1 = f32[16,960]{1,0:T(8,128)S(1)} collective-permute-done((f32[16,960]{1,0:T(8,128)S(1)}, f32[16,960]{1,0:T(8,128)S(1)}, u32[]{:S(2)}, u32[]{:S(2)}) %collective-permute-start.1) | collective-permute-done | bytes 61472 | tf_op jit(solution)/shard_map/ppermute | solution.py:65
  18.0 0.2 slice_select_fusion.5
  18.3 0.0 copy-start.1
  18.3 0.2 slice_select_fusion.4
  18.5 0.2 slice_select_fusion.3
  18.7 0.2 slice_select_fusion.2
  19.0 0.2 slice_select_fusion.1
  19.2 0.2 slice_select_fusion
  19.4 1.0 %copy-done.1 = f32[1024,1024]{1,0:T(8,128)S(1)} copy-done((f32[1024,1024]{1,0:T(8,128)S(1)}, f32[1024,1024]{1,0:T(8,128)}, u32[]{:S(2)}) %copy-start.1) | copy-done | bytes 4194328
  20.5 1.9 %convolution_bitcast_fusion.1 = f32[8,2,8,128]{3,2,1,0:T(8,128)S(1)} fusion(f32[8,128,1024]{2,1,0:T(8,128)S(1)} %bitcast.123, f32[8,16,1088]{2,1,0:T(8,128)S(1)} %slice_select_fusion, pred[8]{0:T(512)(128)(4,1)S(1)} %get-tuple-element.13), kind=kOutput, calls=%fused_computation.1 | convolution fusion | flops 100794368 | bytes 5308928 | tf_op jit(solution)/shard_map/btk,brk->tbr/dot_general | solution.py:36
  22.4 0.2 multiply_reduce_fusion.1
  22.6 12.1 %all_to_all.15 = f32[8,4,16]{2,1,0:T(4,128)S(1)} all-to-all(f32[8,4,16]{2,1,0:T(4,128)S(1)} %broadcast_in_dim.144), channel_id=1, replica_groups=mesh['snp'=8,'ind'=4] {'snp'}, dimensions={0} | all-to-all | bytes 4096 | tf_op jit(solution)/shard_map/all_to_all | solution.py:16
  34.8 0.7 %fusion.28 = (bf16[16,1024]{1,0:T(8,128)(2,1)S(1)}, f32[16,1024]{1,0:T(8,128)}) fusion(f32[16,1024]{1,0:T(8,128)S(1)} %copy-done.2, f32[16]{0:T(128)S(1)} %get-tuple-element.11, f32[16,1984]{1,0:T(8,128)S(1)} %pad_add_fusion.6, f32[16]{0:T(128)S(1)} %get-tuple-element.10, f32[16]{0:T(128)S(1)} %get-tuple-element.12), kind=kLoop, calls=%fused_computation.98 | loop fusion | flops 131072 | bytes 229568 | tf_op jit(solution)/shard_map/convert_element_type | solution.py:104
  35.5 5.4 %all_gather.3 = bf16[64,1024]{1,0:T(8,128)(2,1)S(1)} all-gather(bf16[16,1024]{1,0:T(8,128)(2,1)S(1)} %get-tuple-element.8), channel_id=1, replica_groups=mesh['snp'=8,'ind'=4] {'ind'}, dimensions={0}, use_global_device_ids=true | all-gather | bytes 163840 | tf_op jit(solution)/shard_map/all_gather | solution.py:104
  40.9 0.0 copy-done
  40.9 0.8 %convolution_bitcast_fusion = f32[8,8,8,128]{3,2,1,0:T(8,128)S(1)} fusion(bf16[64,1024]{1,0:T(8,128)(2,1)S(1)} %all_gather.3, bf16[1024,1024]{1,0:T(8,128)(2,1)S(1)} %copy-done), kind=kOutput, calls=%fused_computation | convolution fusion | flops 134217728 | bytes 2490368 | tf_op jit(solution)/shard_map/dot_general | solution.py:105
  41.7 12.1 %all_to_all.16 = f32[8,64,128]{2,1,0:T(8,128)S(1)} all-to-all(f32[8,64,128]{2,1,0:T(8,128)S(1)} %bitcast.124), channel_id=1, replica_groups=mesh['snp'=8,'ind'=4] {'snp'}, dimensions={0} | all-to-all | bytes 524288 | tf_op jit(solution)/shard_map/all_to_all | solution.py:111
  53.8 0.1 fusion.27
  53.9 0.2 multiply_reduce_fusion.3
  54.2 0.1 reshape.120
  54.3 10.5 %all_to_all.17 = f32[32,1,128]{2,1,0:T(1,128)S(1)} all-to-all(f32[32,1,128]{2,1,0:T(1,128)S(1)} %reshape.120), channel_id=1, replica_groups=mesh['snp'=8,'ind'=4] {'ind','snp'}, dimensions={0} | all-to-all | bytes 32768 | tf_op jit(solution)/shard_map/all_to_all | solution.py:118
  64.8 0.5 broadcast.179
  65.3 0.7 %reduce.3 = f32[32,128]{1,0:T(8,128)S(1)} reduce(f32[32,1,128]{2,1,0:T(1,128)S(1)} %all_to_all.17, f32[]{:T(128)} %broadcast.179), dimensions={1}, to_apply=%all_to_all.11.reduce_sub_computation | reduce | bytes 32772 | tf_op jit(solution)/shard_map/all_to_all | solution.py:118
  66.0 0.1 reshape.121
  66.2 0.7 %subtract_multiply_fusion = f32[64,128]{1,0:T(8,128)} fusion(f32[64,128]{1,0:T(8,128)S(1)} %get-tuple-element.3, f32[64]{0:T(128)S(1)} %add_rsqrt_fusion, f32[64]{0:T(128)S(1)} %broadcast_multiply_fusion.2), kind=kLoop, calls=%fused_computation.68 | loop fusion | flops 16384 | bytes 66048 | tf_op jit(solution)/shard_map/mul | solution.py:124
  (28 shorter events, 0.4 us)
Async XLA Ops:
  0.6 40.3 %copy-start = (bf16[1024,1024]{1,0:T(8,128)(2,1)S(1)}, bf16[1024,1024]{1,0:T(8,128)(2,1)}, u32[]{:S(2)}) copy-start(bf16[1024,1024]{1,0:T(8,128)(2,1)} %param.9) | copy-start | bytes 6291460
  5.1 1.5 %copy-start.3 = (f32[16]{0:T(128)S(1)}, f32[16]{0:T(128)}, u32[]{:S(2)}) copy-start(f32[16]{0:T(128)} %param.8) | copy-start | bytes 196
  5.1 1.5 %copy-start.2 = (f32[16,1024]{1,0:T(8,128)S(1)}, f32[16,1024]{1,0:T(8,128)}, u32[]{:S(2)}) copy-start(f32[16,1024]{1,0:T(8,128)} %param.5) | copy-start | bytes 196612
  6.8 6.8 %collective-permute-start = (f32[16,960]{1,0:T(8,128)S(1)}, f32[16,960]{1,0:T(8,128)S(1)}, u32[]{:S(2)}, u32[]{:S(2)}) collective-permute-start(f32[16,960]{1,0:T(8,128)S(1)} %get-tuple-element.23), channel_id=1, source_target_pairs={{0,4},{4,8},{8,12},{12,16},{16,20},{20,24},{24,28},{1,5},{5,9},{9,... | collective-permute-start | bytes 184328 | tf_op jit(solution)/shard_map/ppermute | solution.py:64
  11.7 6.2 %collective-permute-start.1 = (f32[16,960]{1,0:T(8,128)S(1)}, f32[16,960]{1,0:T(8,128)S(1)}, u32[]{:S(2)}, u32[]{:S(2)}) collective-permute-start(f32[16,960]{1,0:T(8,128)S(1)} %get-tuple-element.24), channel_id=1, source_target_pairs={{4,0},{8,4},{12,8},{16,12},{20,16},{24,20},{28,24},{5,1},{9,5},{13... | collective-permute-start | bytes 184328 | tf_op jit(solution)/shard_map/ppermute | solution.py:65
  18.3 2.2 %copy-start.1 = (f32[1024,1024]{1,0:T(8,128)S(1)}, f32[1024,1024]{1,0:T(8,128)}, u32[]{:S(2)}) copy-start(f32[1024,1024]{1,0:T(8,128)} %param.6) | copy-start | bytes 12582916

commit v6 on v4

--- a/solution.py
+++ b/solution.py
@@ -33,7 +33,7 @@
     blocks_here = ld_band.shape[0] // BLK
     windows = windows_of(extended, shifts, band_cols, blocks_here)
     blocks = ld_band.reshape(blocks_here, BLK, band_cols)
-    product = jnp.einsum("btk,brk->tbr", windows, blocks, precision=lax.Precision.HIGHEST)
+    product = jnp.einsum("btk,brk->tbr", windows, blocks, precision=lax.Precision.HIGH)
     return product.reshape(vector.shape) + ridge_shift[:, None] * vector
 
 
@@ -45,7 +45,7 @@
     blocks = ld_band.reshape(blocks_here, BLK, band_cols)
     pieces = jnp.einsum(
         "tbr,brk->btk", vector.reshape(traits, blocks_here, BLK), blocks,
-        precision=lax.Precision.HIGHEST,
+        precision=lax.Precision.HIGH,
     )
     wide = jnp.pad(pieces, ((0, 0), (0, 0), (0, span - band_cols)))
     for bit in range(SHIFT_BITS):
@@ -80,11 +80,6 @@
     ridge_shift = M_GENOME / N_GWAS / heritability
     extended = spread_operator(beta_hat, ld_band, shifts, ridge_shift, halo)
     image = extended[:, halo : halo + rows_here]
-    pair = jnp.concatenate([beta_hat, image], axis=0)
-    arrived = [pair] + [
-        lax.ppermute(pair, "ind", [(j, (j + k) % n_ind) for j in range(n_ind)])
-        for k in range(1, n_ind)
-    ]
     image2 = apply_operator(extended, image, ld_band, shifts, ridge_shift)
 
     moments = jnp.stack(
@@ -98,10 +93,8 @@
     placed = jnp.zeros((4, traits), jnp.float32)
     placed = lax.dynamic_update_slice_in_dim(placed, moments, me_ind * traits_here, 1)
     m0, m1, m2, m3 = all_sum(placed, ("ind", "snp"), n_all)
-    slots = (me_ind - jnp.arange(n_ind)) % n_ind
-    ordered = jnp.take(jnp.stack(arrived), slots, axis=0)
-    beta_all = ordered[:, :traits_here].reshape(traits, rows_here)
-    image_all = ordered[:, traits_here:].reshape(traits, rows_here)
+    pair = lax.all_gather(jnp.stack([beta_hat, image]), "ind", axis=1, tiled=True)
+    beta_all, image_all = pair[0], pair[1]
 
     alpha1 = m0 / m1
     norm1 = alpha1 * alpha1 * m2 - m0

time: 70.8 us -> 68.4 us (0.966)
  blocking collectives: 0 us -> 7.67 us
  waiting for transfers between devices: 24.8 us -> 20.4 us
  matrix products: 8.98 us -> 6.75 us
  starting transfers between devices: 22.9 us -> 20.8 us
  local copies, waits for them, and re-layouts: 4.71 us -> 3.82 us
    all_gather x0 -> x1, blocking collectives: none -> 7.67 us  [local(): lax.all_gather(jnp.stack([beta_hat, image]), 'ind', axis=1, tiled=True)]
    all_to_all x1, waiting for transfers between devices: 3.88 us -> 0.01 us  [all_sum(): return jnp.sum(lax.all_to_all(sent, axes, 0, 0, tiled=True), axis=0)]
    ppermute x3 -> x0, starting transfers between devices: 3.28 us -> none  [local(): lax.ppermute(pair, 'ind', [(j, (j + k) % n_ind) for j in range(n_ind)])]
    dot_general x1, matrix products: 3.66 us -> 1.9 us  [apply_operator(): jnp.einsum('btk,brk->tbr', windows, blocks, precision=lax.Precision.HIGH)]
    all_to_all x1, starting transfers between devices: 4.49 us -> 5.32 us  [local(): complete = jnp.sum(lax.all_to_all(chunks, 'snp', 0, 0, tiled=True), axis=0)]
  transfers between devices with their start and end apart: 8 -> 5, of which waited for: 5 -> 4; matrix products, arithmetic and copies ran while one was open for 4% -> 1% of each run, Pallas kernels for 0% -> 0%
where the time goes in v6:
time: 68.4 us; the launch traced here: 67.9 us
  starting transfers between devices  20.8 us (30%)
  waiting for transfers between devices  20.4 us (30%)
  blocking collectives  7.67 us (11%)
  other arithmetic  7.51 us (11%)
  matrix products  6.75 us (10%)
  local copies, waits for them, and re-layouts  3.82 us (6%)
  between operations  1 us (1%)
    all_to_all x1, waiting for transfers between devices, local(): complete = jnp.sum(lax.all_to_all(chunks, 'snp', 0, 0, tiled=True), axis=0)  9.16 us
    all_gather x1, blocking collectives, local(): lax.all_gather(jnp.stack([beta_hat, image]), 'ind', axis=1, tiled=True)  7.67 us
    all_to_all x1, waiting for transfers between devices, local(): every = lax.all_to_all(sent, ('ind', 'snp'), 0, 0, tiled=True)  6.35 us
    all_to_all x1, starting transfers between devices, all_sum(): return jnp.sum(lax.all_to_all(sent, axes, 0, 0, tiled=True), axis=0)  5.84 us
    all_to_all x1, starting transfers between devices, local(): complete = jnp.sum(lax.all_to_all(chunks, 'snp', 0, 0, tiled=True), axis=0)  5.32 us
    ppermute x1, starting transfers between devices, spread_operator(): from_left = lax.ppermute(own[:, rows:], 'snp', forward)  4.9 us
    ppermute x1, waiting for transfers between devices, spread_operator(): from_right = lax.ppermute(own[:, :2 * halo], 'snp', backward)  4.27 us
    all_to_all x1, starting transfers between devices, local(): every = lax.all_to_all(sent, ('ind', 'snp'), 0, 0, tiled=True)  3.49 us
  transfers between devices with their start and end apart: 5, of which 4 were waited for; matrix products, arithmetic and copies ran while one was open for 1% of the time, Pallas kernels for 0%

profile of v6, /device:TPU:0, one launch (start us, length us, event | category | flops | bytes accessed | tf_op | source)
XLA Modules:
  0.0 67.9 jit_solution(8429423919728142297)
XLA Ops:
  0.6 0.0 copy-start
  0.7 0.8 %and_compare_fusion.6 = (pred[8]{0:T(512)(128)(4,1)S(1)}, s32[8]{0:T(128)S(1)}) fusion(s32[8]{0:T(128)} %param.7, s32[]{:T(128)S(6)} %mul.172), kind=kLoop, calls=%fused_computation.103 | loop fusion | flops 56 | bytes 76 | tf_op jit(solution)/shard_map/eq | solution.py:53
  1.5 3.4 %fusion.23 = f32[8,16,1024]{2,1,0:T(8,128)S(1)} fusion(f32[8,128,1024]{2,1,0:T(8,128)} %bitcast.128, f32[16,1024]{1,0:T(8,128)} %param.5), kind=kOutput, calls=%fused_computation.67 | convolution fusion | flops 100663296 | bytes 4784128 | tf_op jit(solution)/shard_map/tbr,brk->btk/dot_general | solution.py:46
  4.9 0.2 slice_select_fusion.6
  5.1 0.0 copy-start.3
  5.2 0.2 fusion
  5.4 0.2 fusion.1
  5.6 0.2 fusion.2
  5.8 0.2 fusion.3
  6.1 0.2 fusion.4
  6.3 0.2 fusion.5
  6.6 0.1 broadcast_multiply_fusion
  6.7 0.1 fusion.8
  6.8 4.9 %collective-permute-start = (f32[16,960]{1,0:T(8,128)S(1)}, f32[16,960]{1,0:T(8,128)S(1)}, u32[]{:S(2)}, u32[]{:S(2)}) collective-permute-start(f32[16,960]{1,0:T(8,128)S(1)} %get-tuple-element.24), channel_id=1, source_target_pairs={{0,4},{4,8},{8,12},{12,16},{16,20},{20,24},{24,28},{1,5},{5,9},{9,... | collective-permute-start | bytes 184328 | tf_op jit(solution)/shard_map/ppermute | solution.py:64
  11.7 1.3 %collective-permute-start.1 = (f32[16,960]{1,0:T(8,128)S(1)}, f32[16,960]{1,0:T(8,128)S(1)}, u32[]{:S(2)}, u32[]{:S(2)}) collective-permute-start(f32[16,960]{1,0:T(8,128)S(1)} %get-tuple-element.25), channel_id=1, source_target_pairs={{4,0},{8,4},{12,8},{16,12},{20,16},{24,20},{28,24},{5,1},{9,5},{13... | collective-permute-start | bytes 184328 | tf_op jit(solution)/shard_map/ppermute | solution.py:65
  13.0 0.6 collective-permute-done
  13.6 4.3 %collective-permute-done.1 = f32[16,960]{1,0:T(8,128)S(1)} collective-permute-done((f32[16,960]{1,0:T(8,128)S(1)}, f32[16,960]{1,0:T(8,128)S(1)}, u32[]{:S(2)}, u32[]{:S(2)}) %collective-permute-start.1) | collective-permute-done | bytes 61472 | tf_op jit(solution)/shard_map/ppermute | solution.py:65
  18.0 0.2 slice_select_fusion.5
  18.3 0.2 slice_select_fusion.4
  18.5 0.2 slice_select_fusion.3
  18.7 0.2 slice_select_fusion.2
  19.0 0.2 slice_select_fusion.1
  19.2 0.2 slice_select_fusion
  19.4 1.0 %copy-done.1 = f32[1024,1024]{1,0:T(8,128)S(1)} copy-done((f32[1024,1024]{1,0:T(8,128)S(1)}, f32[1024,1024]{1,0:T(8,128)}, u32[]{:S(2)}) %copy-start.1) | copy-done | bytes 4194328
  20.5 1.9 %convolution_bitcast_fusion.1 = f32[8,2,8,128]{3,2,1,0:T(8,128)S(1)} fusion(f32[8,128,1024]{2,1,0:T(8,128)S(1)} %bitcast.129, f32[8,16,1088]{2,1,0:T(8,128)S(1)} %slice_select_fusion, pred[8]{0:T(512)(128)(4,1)S(1)} %get-tuple-element.11), kind=kOutput, calls=%fused_computation.1 | convolution fusion | flops 100794368 | bytes 5308928 | tf_op jit(solution)/shard_map/btk,brk->tbr/dot_general | solution.py:36
  22.4 0.2 multiply_reduce_fusion.1
  22.6 0.1 dynamic_update_slice.5
  22.8 0.7 %reshape.152 = f32[32,1,256]{2,1,0:T(1,128)} reshape(f32[32,4,64]{2,1,0:T(4,128)S(1)} %broadcast_in_dim.148) | data formatting | bytes 65536
  23.5 5.8 %all-to-all-start = ((f32[32,1,256]{2,1,0:T(1,128)}), f32[32,1,256]{2,1,0:T(1,128)S(1)}, u32[]{:S(2)}, u32[]{:S(2)}) async-start(f32[32,1,256]{2,1,0:T(1,128)} %reshape.152), calls=%async_computation | async-start | bytes 65536 | tf_op jit(solution)/shard_map/all_to_all | solution.py:16
  29.4 7.7 %all_gather.3 = f32[2,64,1024]{2,1,0:T(8,128)S(1)} all-gather(f32[2,16,1024]{2,1,0:T(8,128)S(1)} %pad_maximum_fusion), channel_id=1, replica_groups=mesh['snp'=8,'ind'=4] {'ind'}, dimensions={1}, use_global_device_ids=true | all-gather | bytes 655360 | tf_op jit(solution)/shard_map/all_gather | solution.py:96
  37.1 0.6 broadcast.183
  37.6 0.7 %reduce.3 = f32[32,256]{1,0:T(8,128)S(1)} reduce(f32[32,1,256]{2,1,0:T(1,128)S(1)} %all-to-all-done, f32[]{:T(128)} %broadcast.183), dimensions={1}, to_apply=%all_to_all.9.reduce_sub_computation | reduce | bytes 65540 | tf_op jit(solution)/shard_map/all_to_all | solution.py:16
  38.3 0.1 reshape.153
  38.5 1.5 %convolution_bitcast_fusion = f32[8,64,128]{2,1,0:T(8,128)} fusion(bf16[8,128,1024]{2,1,0:T(8,128)(2,1)S(1)} %bitcast.127, f32[2,64,1024]{2,1,0:T(8,128)S(1)} %all_gather.3, f32[64]{0:T(128)S(1)} %get-tuple-element.9, f32[64]{0:T(128)S(1)} %get-tuple-element.8, f32[64]{0:T(128)S(1)} %get-tuple-element.10), kind=kOutput, calls=%fused_computation | convolution fusion | flops 134742016 | bytes 2884352 | tf_op jit(solution)/shard_map/dot_general | solution.py:111
  40.0 5.3 %all-to-all-start.1 = ((f32[8,64,128]{2,1,0:T(8,128)}), f32[8,64,128]{2,1,0:T(8,128)S(1)}, u32[]{:S(2)}, u32[]{:S(2)}) async-start(f32[8,64,128]{2,1,0:T(8,128)} %convolution_bitcast_fusion), calls=%async_computation.1 | async-start | bytes 524288 | tf_op jit(solution)/shard_map/all_to_all | solution.py:117
  45.3 0.1 dynamic-slice
  45.4 0.1 dynamic-slice.1
  45.5 0.1 dynamic-slice.2
  45.6 9.2 %all-to-all-done.1 = f32[8,64,128]{2,1,0:T(8,128)S(1)} async-done(((f32[8,64,128]{2,1,0:T(8,128)}), f32[8,64,128]{2,1,0:T(8,128)S(1)}, u32[]{:S(2)}, u32[]{:S(2)}) %all-to-all-start.1) | async-done | bytes 262176 | tf_op jit(solution)/shard_map/all_to_all | solution.py:117
  54.7 0.1 fusion.34
  54.9 0.2 multiply_reduce_fusion.3
  55.1 0.7 %reshape.154 = f32[32,1,128]{2,1,0:T(1,128)} reshape(f32[32,2,64]{2,1,0:T(2,128)S(1)} %broadcast_in_dim.149) | data formatting | bytes 32768
  55.8 3.5 %all-to-all-start.2 = ((f32[32,1,128]{2,1,0:T(1,128)}), f32[32,1,128]{2,1,0:T(1,128)S(1)}, u32[]{:S(2)}, u32[]{:S(2)}) async-start(f32[32,1,128]{2,1,0:T(1,128)} %reshape.154), calls=%async_computation.2 | async-start | bytes 32768 | tf_op jit(solution)/shard_map/all_to_all | solution.py:124
  59.3 0.7 %fusion.29 = f32[16,1024]{1,0:T(8,128)} fusion(f32[64,1024]{1,0:T(8,128)S(1)} %get-tuple-element.22, s32[]{:T(128)S(6)} %select_n.68, f32[64,1024]{1,0:T(8,128)S(1)} %get-tuple-element.21, f32[16]{0:T(128)S(1)} %dynamic-slice.2, f32[16]{0:T(128)S(1)} %dynamic-slice.1, f32[16]{0:T(128)S(1)} %dynamic-slice), kind=kLoop, calls=%fused_computation.74 | loop fusion | flops 114688 | bytes 196804 | tf_op jit(solution)/shard_map/add | solution.py:107
  60.0 6.3 %all-to-all-done.2 = f32[32,1,128]{2,1,0:T(1,128)S(1)} async-done(((f32[32,1,128]{2,1,0:T(1,128)}), f32[32,1,128]{2,1,0:T(1,128)S(1)}, u32[]{:S(2)}, u32[]{:S(2)}) %all-to-all-start.2) | async-done | bytes 16416 | tf_op jit(solution)/shard_map/all_to_all | solution.py:124
  66.3 0.7 reduce.4
  67.0 0.1 reshape.155
  67.2 0.7 %subtract_multiply_fusion = f32[64,128]{1,0:T(8,128)} fusion(f32[64,128]{1,0:T(8,128)S(1)} %get-tuple-element.3, f32[64]{0:T(128)S(1)} %add_rsqrt_fusion, f32[64]{0:T(128)S(1)} %broadcast_multiply_fusion.2), kind=kLoop, calls=%fused_computation.79 | loop fusion | flops 16384 | bytes 66048 | tf_op jit(solution)/shard_map/mul | solution.py:130
  (36 shorter events, 0.5 us)
Async XLA Ops:
  0.6 37.9 %copy-start = (bf16[1024,1024]{1,0:T(8,128)(2,1)S(1)}, bf16[1024,1024]{1,0:T(8,128)(2,1)}, u32[]{:S(2)}) copy-start(bf16[1024,1024]{1,0:T(8,128)(2,1)} %param.9) | copy-start | bytes 6291460
  5.1 1.5 %copy-start.3 = (f32[16]{0:T(128)S(1)}, f32[16]{0:T(128)}, u32[]{:S(2)}) copy-start(f32[16]{0:T(128)} %param.8) | copy-start | bytes 196
  5.1 1.5 %copy-start.2 = (f32[16,1024]{1,0:T(8,128)S(1)}, f32[16,1024]{1,0:T(8,128)}, u32[]{:S(2)}) copy-start(f32[16,1024]{1,0:T(8,128)} %param.5) | copy-start | bytes 196612
  6.8 6.8 %collective-permute-start = (f32[16,960]{1,0:T(8,128)S(1)}, f32[16,960]{1,0:T(8,128)S(1)}, u32[]{:S(2)}, u32[]{:S(2)}) collective-permute-start(f32[16,960]{1,0:T(8,128)S(1)} %get-tuple-element.24), channel_id=1, source_target_pairs={{0,4},{4,8},{8,12},{12,16},{16,20},{20,24},{24,28},{1,5},{5,9},{9,... | collective-permute-start | bytes 184328 | tf_op jit(solution)/shard_map/ppermute | solution.py:64
  11.7 6.2 %collective-permute-start.1 = (f32[16,960]{1,0:T(8,128)S(1)}, f32[16,960]{1,0:T(8,128)S(1)}, u32[]{:S(2)}, u32[]{:S(2)}) collective-permute-start(f32[16,960]{1,0:T(8,128)S(1)} %get-tuple-element.25), channel_id=1, source_target_pairs={{4,0},{8,4},{12,8},{16,12},{20,16},{24,20},{28,24},{5,1},{9,5},{13... | collective-permute-start | bytes 184328 | tf_op jit(solution)/shard_map/ppermute | solution.py:65
  18.3 2.2 %copy-start.1 = (f32[1024,1024]{1,0:T(8,128)S(1)}, f32[1024,1024]{1,0:T(8,128)}, u32[]{:S(2)}) copy-start(f32[1024,1024]{1,0:T(8,128)} %param.6) | copy-start | bytes 12582916
  23.5 13.5 %all-to-all-start = ((f32[32,1,256]{2,1,0:T(1,128)}), f32[32,1,256]{2,1,0:T(1,128)S(1)}, u32[]{:S(2)}, u32[]{:S(2)}) async-start(f32[32,1,256]{2,1,0:T(1,128)} %reshape.152), calls=%async_computation | async-start | bytes 65536 | tf_op jit(solution)/shard_map/all_to_all | solution.py:16
  40.0 14.8 %all-to-all-start.1 = ((f32[8,64,128]{2,1,0:T(8,128)}), f32[8,64,128]{2,1,0:T(8,128)S(1)}, u32[]{:S(2)}, u32[]{:S(2)}) async-start(f32[8,64,128]{2,1,0:T(8,128)} %convolution_bitcast_fusion), calls=%async_computation.1 | async-start | bytes 524288 | tf_op jit(solution)/shard_map/all_to_all | solution.py:117
  55.8 10.6 %all-to-all-start.2 = ((f32[32,1,128]{2,1,0:T(1,128)}), f32[32,1,128]{2,1,0:T(1,128)S(1)}, u32[]{:S(2)}, u32[]{:S(2)}) async-start(f32[32,1,128]{2,1,0:T(1,128)} %reshape.154), calls=%async_computation.2 | async-start | bytes 32768 | tf_op jit(solution)/shard_map/all_to_all | solution.py:124

commit v7 on v6

--- a/solution.py
+++ b/solution.py
@@ -114,6 +114,7 @@
     inds_here = genotypes.shape[0]
     share = inds_here // n_snp
     chunks = partial.reshape(traits, n_snp, share).transpose(1, 0, 2)
+    weights, chunks = lax.optimization_barrier((weights, chunks))
     complete = jnp.sum(lax.all_to_all(chunks, "snp", 0, 0, tiled=True), axis=0)
     count = inds_here * n_ind
     local_sum = jnp.sum(complete, axis=1)

time: 68.4 us -> 67.6 us (0.988)
  blocking collectives: 7.67 us -> 32.6 us
  waiting for transfers between devices: 20.4 us -> 4.86 us
  starting transfers between devices: 20.8 us -> 12 us
  matrix products: 6.75 us -> 6.04 us
    all_to_all x0 -> x2, blocking collectives: none -> 25 us  [the longest x1 14.5 us: local(): complete = jnp.sum(lax.all_to_all(chunks, 'snp', 0, 0, tiled=True), axis=0)]
    all_to_all x2 -> x0, waiting for transfers between devices: 15.5 us -> none  [the longest x1 9.16 us: local(): complete = jnp.sum(lax.all_to_all(chunks, 'snp', 0, 0, tiled=True), axis=0)]
    all_to_all x2 -> x0, starting transfers between devices: 8.81 us -> none  [the longest x1 5.32 us: local(): complete = jnp.sum(lax.all_to_all(chunks, 'snp', 0, 0, tiled=True), axis=0)]
    dot_general x1, matrix products: 1.47 us -> 0.76 us  [local(): lax.dot_general(rounded, genotypes, (((1,), (1,)), ((), ())), preferred_e...]
  transfers between devices with their start and end apart: 5 -> 3, of which waited for: 4 -> 2; matrix products, arithmetic and copies ran while one was open for 1% -> 0% of each run, Pallas kernels for 0% -> 0%
where the time goes in v7:
time: 67.6 us; the launch traced here: 67.3 us
  blocking collectives  32.6 us (48%)
  starting transfers between devices  12 us (18%)
  other arithmetic  7.56 us (11%)
  matrix products  6.04 us (9%)
  waiting for transfers between devices  4.86 us (7%)
  local copies, waits for them, and re-layouts  3.15 us (5%)
  between operations  1 us (1%)
    all_to_all x1, blocking collectives, local(): complete = jnp.sum(lax.all_to_all(chunks, 'snp', 0, 0, tiled=True), axis=0)  14.5 us
    all_to_all x1, blocking collectives, local(): every = lax.all_to_all(sent, ('ind', 'snp'), 0, 0, tiled=True)  10.4 us
    all_gather x1, blocking collectives, local(): lax.all_gather(jnp.stack([beta_hat, image]), 'ind', axis=1, tiled=True)  7.67 us
    all_to_all x1, starting transfers between devices, all_sum(): return jnp.sum(lax.all_to_all(sent, axes, 0, 0, tiled=True), axis=0)  5.84 us
    ppermute x1, starting transfers between devices, spread_operator(): from_left = lax.ppermute(own[:, rows:], 'snp', forward)  4.9 us
    ppermute x1, waiting for transfers between devices, spread_operator(): from_right = lax.ppermute(own[:, :2 * halo], 'snp', backward)  4.27 us
    dot_general x1, matrix products, spread_operator(): jnp.einsum('tbr,brk->btk', vector.reshape(traits, blocks_here, BLK), bloc...  3.38 us
    unnamed x19, local copies, waits for them, and re-layouts  2.1 us
  transfers between devices with their start and end apart: 3, of which 2 were waited for; matrix products, arithmetic and copies ran while one was open for 0% of the time, Pallas kernels for 0%

profile of v7, /device:TPU:0, one launch (start us, length us, event | category | flops | bytes accessed | tf_op | source)
XLA Modules:
  0.0 67.3 jit_solution(5465073824410674805)
XLA Ops:
  0.6 0.0 copy-start
  0.7 0.8 %and_compare_fusion.6 = (pred[8]{0:T(512)(128)(4,1)S(1)}, s32[8]{0:T(128)S(1)}) fusion(s32[8]{0:T(128)} %param.7, s32[]{:T(128)S(6)} %mul.172), kind=kLoop, calls=%fused_computation.103 | loop fusion | flops 56 | bytes 76 | tf_op jit(solution)/shard_map/eq | solution.py:53
  1.5 3.4 %fusion.23 = f32[8,16,1024]{2,1,0:T(8,128)S(1)} fusion(f32[8,128,1024]{2,1,0:T(8,128)} %bitcast.128, f32[16,1024]{1,0:T(8,128)} %param.5), kind=kOutput, calls=%fused_computation.67 | convolution fusion | flops 100663296 | bytes 4784128 | tf_op jit(solution)/shard_map/tbr,brk->btk/dot_general | solution.py:46
  4.9 0.2 slice_select_fusion.6
  5.1 0.0 copy-start.3
  5.1 0.0 copy-start.2
  5.2 0.2 fusion
  5.4 0.2 fusion.1
  5.6 0.2 fusion.2
  5.8 0.2 fusion.3
  6.1 0.2 fusion.4
  6.3 0.2 fusion.5
  6.6 0.1 broadcast_multiply_fusion
  6.7 0.1 fusion.8
  6.8 4.9 %collective-permute-start = (f32[16,960]{1,0:T(8,128)S(1)}, f32[16,960]{1,0:T(8,128)S(1)}, u32[]{:S(2)}, u32[]{:S(2)}) collective-permute-start(f32[16,960]{1,0:T(8,128)S(1)} %get-tuple-element.28), channel_id=1, source_target_pairs={{0,4},{4,8},{8,12},{12,16},{16,20},{20,24},{24,28},{1,5},{5,9},{9,... | collective-permute-start | bytes 184328 | tf_op jit(solution)/shard_map/ppermute | solution.py:64
  11.7 1.3 %collective-permute-start.1 = (f32[16,960]{1,0:T(8,128)S(1)}, f32[16,960]{1,0:T(8,128)S(1)}, u32[]{:S(2)}, u32[]{:S(2)}) collective-permute-start(f32[16,960]{1,0:T(8,128)S(1)} %get-tuple-element.29), channel_id=1, source_target_pairs={{4,0},{8,4},{12,8},{16,12},{20,16},{24,20},{28,24},{5,1},{9,5},{13... | collective-permute-start | bytes 184328 | tf_op jit(solution)/shard_map/ppermute | solution.py:65
  13.0 0.6 collective-permute-done
  13.6 4.3 %collective-permute-done.1 = f32[16,960]{1,0:T(8,128)S(1)} collective-permute-done((f32[16,960]{1,0:T(8,128)S(1)}, f32[16,960]{1,0:T(8,128)S(1)}, u32[]{:S(2)}, u32[]{:S(2)}) %collective-permute-start.1) | collective-permute-done | bytes 61472 | tf_op jit(solution)/shard_map/ppermute | solution.py:65
  18.0 0.2 slice_select_fusion.5
  18.3 0.0 copy-start.1
  18.3 0.2 slice_select_fusion.4
  18.5 0.2 slice_select_fusion.3
  18.7 0.2 slice_select_fusion.2
  19.0 0.2 slice_select_fusion.1
  19.2 0.2 slice_select_fusion
  19.4 1.0 %copy-done.1 = f32[1024,1024]{1,0:T(8,128)S(1)} copy-done((f32[1024,1024]{1,0:T(8,128)S(1)}, f32[1024,1024]{1,0:T(8,128)}, u32[]{:S(2)}) %copy-start.1) | copy-done | bytes 4194328
  20.5 1.9 %convolution_bitcast_fusion.1 = f32[8,2,8,128]{3,2,1,0:T(8,128)S(1)} fusion(f32[8,128,1024]{2,1,0:T(8,128)S(1)} %bitcast.129, f32[8,16,1088]{2,1,0:T(8,128)S(1)} %slice_select_fusion, pred[8]{0:T(512)(128)(4,1)S(1)} %get-tuple-element.15), kind=kOutput, calls=%fused_computation.1 | convolution fusion | flops 100794368 | bytes 5308928 | tf_op jit(solution)/shard_map/btk,brk->tbr/dot_general | solution.py:36
  22.4 0.2 multiply_reduce_fusion.1
  22.6 0.1 dynamic_update_slice.5
  22.8 0.7 %reshape.152 = f32[32,1,256]{2,1,0:T(1,128)} reshape(f32[32,4,64]{2,1,0:T(4,128)S(1)} %broadcast_in_dim.148) | data formatting | bytes 65536
  23.5 5.8 %all-to-all-start = ((f32[32,1,256]{2,1,0:T(1,128)}), f32[32,1,256]{2,1,0:T(1,128)S(1)}, u32[]{:S(2)}, u32[]{:S(2)}) async-start(f32[32,1,256]{2,1,0:T(1,128)} %reshape.152), calls=%async_computation | async-start | bytes 65536 | tf_op jit(solution)/shard_map/all_to_all | solution.py:16
  29.4 7.7 %all_gather.3 = f32[2,64,1024]{2,1,0:T(8,128)S(1)} all-gather(f32[2,16,1024]{2,1,0:T(8,128)S(1)} %pad_maximum_fusion), channel_id=1, replica_groups=mesh['snp'=8,'ind'=4] {'ind'}, dimensions={1}, use_global_device_ids=true | all-gather | bytes 655360 | tf_op jit(solution)/shard_map/all_gather | solution.py:96
  37.1 0.5 broadcast.183
  37.6 0.7 %reduce.3 = f32[32,256]{1,0:T(8,128)S(1)} reduce(f32[32,1,256]{2,1,0:T(1,128)S(1)} %all-to-all-done, f32[]{:T(128)} %broadcast.183), dimensions={1}, to_apply=%all_to_all.9.reduce_sub_computation | reduce | bytes 65540 | tf_op jit(solution)/shard_map/all_to_all | solution.py:16
  38.4 0.1 reshape.153
  38.5 0.1 dynamic-slice
  38.6 0.1 dynamic-slice.1
  38.7 0.1 dynamic-slice.2
  38.7 0.8 %convolution_bitcast_fusion = f32[8,64,128]{2,1,0:T(8,128)S(1)} fusion(bf16[8,128,1024]{2,1,0:T(8,128)(2,1)S(1)} %bitcast.127, f32[2,64,1024]{2,1,0:T(8,128)S(1)} %all_gather.3, f32[64]{0:T(128)S(1)} %get-tuple-element.13, f32[64]{0:T(128)S(1)} %get-tuple-element.12, f32[64]{0:T(128)S(1)} %get-tuple-element.14), kind=kOutput, calls=%fused_computation | convolution fusion | flops 134742016 | bytes 2884352 | tf_op jit(solution)/shard_map/dot_general | solution.py:111
  39.5 0.7 %fusion.29 = f32[16,1024]{1,0:T(8,128)} fusion(f32[64,1024]{1,0:T(8,128)S(1)} %get-tuple-element.26, s32[]{:T(128)S(6)} %select_n.68, f32[64,1024]{1,0:T(8,128)S(1)} %get-tuple-element.25, f32[16]{0:T(128)S(1)} %dynamic-slice.2, f32[16]{0:T(128)S(1)} %dynamic-slice.1, f32[16]{0:T(128)S(1)} %dynamic-slice), kind=kLoop, calls=%fused_computation.74 | loop fusion | flops 114688 | bytes 196804 | tf_op jit(solution)/shard_map/add | solution.py:107
  40.2 14.5 %all_to_all.15 = f32[8,64,128]{2,1,0:T(8,128)S(1)} all-to-all(f32[8,64,128]{2,1,0:T(8,128)S(1)} %convolution_bitcast_fusion), channel_id=1, replica_groups=mesh['snp'=8,'ind'=4] {'snp'}, dimensions={0} | all-to-all | bytes 524288 | tf_op jit(solution)/shard_map/all_to_all | solution.py:118
  54.8 0.1 fusion.34
  54.9 0.2 multiply_reduce_fusion.3
  55.1 0.1 reshape.154
  55.2 10.4 %all_to_all.16 = f32[32,1,128]{2,1,0:T(1,128)S(1)} all-to-all(f32[32,1,128]{2,1,0:T(1,128)S(1)} %reshape.154), channel_id=1, replica_groups=mesh['snp'=8,'ind'=4] {'ind','snp'}, dimensions={0} | all-to-all | bytes 32768 | tf_op jit(solution)/shard_map/all_to_all | solution.py:125
  65.7 0.7 %reduce.4 = f32[32,128]{1,0:T(8,128)S(1)} reduce(f32[32,1,128]{2,1,0:T(1,128)S(1)} %all_to_all.16, f32[]{:T(128)} %broadcast.183), dimensions={1}, to_apply=%all_to_all.11.reduce_sub_computation | reduce | bytes 32772 | tf_op jit(solution)/shard_map/all_to_all | solution.py:125
  66.4 0.1 reshape.155
  66.6 0.7 %subtract_multiply_fusion = f32[64,128]{1,0:T(8,128)} fusion(f32[64,128]{1,0:T(8,128)S(1)} %get-tuple-element.7, f32[64]{0:T(128)S(1)} %add_rsqrt_fusion, f32[64]{0:T(128)S(1)} %broadcast_multiply_fusion.2), kind=kLoop, calls=%fused_computation.79 | loop fusion | flops 16384 | bytes 66048 | tf_op jit(solution)/shard_map/mul | solution.py:131
  (34 shorter events, 0.5 us)
Async XLA Ops:
  0.6 38.1 %copy-start = (bf16[1024,1024]{1,0:T(8,128)(2,1)S(1)}, bf16[1024,1024]{1,0:T(8,128)(2,1)}, u32[]{:S(2)}) copy-start(bf16[1024,1024]{1,0:T(8,128)(2,1)} %param.9) | copy-start | bytes 6291460
  5.1 1.5 %copy-start.3 = (f32[16]{0:T(128)S(1)}, f32[16]{0:T(128)}, u32[]{:S(2)}) copy-start(f32[16]{0:T(128)} %param.8) | copy-start | bytes 196
  5.1 1.5 %copy-start.2 = (f32[16,1024]{1,0:T(8,128)S(1)}, f32[16,1024]{1,0:T(8,128)}, u32[]{:S(2)}) copy-start(f32[16,1024]{1,0:T(8,128)} %param.5) | copy-start | bytes 196612
  6.8 6.8 %collective-permute-start = (f32[16,960]{1,0:T(8,128)S(1)}, f32[16,960]{1,0:T(8,128)S(1)}, u32[]{:S(2)}, u32[]{:S(2)}) collective-permute-start(f32[16,960]{1,0:T(8,128)S(1)} %get-tuple-element.28), channel_id=1, source_target_pairs={{0,4},{4,8},{8,12},{12,16},{16,20},{20,24},{24,28},{1,5},{5,9},{9,... | collective-permute-start | bytes 184328 | tf_op jit(solution)/shard_map/ppermute | solution.py:64
  11.7 6.2 %collective-permute-start.1 = (f32[16,960]{1,0:T(8,128)S(1)}, f32[16,960]{1,0:T(8,128)S(1)}, u32[]{:S(2)}, u32[]{:S(2)}) collective-permute-start(f32[16,960]{1,0:T(8,128)S(1)} %get-tuple-element.29), channel_id=1, source_target_pairs={{4,0},{8,4},{12,8},{16,12},{20,16},{24,20},{28,24},{5,1},{9,5},{13... | collective-permute-start | bytes 184328 | tf_op jit(solution)/shard_map/ppermute | solution.py:65
  18.3 2.2 %copy-start.1 = (f32[1024,1024]{1,0:T(8,128)S(1)}, f32[1024,1024]{1,0:T(8,128)}, u32[]{:S(2)}) copy-start(f32[1024,1024]{1,0:T(8,128)} %param.6) | copy-start | bytes 12582916
  23.5 13.6 %all-to-all-start = ((f32[32,1,256]{2,1,0:T(1,128)}), f32[32,1,256]{2,1,0:T(1,128)S(1)}, u32[]{:S(2)}, u32[]{:S(2)}) async-start(f32[32,1,256]{2,1,0:T(1,128)} %reshape.152), calls=%async_computation | async-start | bytes 65536 | tf_op jit(solution)/shard_map/all_to_all | solution.py:16

commit v8 on v5

--- a/solution.py
+++ b/solution.py
@@ -16,6 +16,17 @@
     return jnp.sum(lax.all_to_all(sent, axes, 0, 0, tiled=True), axis=0)
 
 
+def halves(x):
+    high = x.astype(jnp.bfloat16)
+    return high, (x - high.astype(jnp.float32)).astype(jnp.bfloat16)
+
+
+def three_pass(spec, left, right):
+    def dot(a, b):
+        return jnp.einsum(spec, a, b, preferred_element_type=jnp.float32)
+    return dot(left[0], right[0]) + (dot(left[0], right[1]) + dot(left[1], right[0]))
+
+
 def windows_of(padded, shifts, band_cols, blocks_here):
     span = band_cols + (1 << SHIFT_BITS) - 1
     need = (blocks_here - 1) * BLK + span
@@ -29,24 +40,17 @@
 
 
 def apply_operator(extended, vector, ld_band, shifts, ridge_shift):
-    band_cols = ld_band.shape[1]
-    blocks_here = ld_band.shape[0] // BLK
+    blocks_here, _, band_cols = ld_band[0].shape
     windows = windows_of(extended, shifts, band_cols, blocks_here)
-    blocks = ld_band.reshape(blocks_here, BLK, band_cols)
-    product = jnp.einsum("btk,brk->tbr", windows, blocks, precision=lax.Precision.HIGH)
+    product = three_pass("btk,brk->tbr", halves(windows), ld_band)
     return product.reshape(vector.shape) + ridge_shift[:, None] * vector
 
 
 def spread_operator(vector, ld_band, shifts, ridge_shift, halo):
-    band_cols = ld_band.shape[1]
-    blocks_here = ld_band.shape[0] // BLK
+    blocks_here, _, band_cols = ld_band[0].shape
     traits, rows = vector.shape
     span = band_cols + (1 << SHIFT_BITS) - 1
-    blocks = ld_band.reshape(blocks_here, BLK, band_cols)
-    pieces = jnp.einsum(
-        "tbr,brk->btk", vector.reshape(traits, blocks_here, BLK), blocks,
-        precision=lax.Precision.HIGH,
-    )
+    pieces = three_pass("tbr,brk->btk", halves(vector.reshape(traits, blocks_here, BLK)), ld_band)
     wide = jnp.pad(pieces, ((0, 0), (0, 0), (0, span - band_cols)))
     for bit in range(SHIFT_BITS):
         step = 1 << bit
@@ -77,9 +81,10 @@
     shifts = offsets - jnp.arange(band_start.shape[0], dtype=jnp.int32) * BLK
 
     ridge_shift = M_GENOME / N_GWAS / heritability
-    extended = spread_operator(beta_hat, ld_band, shifts, ridge_shift, halo)
+    band_parts = halves(ld_band.reshape(-1, BLK, ld_band.shape[1]))
+    extended = spread_operator(beta_hat, band_parts, shifts, ridge_shift, halo)
     image = extended[:, halo : halo + rows_here]
-    image2 = apply_operator(extended, image, ld_band, shifts, ridge_shift)
+    image2 = apply_operator(extended, image, band_parts, shifts, ridge_shift)
 
     moments = jnp.stack(
         [

time: 67.3 us -> 68.5 us (1.018)
  local copies, waits for them, and re-layouts: 1.94 us -> 3.59 us
    unnamed x17 -> x21, local copies, waits for them, and re-layouts: 1.29 us -> 2.95 us
    eq x2, other arithmetic: 0.82 us -> 0.02 us  [spread_operator(): take = (shifts >> bit & 1)[:, None, None] == 1]
    dot_general x2 -> x6, matrix products: 5.28 us -> 5.54 us  [dot(): return jnp.einsum(spec, a, b, preferred_element_type=jnp.float32)]
where the time goes in v8:
time: 68.5 us; the launch traced here: 68.2 us
  blocking collectives  40.2 us (59%)
  matrix products  6.3 us (9%)
  starting transfers between devices  6.19 us (9%)
  other arithmetic  6.18 us (9%)
  waiting for transfers between devices  4.86 us (7%)
  local copies, waits for them, and re-layouts  3.59 us (5%)
  between operations  0.95 us (1%)
    all_to_all x1, blocking collectives, local(): complete = jnp.sum(lax.all_to_all(chunks, 'snp', 0, 0, tiled=True), axis=0)  12.1 us
    all_to_all x1, blocking collectives, all_sum(): return jnp.sum(lax.all_to_all(sent, axes, 0, 0, tiled=True), axis=0)  12.1 us
    all_to_all x1, blocking collectives, local(): every = lax.all_to_all(sent, ('ind', 'snp'), 0, 0, tiled=True)  10.5 us
    dot_general x6, matrix products, dot(): return jnp.einsum(spec, a, b, preferred_element_type=jnp.float32)  5.54 us
    all_gather x1, blocking collectives, local(): lax.all_gather(weights.astype(jnp.bfloat16), 'ind', axis=0, tiled=True)  5.4 us
    ppermute x1, starting transfers between devices, spread_operator(): from_left = lax.ppermute(own[:, rows:], 'snp', forward)  4.9 us
    ppermute x1, waiting for transfers between devices, spread_operator(): from_right = lax.ppermute(own[:, :2 * halo], 'snp', backward)  4.27 us
    unnamed x21, local copies, waits for them, and re-layouts  2.95 us
  transfers between devices with their start and end apart: 2, of which 2 were waited for; matrix products, arithmetic and copies ran while one was open for 0% of the time, Pallas kernels for 0%

profile of v8, /device:TPU:0, one launch (start us, length us, event | category | flops | bytes accessed | tf_op | source)
XLA Modules:
  0.0 68.2 jit_solution(234442718584425230)
XLA Ops:
  0.6 0.0 copy-start
  0.6 0.0 copy-start.1
  0.7 0.0 copy-start.3
  0.7 2.8 %fusion.24 = f32[8,16,1024]{2,1,0:T(8,128)S(1)} fusion(f32[8,128,1024]{2,1,0:T(8,128)} %bitcast.151, f32[16,1024]{1,0:T(8,128)} %param.5), kind=kOutput, calls=%fused_computation.77 | convolution fusion | flops 34668544 | bytes 4784128 | tf_op jit(solution)/shard_map/tbr,brk->btk/dot_general | solution.py:26
  3.4 0.9 %copy-done.1 = f32[1024,1024]{1,0:T(8,128)S(1)} copy-done((f32[1024,1024]{1,0:T(8,128)S(1)}, f32[1024,1024]{1,0:T(8,128)}, u32[]{:S(2)}) %copy-start.1) | copy-done | bytes 4194328
  4.3 0.4 fusion
  4.7 0.4 convolution_add_fusion
  5.1 0.3 copy-done.4
  5.4 0.2 slice_select_fusion.6
  5.6 0.2 fusion.4
  5.9 0.2 fusion.5
  6.1 0.2 fusion.6
  6.3 0.0 copy-start.5
  6.3 0.2 fusion.7
  6.6 0.2 fusion.8
  6.8 0.2 fusion.9
  7.1 0.1 broadcast_multiply_fusion
  7.2 0.1 fusion.10
  7.3 4.9 %collective-permute-start = (f32[16,960]{1,0:T(8,128)S(1)}, f32[16,960]{1,0:T(8,128)S(1)}, u32[]{:S(2)}, u32[]{:S(2)}) collective-permute-start(f32[16,960]{1,0:T(8,128)S(1)} %get-tuple-element.23), channel_id=1, source_target_pairs={{0,4},{4,8},{8,12},{12,16},{16,20},{20,24},{24,28},{1,5},{5,9},{9,... | collective-permute-start | bytes 184328 | tf_op jit(solution)/shard_map/ppermute | solution.py:68
  12.2 1.3 %collective-permute-start.1 = (f32[16,960]{1,0:T(8,128)S(1)}, f32[16,960]{1,0:T(8,128)S(1)}, u32[]{:S(2)}, u32[]{:S(2)}) collective-permute-start(f32[16,960]{1,0:T(8,128)S(1)} %get-tuple-element.24), channel_id=1, source_target_pairs={{4,0},{8,4},{12,8},{16,12},{20,16},{24,20},{28,24},{5,1},{9,5},{13... | collective-permute-start | bytes 184328 | tf_op jit(solution)/shard_map/ppermute | solution.py:69
  13.5 0.6 collective-permute-done
  14.1 4.3 %collective-permute-done.1 = f32[16,960]{1,0:T(8,128)S(1)} collective-permute-done((f32[16,960]{1,0:T(8,128)S(1)}, f32[16,960]{1,0:T(8,128)S(1)}, u32[]{:S(2)}, u32[]{:S(2)}) %collective-permute-start.1) | collective-permute-done | bytes 61472 | tf_op jit(solution)/shard_map/ppermute | solution.py:69
  18.5 0.2 slice_select_fusion.5
  18.7 0.2 slice_select_fusion.4
  19.0 0.2 slice_select_fusion.3
  19.2 0.2 slice_select_fusion.2
  19.4 0.0 copy-start.2
  19.4 0.2 slice_select_fusion.1
  19.7 0.2 slice_select_fusion
  19.9 0.1 fusion.23
  20.1 1.6 %copy-done.2 = f32[1024,1024]{1,0:T(8,128)S(1)} copy-done((f32[1024,1024]{1,0:T(8,128)S(1)}, f32[1024,1024]{1,0:T(8,128)}, u32[]{:S(2)}) %copy-start.2) | copy-done | bytes 4194328
  21.6 0.6 convolution_bitcast_fusion.3
  22.3 0.7 convolution_bitcast_fusion.4
  22.9 0.7 %fusion.3 = f32[8,2,8,128]{3,2,1,0:T(8,128)S(1)} fusion(f32[16,8,128]{2,0,1:T(8,128)S(1)} %convolution_bitcast_fusion.4, f32[16,8,128]{2,0,1:T(8,128)S(1)} %convolution_bitcast_fusion.3, bf16[8,16,1024]{2,1,0:T(8,128)(2,1)S(1)} %fusion.23, f32[8,16,1088]{2,1,0:T(8,128)S(1)} %slice_select_fusion, pred[8]{0:T(512)(128)(4,1)S(1)} %get-tuple-element.13, ...), kind=kOutput, calls=%fused_computation.8 | convolution fusion | flops 35160064 | bytes 5702144 | tf_op jit(solution)/shard_map/btk,brk->tbr/dot_general | solution.py:26
  23.6 0.3 multiply_reduce_fusion.1
  23.9 12.1 %all_to_all.15 = f32[8,4,16]{2,1,0:T(4,128)S(1)} all-to-all(f32[8,4,16]{2,1,0:T(4,128)S(1)} %broadcast_in_dim.144), channel_id=1, replica_groups=mesh['snp'=8,'ind'=4] {'snp'}, dimensions={0} | all-to-all | bytes 4096 | tf_op jit(solution)/shard_map/all_to_all | solution.py:16
  36.1 0.7 %fusion.37 = (bf16[16,1024]{1,0:T(8,128)(2,1)S(1)}, f32[16,1024]{1,0:T(8,128)}) fusion(f32[16,1024]{1,0:T(8,128)S(1)} %copy-done.3, f32[16]{0:T(128)S(1)} %get-tuple-element.11, f32[16,1984]{1,0:T(8,128)S(1)} %pad_add_fusion.6, f32[16]{0:T(128)S(1)} %get-tuple-element.10, f32[16]{0:T(128)S(1)} %get-tuple-element.12), kind=kLoop, calls=%fused_computation.114 | loop fusion | flops 131072 | bytes 229568 | tf_op jit(solution)/shard_map/convert_element_type | solution.py:109
  36.8 5.4 %all_gather.3 = bf16[64,1024]{1,0:T(8,128)(2,1)S(1)} all-gather(bf16[16,1024]{1,0:T(8,128)(2,1)S(1)} %get-tuple-element.8), channel_id=1, replica_groups=mesh['snp'=8,'ind'=4] {'ind'}, dimensions={0}, use_global_device_ids=true | all-gather | bytes 163840 | tf_op jit(solution)/shard_map/all_gather | solution.py:109
  42.2 0.8 %convolution_bitcast_fusion.1 = f32[8,8,8,128]{3,2,1,0:T(8,128)S(1)} fusion(bf16[64,1024]{1,0:T(8,128)(2,1)S(1)} %all_gather.3, bf16[1024,1024]{1,0:T(8,128)(2,1)S(1)} %copy-done), kind=kOutput, calls=%fused_computation.4 | convolution fusion | flops 134217728 | bytes 2490368 | tf_op jit(solution)/shard_map/dot_general | solution.py:110
  43.0 12.1 %all_to_all.16 = f32[8,64,128]{2,1,0:T(8,128)S(1)} all-to-all(f32[8,64,128]{2,1,0:T(8,128)S(1)} %bitcast.157), channel_id=1, replica_groups=mesh['snp'=8,'ind'=4] {'snp'}, dimensions={0} | all-to-all | bytes 524288 | tf_op jit(solution)/shard_map/all_to_all | solution.py:116
  55.1 0.1 fusion.36
  55.2 0.2 multiply_reduce_fusion.3
  55.5 0.1 reshape.119
  55.6 10.5 %all_to_all.17 = f32[32,1,128]{2,1,0:T(1,128)S(1)} all-to-all(f32[32,1,128]{2,1,0:T(1,128)S(1)} %reshape.119), channel_id=1, replica_groups=mesh['snp'=8,'ind'=4] {'ind','snp'}, dimensions={0} | all-to-all | bytes 32768 | tf_op jit(solution)/shard_map/all_to_all | solution.py:123
  66.1 0.5 broadcast.179
  66.6 0.7 %reduce.3 = f32[32,128]{1,0:T(8,128)S(1)} reduce(f32[32,1,128]{2,1,0:T(1,128)S(1)} %all_to_all.17, f32[]{:T(128)} %broadcast.179), dimensions={1}, to_apply=%all_to_all.11.reduce_sub_computation | reduce | bytes 32772 | tf_op jit(solution)/shard_map/all_to_all | solution.py:123
  67.3 0.1 reshape.120
  67.5 0.7 %subtract_multiply_fusion = f32[64,128]{1,0:T(8,128)} fusion(f32[64,128]{1,0:T(8,128)S(1)} %get-tuple-element.3, f32[64]{0:T(128)S(1)} %add_rsqrt_fusion, f32[64]{0:T(128)S(1)} %broadcast_multiply_fusion.2), kind=kLoop, calls=%fused_computation.78 | loop fusion | flops 16384 | bytes 66048 | tf_op jit(solution)/shard_map/mul | solution.py:129
  (33 shorter events, 0.4 us)
Async XLA Ops:
  0.6 41.6 %copy-start = (bf16[1024,1024]{1,0:T(8,128)(2,1)S(1)}, bf16[1024,1024]{1,0:T(8,128)(2,1)}, u32[]{:S(2)}) copy-start(bf16[1024,1024]{1,0:T(8,128)(2,1)} %param.9) | copy-start | bytes 6291460
  0.6 3.6 %copy-start.1 = (f32[1024,1024]{1,0:T(8,128)S(1)}, f32[1024,1024]{1,0:T(8,128)}, u32[]{:S(2)}) copy-start(f32[1024,1024]{1,0:T(8,128)} %param.6) | copy-start | bytes 12582916
  0.7 3.6 %copy-start.3 = (f32[16,1024]{1,0:T(8,128)S(1)}, f32[16,1024]{1,0:T(8,128)}, u32[]{:S(2)}) copy-start(f32[16,1024]{1,0:T(8,128)} %param.5) | copy-start | bytes 196612
  4.7 0.7 copy-start.4
  6.3 0.8 %copy-start.5 = (f32[16]{0:T(128)S(1)}, f32[16]{0:T(128)}, u32[]{:S(2)}) copy-start(f32[16]{0:T(128)} %param.8) | copy-start | bytes 196
  7.3 6.8 %collective-permute-start = (f32[16,960]{1,0:T(8,128)S(1)}, f32[16,960]{1,0:T(8,128)S(1)}, u32[]{:S(2)}, u32[]{:S(2)}) collective-permute-start(f32[16,960]{1,0:T(8,128)S(1)} %get-tuple-element.23), channel_id=1, source_target_pairs={{0,4},{4,8},{8,12},{12,16},{16,20},{20,24},{24,28},{1,5},{5,9},{9,... | collective-permute-start | bytes 184328 | tf_op jit(solution)/shard_map/ppermute | solution.py:68
  12.2 6.2 %collective-permute-start.1 = (f32[16,960]{1,0:T(8,128)S(1)}, f32[16,960]{1,0:T(8,128)S(1)}, u32[]{:S(2)}, u32[]{:S(2)}) collective-permute-start(f32[16,960]{1,0:T(8,128)S(1)} %get-tuple-element.24), channel_id=1, source_target_pairs={{4,0},{8,4},{12,8},{16,12},{20,16},{24,20},{28,24},{5,1},{9,5},{13... | collective-permute-start | bytes 184328 | tf_op jit(solution)/shard_map/ppermute | solution.py:69
  19.4 2.2 %copy-start.2 = (f32[1024,1024]{1,0:T(8,128)S(1)}, f32[1024,1024]{1,0:T(8,128)}, u32[]{:S(2)}) copy-start(f32[1024,1024]{1,0:T(8,128)} %param.6) | copy-start | bytes 12582916

commit v9 on v5

--- a/solution.py
+++ b/solution.py
@@ -8,7 +8,8 @@
 M_GENOME = 1100000
 N_GWAS = 1000000
 REACH = 416
-SHIFT_BITS = 7
+COARSE = 8
+FINE = 8
 
 
 def all_sum(x, axes, count):
@@ -16,16 +17,22 @@
     return jnp.sum(lax.all_to_all(sent, axes, 0, 0, tiled=True), axis=0)
 
 
+def pick(source, choice, starts, length):
+    out = source[:, :, starts[0] : starts[0] + length]
+    for j in range(1, len(starts)):
+        out = jnp.where(choice == j, source[:, :, starts[j] : starts[j] + length], out)
+    return out
+
+
 def windows_of(padded, shifts, band_cols, blocks_here):
-    span = band_cols + (1 << SHIFT_BITS) - 1
+    span = band_cols + COARSE * (FINE + 1) - 1
     need = (blocks_here - 1) * BLK + span
     padded = jnp.pad(padded, ((0, 0), (0, max(0, need - padded.shape[1]))))
     wide = jnp.stack([padded[:, b * BLK : b * BLK + span] for b in range(blocks_here)])
-    for bit in range(SHIFT_BITS):
-        step = 1 << bit
-        take = ((shifts >> bit) & 1)[:, None, None] == 1
-        wide = jnp.where(take, wide[:, :, step:], wide[:, :, :-step])
-    return wide[:, :, :band_cols]
+    coarse = (shifts // COARSE)[:, None, None]
+    fine = (shifts % COARSE)[:, None, None]
+    wide = pick(wide, coarse, [COARSE * j for j in range(FINE + 1)], band_cols + COARSE - 1)
+    return pick(wide, fine, list(range(COARSE)), band_cols)
 
 
 def apply_operator(extended, vector, ld_band, shifts, ridge_shift):
@@ -41,18 +48,18 @@
     band_cols = ld_band.shape[1]
     blocks_here = ld_band.shape[0] // BLK
     traits, rows = vector.shape
-    span = band_cols + (1 << SHIFT_BITS) - 1
+    span = band_cols + COARSE * (FINE + 1) - 1
     blocks = ld_band.reshape(blocks_here, BLK, band_cols)
     pieces = jnp.einsum(
         "tbr,brk->btk", vector.reshape(traits, blocks_here, BLK), blocks,
         precision=lax.Precision.HIGH,
     )
-    wide = jnp.pad(pieces, ((0, 0), (0, 0), (0, span - band_cols)))
-    for bit in range(SHIFT_BITS):
-        step = 1 << bit
-        take = ((shifts >> bit) & 1)[:, None, None] == 1
-        moved = jnp.pad(wide, ((0, 0), (0, 0), (step, 0)))[:, :, :span]
-        wide = jnp.where(take, moved, wide)
+    lead = COARSE * FINE + COARSE - 1
+    source = jnp.pad(pieces, ((0, 0), (0, 0), (lead, lead)))
+    coarse = (shifts // COARSE)[:, None, None]
+    fine = (shifts % COARSE)[:, None, None]
+    moved = pick(source, coarse, [COARSE * (FINE - j) for j in range(FINE + 1)], span + COARSE - 1)
+    wide = pick(moved, fine, [COARSE - 1 - j for j in range(COARSE)], span)
     width = max((blocks_here - 1) * BLK + span, rows + 2 * halo)
     own = sum(
         jnp.pad(wide[b], ((0, 0), (b * BLK, width - b * BLK - span))) for b in range(blocks_here)

time: 67.3 us -> 68.6 us (1.019)
  other arithmetic: 6.82 us -> 8.69 us
  local copies, waits for them, and re-layouts: 1.94 us -> 0.87 us
    select_n x13 -> x3, other arithmetic: 2.94 us -> 4.14 us  [pick(): jnp.where(choice == j, source[:, :, starts[j]:starts[j] + length], out)]
    unnamed x17, local copies, waits for them, and re-layouts: 1.29 us -> 0.26 us
    eq x2 -> x3, other arithmetic: 0.82 us -> 1.5 us  [pick(): choice == j]
where the time goes in v9:
time: 68.6 us; the launch traced here: 68.3 us
  blocking collectives  40.2 us (59%)
  other arithmetic  8.69 us (13%)
  starting transfers between devices  6.46 us (9%)
  matrix products  6.38 us (9%)
  waiting for transfers between devices  4.86 us (7%)
  between operations  0.89 us (1%)
  local copies, waits for them, and re-layouts  0.87 us (1%)
    all_to_all x1, blocking collectives, local(): complete = jnp.sum(lax.all_to_all(chunks, 'snp', 0, 0, tiled=True), axis=0)  12.1 us
    all_to_all x1, blocking collectives, all_sum(): return jnp.sum(lax.all_to_all(sent, axes, 0, 0, tiled=True), axis=0)  12.1 us
    all_to_all x1, blocking collectives, local(): every = lax.all_to_all(sent, ('ind', 'snp'), 0, 0, tiled=True)  10.5 us
    all_gather x1, blocking collectives, local(): lax.all_gather(weights.astype(jnp.bfloat16), 'ind', axis=0, tiled=True)  5.4 us
    ppermute x1, starting transfers between devices, spread_operator(): from_left = lax.ppermute(own[:, rows:], 'snp', forward)  5.17 us
    ppermute x1, waiting for transfers between devices, spread_operator(): from_right = lax.ppermute(own[:, :2 * halo], 'snp', backward)  4.27 us
    select_n x3, other arithmetic, pick(): jnp.where(choice == j, source[:, :, starts[j]:starts[j] + length], out)  4.14 us
    dot_general x1, matrix products, spread_operator(): jnp.einsum('tbr,brk->btk', vector.reshape(traits, blocks_here, BLK), bloc...  3.38 us
  transfers between devices with their start and end apart: 2, of which 2 were waited for; matrix products, arithmetic and copies ran while one was open for 0% of the time, Pallas kernels for 0%

profile of v9, /device:TPU:0, one launch (start us, length us, event | category | flops | bytes accessed | tf_op | source)
XLA Modules:
  0.0 68.3 jit_solution(625358880545183375)
XLA Ops:
  0.6 0.0 copy-start
  0.6 0.8 %broadcast_compare_fusion.14 = (pred[8]{0:T(512)(128)(4,1)S(1)}, s32[8]{0:T(128)S(1)}, s32[8]{0:T(128)S(1)}) fusion(s32[8]{0:T(128)} %param.7, s32[]{:T(128)S(6)} %mul.147), kind=kLoop, calls=%fused_computation.140 | loop fusion | flops 128 | bytes 108 | tf_op jit(solution)/shard_map/eq | solution.py:23
  1.5 0.7 broadcast_compare_fusion.6
  2.2 3.4 %fusion.54 = f32[8,16,1024]{2,1,0:T(8,128)S(1)} fusion(f32[8,128,1024]{2,1,0:T(8,128)} %bitcast.122, f32[16,1024]{1,0:T(8,128)} %param.5), kind=kOutput, calls=%fused_computation.92 | convolution fusion | flops 100663296 | bytes 4784128 | tf_op jit(solution)/shard_map/tbr,brk->btk/dot_general | solution.py:53
  5.5 0.0 copy-start.3
  5.5 0.0 copy-start.2
  5.6 1.5 %fusion = f32[8,16,1102]{2,1,0:T(8,128)S(1)} fusion(f32[8,16,1024]{2,1,0:T(8,128)S(1)} %fusion.54, pred[8]{0:T(512)(128)(4,1)S(1)} %get-tuple-element.43, pred[8]{0:T(512)(128)(4,1)S(1)} %get-tuple-element.38, pred[8]{0:T(512)(128)(4,1)S(1)} %get-tuple-element.39, pred[8]{0:T(512)(128)(4,1)S(1)} %get-tuple-element.40, pred[8]{0:T(512)(128)(4,1)S(1)} %get-tuple-element.41, ...), kind=kLoop, calls=%fused_computation.11 | loop fusion | flops 1128448 | bytes 1088576 | tf_op jit(solution)/shard_map/jit(_where)/select_n | solution.py:23
  7.1 1.2 %fusion.20 = f32[8,16,1095]{2,1,0:T(8,128)S(1)} fusion(f32[8,16,1102]{2,1,0:T(8,128)S(1)} %fusion, pred[8]{0:T(512)(128)(4,1)S(1)} %get-tuple-element.36, pred[8]{0:T(512)(128)(4,1)S(1)} %get-tuple-element.32, pred[8]{0:T(512)(128)(4,1)S(1)} %get-tuple-element.33, pred[8]{0:T(512)(128)(4,1)S(1)} %get-tuple-element.34, pred[8]{0:T(512)(128)(4,1)S(1)} %get-tuple-element.35, ...), kind=kLoop, calls=%fused_computation.33 | loop fusion | flops 981120 | bytes 5045816 | tf_op jit(solution)/shard_map/jit(_where)/select_n | solution.py:23
  8.4 0.0 copy-done.3
  8.4 0.0 copy-done.2
  8.4 0.1 broadcast_multiply_fusion
  8.5 0.0 copy-start.1
  8.5 0.1 fusion.42
  8.6 5.2 %collective-permute-start = (f32[16,960]{1,0:T(8,128)S(1)}, f32[16,960]{1,0:T(8,128)S(1)}, u32[]{:S(2)}, u32[]{:S(2)}) collective-permute-start(f32[16,960]{1,0:T(8,128)S(1)} %get-tuple-element.26), channel_id=1, source_target_pairs={{0,4},{4,8},{8,12},{12,16},{16,20},{20,24},{24,28},{1,5},{5,9},{9,... | collective-permute-start | bytes 184328 | tf_op jit(solution)/shard_map/ppermute | solution.py:71
  13.8 1.3 %collective-permute-start.1 = (f32[16,960]{1,0:T(8,128)S(1)}, f32[16,960]{1,0:T(8,128)S(1)}, u32[]{:S(2)}, u32[]{:S(2)}) collective-permute-start(f32[16,960]{1,0:T(8,128)S(1)} %get-tuple-element.27), channel_id=1, source_target_pairs={{4,0},{8,4},{12,8},{16,12},{20,16},{24,20},{28,24},{5,1},{9,5},{13... | collective-permute-start | bytes 184328 | tf_op jit(solution)/shard_map/ppermute | solution.py:72
  15.1 0.6 collective-permute-done
  15.6 4.3 %collective-permute-done.1 = f32[16,960]{1,0:T(8,128)S(1)} collective-permute-done((f32[16,960]{1,0:T(8,128)S(1)}, f32[16,960]{1,0:T(8,128)S(1)}, u32[]{:S(2)}, u32[]{:S(2)}) %collective-permute-start.1) | collective-permute-done | bytes 61472 | tf_op jit(solution)/shard_map/ppermute | solution.py:72
  20.1 1.4 %fusion.14 = f32[8,16,1031]{2,1,0:T(8,128)S(1)} fusion(f32[8,16,1095]{2,1,0:T(8,128)S(1)} %fusion.44, pred[8]{0:T(512)(128)(4,1)S(1)} %get-tuple-element.43, pred[8]{0:T(512)(128)(4,1)S(1)} %get-tuple-element.38, pred[8]{0:T(512)(128)(4,1)S(1)} %get-tuple-element.39, pred[8]{0:T(512)(128)(4,1)S(1)} %get-tuple-element.40, ...), kind=kLoop, calls=%fused_computation.26 | loop fusion | flops 1055744 | bytes 5278784 | tf_op jit(solution)/shard_map/jit(_where)/select_n | solution.py:23
  21.5 0.0 copy-done.1
  21.5 2.2 %convolution_bitcast_fusion.1 = f32[8,2,8,128]{3,2,1,0:T(8,128)S(1)} fusion(f32[8,128,1024]{2,1,0:T(8,128)S(1)} %bitcast.123, f32[8,16,1031]{2,1,0:T(8,128)S(1)} %fusion.14, pred[8]{0:T(512)(128)(4,1)S(1)} %get-tuple-element.36, pred[8]{0:T(512)(128)(4,1)S(1)} %get-tuple-element.32, pred[8]{0:T(512)(128)(4,1)S(1)} %get-tuple-element.33, ...), kind=kOutput, calls=%fused_computation.1 | convolution fusion | flops 101580800 | bytes 8457728 | tf_op jit(solution)/shard_map/btk,brk->tbr/dot_general | solution.py:43
  23.7 0.2 multiply_reduce_fusion.1
  24.0 12.1 %all_to_all.15 = f32[8,4,16]{2,1,0:T(4,128)S(1)} all-to-all(f32[8,4,16]{2,1,0:T(4,128)S(1)} %broadcast_in_dim.218), channel_id=1, replica_groups=mesh['snp'=8,'ind'=4] {'snp'}, dimensions={0} | all-to-all | bytes 4096 | tf_op jit(solution)/shard_map/all_to_all | solution.py:17
  36.1 0.7 %fusion.62 = (bf16[16,1024]{1,0:T(8,128)(2,1)S(1)}, f32[16,1024]{1,0:T(8,128)}) fusion(f32[16,1024]{1,0:T(8,128)S(1)} %copy-done.2, f32[16]{0:T(128)S(1)} %get-tuple-element.11, f32[16,1984]{1,0:T(8,128)S(1)} %pad_add_fusion.6, f32[16]{0:T(128)S(1)} %get-tuple-element.10, f32[16]{0:T(128)S(1)} %get-tuple-element.12), kind=kLoop, calls=%fused_computation.142 | loop fusion | flops 131072 | bytes 229568 | tf_op jit(solution)/shard_map/convert_element_type | solution.py:111
  36.9 5.4 %all_gather.3 = bf16[64,1024]{1,0:T(8,128)(2,1)S(1)} all-gather(bf16[16,1024]{1,0:T(8,128)(2,1)S(1)} %get-tuple-element.8), channel_id=1, replica_groups=mesh['snp'=8,'ind'=4] {'ind'}, dimensions={0}, use_global_device_ids=true | all-gather | bytes 163840 | tf_op jit(solution)/shard_map/all_gather | solution.py:111
  42.3 0.0 copy-done
  42.3 0.8 %convolution_bitcast_fusion = f32[8,8,8,128]{3,2,1,0:T(8,128)S(1)} fusion(bf16[64,1024]{1,0:T(8,128)(2,1)S(1)} %all_gather.3, bf16[1024,1024]{1,0:T(8,128)(2,1)S(1)} %copy-done), kind=kOutput, calls=%fused_computation | convolution fusion | flops 134217728 | bytes 2490368 | tf_op jit(solution)/shard_map/dot_general | solution.py:112
  43.1 12.1 %all_to_all.16 = f32[8,64,128]{2,1,0:T(8,128)S(1)} all-to-all(f32[8,64,128]{2,1,0:T(8,128)S(1)} %bitcast.124), channel_id=1, replica_groups=mesh['snp'=8,'ind'=4] {'snp'}, dimensions={0} | all-to-all | bytes 524288 | tf_op jit(solution)/shard_map/all_to_all | solution.py:118
  55.2 0.1 fusion.61
  55.3 0.2 multiply_reduce_fusion.3
  55.5 0.1 reshape.136
  55.6 10.5 %all_to_all.17 = f32[32,1,128]{2,1,0:T(1,128)S(1)} all-to-all(f32[32,1,128]{2,1,0:T(1,128)S(1)} %reshape.136), channel_id=1, replica_groups=mesh['snp'=8,'ind'=4] {'ind','snp'}, dimensions={0} | all-to-all | bytes 32768 | tf_op jit(solution)/shard_map/all_to_all | solution.py:125
  66.2 0.5 broadcast.212
  66.7 0.7 reduce.3
  67.4 0.1 reshape.137
  67.6 0.7 %subtract_multiply_fusion = f32[64,128]{1,0:T(8,128)} fusion(f32[64,128]{1,0:T(8,128)S(1)} %get-tuple-element.3, f32[64]{0:T(128)S(1)} %add_rsqrt_fusion, f32[64]{0:T(128)S(1)} %broadcast_multiply_fusion.2), kind=kLoop, calls=%fused_computation.99 | loop fusion | flops 16384 | bytes 66048 | tf_op jit(solution)/shard_map/mul | solution.py:131
  (27 shorter events, 0.4 us)
Async XLA Ops:
  0.6 41.7 %copy-start = (bf16[1024,1024]{1,0:T(8,128)(2,1)S(1)}, bf16[1024,1024]{1,0:T(8,128)(2,1)}, u32[]{:S(2)}) copy-start(bf16[1024,1024]{1,0:T(8,128)(2,1)} %param.9) | copy-start | bytes 6291460
  5.5 2.8 %copy-start.3 = (f32[16]{0:T(128)S(1)}, f32[16]{0:T(128)}, u32[]{:S(2)}) copy-start(f32[16]{0:T(128)} %param.8) | copy-start | bytes 196
  5.5 2.8 %copy-start.2 = (f32[16,1024]{1,0:T(8,128)S(1)}, f32[16,1024]{1,0:T(8,128)}, u32[]{:S(2)}) copy-start(f32[16,1024]{1,0:T(8,128)} %param.5) | copy-start | bytes 196612
  8.5 13.0 %copy-start.1 = (f32[1024,1024]{1,0:T(8,128)S(1)}, f32[1024,1024]{1,0:T(8,128)}, u32[]{:S(2)}) copy-start(f32[1024,1024]{1,0:T(8,128)} %param.6) | copy-start | bytes 12582916
  8.6 7.1 %collective-permute-start = (f32[16,960]{1,0:T(8,128)S(1)}, f32[16,960]{1,0:T(8,128)S(1)}, u32[]{:S(2)}, u32[]{:S(2)}) collective-permute-start(f32[16,960]{1,0:T(8,128)S(1)} %get-tuple-element.26), channel_id=1, source_target_pairs={{0,4},{4,8},{8,12},{12,16},{16,20},{20,24},{24,28},{1,5},{5,9},{9,... | collective-permute-start | bytes 184328 | tf_op jit(solution)/shard_map/ppermute | solution.py:71
  13.8 6.2 %collective-permute-start.1 = (f32[16,960]{1,0:T(8,128)S(1)}, f32[16,960]{1,0:T(8,128)S(1)}, u32[]{:S(2)}, u32[]{:S(2)}) collective-permute-start(f32[16,960]{1,0:T(8,128)S(1)} %get-tuple-element.27), channel_id=1, source_target_pairs={{4,0},{8,4},{12,8},{16,12},{20,16},{24,20},{28,24},{5,1},{9,5},{13... | collective-permute-start | bytes 184328 | tf_op jit(solution)/shard_map/ppermute | solution.py:72

commit v10 on v5

--- a/solution.py
+++ b/solution.py
@@ -44,18 +44,18 @@
     span = band_cols + (1 << SHIFT_BITS) - 1
     blocks = ld_band.reshape(blocks_here, BLK, band_cols)
     pieces = jnp.einsum(
-        "tbr,brk->btk", vector.reshape(traits, blocks_here, BLK), blocks,
+        "tbr,brk->tbk", vector.reshape(traits, blocks_here, BLK), blocks,
         precision=lax.Precision.HIGH,
     )
     wide = jnp.pad(pieces, ((0, 0), (0, 0), (0, span - band_cols)))
     for bit in range(SHIFT_BITS):
         step = 1 << bit
-        take = ((shifts >> bit) & 1)[:, None, None] == 1
+        take = ((shifts >> bit) & 1)[None, :, None] == 1
         moved = jnp.pad(wide, ((0, 0), (0, 0), (step, 0)))[:, :, :span]
         wide = jnp.where(take, moved, wide)
     width = max((blocks_here - 1) * BLK + span, rows + 2 * halo)
     own = sum(
-        jnp.pad(wide[b], ((0, 0), (b * BLK, width - b * BLK - span))) for b in range(blocks_here)
+        jnp.pad(wide[:, b], ((0, 0), (b * BLK, width - b * BLK - span))) for b in range(blocks_here)
     )[:, : rows + 2 * halo]
     own = own + jnp.pad(ridge_shift[:, None] * vector, ((0, 0), (halo, halo)))
     count = lax.axis_size("snp")

time: 67.3 us -> 67.1 us (level)
  no operation moved by 1% of the time
where the time goes in v10:
time: 67.1 us; the launch traced here: 66.8 us
  blocking collectives  40.2 us (60%)
  other arithmetic  6.82 us (10%)
  starting transfers between devices  6.19 us (9%)
  matrix products  5.89 us (9%)
  waiting for transfers between devices  4.86 us (7%)
  local copies, waits for them, and re-layouts  1.94 us (3%)
  between operations  0.94 us (1%)
    all_to_all x1, blocking collectives, local(): complete = jnp.sum(lax.all_to_all(chunks, 'snp', 0, 0, tiled=True), axis=0)  12.1 us
    all_to_all x1, blocking collectives, all_sum(): return jnp.sum(lax.all_to_all(sent, axes, 0, 0, tiled=True), axis=0)  12.1 us
    all_to_all x1, blocking collectives, local(): every = lax.all_to_all(sent, ('ind', 'snp'), 0, 0, tiled=True)  10.5 us
    all_gather x1, blocking collectives, local(): lax.all_gather(weights.astype(jnp.bfloat16), 'ind', axis=0, tiled=True)  5.4 us
    ppermute x1, starting transfers between devices, spread_operator(): from_left = lax.ppermute(own[:, rows:], 'snp', forward)  4.9 us
    ppermute x1, waiting for transfers between devices, spread_operator(): from_right = lax.ppermute(own[:, :2 * halo], 'snp', backward)  4.27 us
    dot_general x1, matrix products, spread_operator(): jnp.einsum('tbr,brk->tbk', vector.reshape(traits, blocks_here, BLK), bloc...  3.23 us
    dot_general x1, matrix products, apply_operator(): jnp.einsum('btk,brk->tbr', windows, blocks, precision=lax.Precision.HIGH)  1.9 us
  transfers between devices with their start and end apart: 2, of which 2 were waited for; matrix products, arithmetic and copies ran while one was open for 0% of the time, Pallas kernels for 0%

profile of v10, /device:TPU:0, one launch (start us, length us, event | category | flops | bytes accessed | tf_op | source)
XLA Modules:
  0.0 66.8 jit_solution(2139049888151488527)
XLA Ops:
  0.6 0.0 copy-start
  0.6 0.8 %and_compare_fusion.6 = (pred[8]{0:T(512)(128)(4,1)S(1)}, s32[8]{0:T(128)S(1)}) fusion(s32[8]{0:T(128)} %param.7, s32[]{:T(128)S(6)} %mul.147), kind=kLoop, calls=%fused_computation.92 | loop fusion | flops 56 | bytes 76 | tf_op jit(solution)/shard_map/eq | solution.py:53
  1.5 3.2 %convolution_bitcast_fusion = f32[16,8,1024]{2,0,1:T(8,128)S(1)} fusion(f32[8,128,1024]{2,1,0:T(8,128)} %bitcast.124, f32[16,1024]{1,0:T(8,128)} %param.5), kind=kOutput, calls=%fused_computation | convolution fusion | flops 100663296 | bytes 4784128 | tf_op jit(solution)/shard_map/tbr,brk->tbk/dot_general | solution.py:46
  4.8 0.2 slice_select_fusion.6
  5.0 0.0 copy-start.3
  5.0 0.0 copy-start.2
  5.0 0.2 fusion
  5.2 0.2 fusion.1
  5.5 0.2 fusion.2
  5.7 0.2 fusion.3
  5.9 0.2 fusion.4
  6.2 0.2 fusion.5
  6.4 0.0 copy-done.3
  6.5 0.0 copy-done.2
  6.5 0.1 broadcast_multiply_fusion
  6.6 0.1 fusion.8
  6.7 4.9 %collective-permute-start = (f32[16,960]{1,0:T(8,128)S(1)}, f32[16,960]{1,0:T(8,128)S(1)}, u32[]{:S(2)}, u32[]{:S(2)}) collective-permute-start(f32[16,960]{1,0:T(8,128)S(1)} %get-tuple-element.23), channel_id=1, source_target_pairs={{0,4},{4,8},{8,12},{12,16},{16,20},{20,24},{24,28},{1,5},{5,9},{9,... | collective-permute-start | bytes 184328 | tf_op jit(solution)/shard_map/ppermute | solution.py:64
  11.6 1.3 %collective-permute-start.1 = (f32[16,960]{1,0:T(8,128)S(1)}, f32[16,960]{1,0:T(8,128)S(1)}, u32[]{:S(2)}, u32[]{:S(2)}) collective-permute-start(f32[16,960]{1,0:T(8,128)S(1)} %get-tuple-element.24), channel_id=1, source_target_pairs={{4,0},{8,4},{12,8},{16,12},{20,16},{24,20},{28,24},{5,1},{9,5},{13... | collective-permute-start | bytes 184328 | tf_op jit(solution)/shard_map/ppermute | solution.py:65
  12.9 0.6 collective-permute-done
  13.5 4.3 %collective-permute-done.1 = f32[16,960]{1,0:T(8,128)S(1)} collective-permute-done((f32[16,960]{1,0:T(8,128)S(1)}, f32[16,960]{1,0:T(8,128)S(1)}, u32[]{:S(2)}, u32[]{:S(2)}) %collective-permute-start.1) | collective-permute-done | bytes 61472 | tf_op jit(solution)/shard_map/ppermute | solution.py:65
  17.9 0.2 slice_select_fusion.5
  18.1 0.0 copy-start.1
  18.1 0.2 slice_select_fusion.4
  18.4 0.2 slice_select_fusion.3
  18.6 0.2 slice_select_fusion.2
  18.8 0.2 slice_select_fusion.1
  19.1 0.2 slice_select_fusion
  19.3 1.0 %copy-done.1 = f32[1024,1024]{1,0:T(8,128)S(1)} copy-done((f32[1024,1024]{1,0:T(8,128)S(1)}, f32[1024,1024]{1,0:T(8,128)}, u32[]{:S(2)}) %copy-start.1) | copy-done | bytes 4194328
  20.3 1.9 %convolution_bitcast_fusion.2 = f32[8,2,8,128]{3,2,1,0:T(8,128)S(1)} fusion(f32[8,128,1024]{2,1,0:T(8,128)S(1)} %bitcast.125, f32[8,16,1088]{2,1,0:T(8,128)S(1)} %slice_select_fusion, pred[8]{0:T(512)(128)(4,1)S(1)} %get-tuple-element.13), kind=kOutput, calls=%fused_computation.2 | convolution fusion | flops 100794368 | bytes 5308928 | tf_op jit(solution)/shard_map/btk,brk->tbr/dot_general | solution.py:36
  22.2 0.2 multiply_reduce_fusion.1
  22.5 12.1 %all_to_all.15 = f32[8,4,16]{2,1,0:T(4,128)S(1)} all-to-all(f32[8,4,16]{2,1,0:T(4,128)S(1)} %broadcast_in_dim.144), channel_id=1, replica_groups=mesh['snp'=8,'ind'=4] {'snp'}, dimensions={0} | all-to-all | bytes 4096 | tf_op jit(solution)/shard_map/all_to_all | solution.py:16
  34.6 0.7 %fusion.27 = (bf16[16,1024]{1,0:T(8,128)(2,1)S(1)}, f32[16,1024]{1,0:T(8,128)}) fusion(f32[16,1024]{1,0:T(8,128)S(1)} %copy-done.2, f32[16]{0:T(128)S(1)} %get-tuple-element.11, f32[16,1984]{1,0:T(8,128)S(1)} %pad_add_fusion.6, f32[16]{0:T(128)S(1)} %get-tuple-element.10, f32[16]{0:T(128)S(1)} %get-tuple-element.12), kind=kLoop, calls=%fused_computation.98 | loop fusion | flops 131072 | bytes 229568 | tf_op jit(solution)/shard_map/convert_element_type | solution.py:104
  35.4 5.4 %all_gather.3 = bf16[64,1024]{1,0:T(8,128)(2,1)S(1)} all-gather(bf16[16,1024]{1,0:T(8,128)(2,1)S(1)} %get-tuple-element.8), channel_id=1, replica_groups=mesh['snp'=8,'ind'=4] {'ind'}, dimensions={0}, use_global_device_ids=true | all-gather | bytes 163840 | tf_op jit(solution)/shard_map/all_gather | solution.py:104
  40.8 0.0 copy-done
  40.8 0.8 %convolution_bitcast_fusion.1 = f32[8,8,8,128]{3,2,1,0:T(8,128)S(1)} fusion(bf16[64,1024]{1,0:T(8,128)(2,1)S(1)} %all_gather.3, bf16[1024,1024]{1,0:T(8,128)(2,1)S(1)} %copy-done), kind=kOutput, calls=%fused_computation.1 | convolution fusion | flops 134217728 | bytes 2490368 | tf_op jit(solution)/shard_map/dot_general | solution.py:105
  41.5 12.1 %all_to_all.16 = f32[8,64,128]{2,1,0:T(8,128)S(1)} all-to-all(f32[8,64,128]{2,1,0:T(8,128)S(1)} %bitcast.126), channel_id=1, replica_groups=mesh['snp'=8,'ind'=4] {'snp'}, dimensions={0} | all-to-all | bytes 524288 | tf_op jit(solution)/shard_map/all_to_all | solution.py:111
  53.7 0.1 fusion.26
  53.8 0.2 multiply_reduce_fusion.3
  54.0 0.1 reshape.134
  54.1 10.5 %all_to_all.17 = f32[32,1,128]{2,1,0:T(1,128)S(1)} all-to-all(f32[32,1,128]{2,1,0:T(1,128)S(1)} %reshape.134), channel_id=1, replica_groups=mesh['snp'=8,'ind'=4] {'ind','snp'}, dimensions={0} | all-to-all | bytes 32768 | tf_op jit(solution)/shard_map/all_to_all | solution.py:118
  64.7 0.5 broadcast.194
  65.2 0.7 %reduce.3 = f32[32,128]{1,0:T(8,128)S(1)} reduce(f32[32,1,128]{2,1,0:T(1,128)S(1)} %all_to_all.17, f32[]{:T(128)} %broadcast.194), dimensions={1}, to_apply=%all_to_all.11.reduce_sub_computation | reduce | bytes 32772 | tf_op jit(solution)/shard_map/all_to_all | solution.py:118
  65.9 0.1 reshape.135
  66.1 0.7 %subtract_multiply_fusion = f32[64,128]{1,0:T(8,128)} fusion(f32[64,128]{1,0:T(8,128)S(1)} %get-tuple-element.3, f32[64]{0:T(128)S(1)} %add_rsqrt_fusion, f32[64]{0:T(128)S(1)} %broadcast_multiply_fusion.2), kind=kLoop, calls=%fused_computation.68 | loop fusion | flops 16384 | bytes 66048 | tf_op jit(solution)/shard_map/mul | solution.py:124
  (28 shorter events, 0.4 us)
Async XLA Ops:
  0.6 40.1 %copy-start = (bf16[1024,1024]{1,0:T(8,128)(2,1)S(1)}, bf16[1024,1024]{1,0:T(8,128)(2,1)}, u32[]{:S(2)}) copy-start(bf16[1024,1024]{1,0:T(8,128)(2,1)} %param.9) | copy-start | bytes 6291460
  5.0 1.5 %copy-start.3 = (f32[16]{0:T(128)S(1)}, f32[16]{0:T(128)}, u32[]{:S(2)}) copy-start(f32[16]{0:T(128)} %param.8) | copy-start | bytes 196
  5.0 1.5 %copy-start.2 = (f32[16,1024]{1,0:T(8,128)S(1)}, f32[16,1024]{1,0:T(8,128)}, u32[]{:S(2)}) copy-start(f32[16,1024]{1,0:T(8,128)} %param.5) | copy-start | bytes 196612
  6.7 6.8 %collective-permute-start = (f32[16,960]{1,0:T(8,128)S(1)}, f32[16,960]{1,0:T(8,128)S(1)}, u32[]{:S(2)}, u32[]{:S(2)}) collective-permute-start(f32[16,960]{1,0:T(8,128)S(1)} %get-tuple-element.23), channel_id=1, source_target_pairs={{0,4},{4,8},{8,12},{12,16},{16,20},{20,24},{24,28},{1,5},{5,9},{9,... | collective-permute-start | bytes 184328 | tf_op jit(solution)/shard_map/ppermute | solution.py:64
  11.6 6.2 %collective-permute-start.1 = (f32[16,960]{1,0:T(8,128)S(1)}, f32[16,960]{1,0:T(8,128)S(1)}, u32[]{:S(2)}, u32[]{:S(2)}) collective-permute-start(f32[16,960]{1,0:T(8,128)S(1)} %get-tuple-element.24), channel_id=1, source_target_pairs={{4,0},{8,4},{12,8},{16,12},{20,16},{24,20},{28,24},{5,1},{9,5},{13... | collective-permute-start | bytes 184328 | tf_op jit(solution)/shard_map/ppermute | solution.py:65
  18.1 2.2 %copy-start.1 = (f32[1024,1024]{1,0:T(8,128)S(1)}, f32[1024,1024]{1,0:T(8,128)}, u32[]{:S(2)}) copy-start(f32[1024,1024]{1,0:T(8,128)} %param.6) | copy-start | bytes 12582916

commit v11 on v6

--- a/solution.py
+++ b/solution.py
@@ -108,6 +108,7 @@
     weights = lax.dynamic_slice_in_dim(weights_all, me_ind * traits_here, traits_here, 0)
 
     rounded = weights_all.astype(jnp.bfloat16)
+    weights, rounded = lax.optimization_barrier((weights, rounded))
     partial = lax.dot_general(
         rounded, genotypes, (((1,), (1,)), ((), ())), preferred_element_type=jnp.float32
     )

time: 68.4 us -> 67.5 us (0.987)
  blocking collectives: 7.67 us -> 32.7 us
  waiting for transfers between devices: 20.4 us -> 4.86 us
  starting transfers between devices: 20.8 us -> 12 us
  matrix products: 6.75 us -> 6.03 us
    all_to_all x0 -> x2, blocking collectives: none -> 25 us  [the longest x1 14.6 us: local(): complete = jnp.sum(lax.all_to_all(chunks, 'snp', 0, 0, tiled=True), axis=0)]
    all_to_all x2 -> x0, waiting for transfers between devices: 15.5 us -> none  [the longest x1 9.16 us: local(): complete = jnp.sum(lax.all_to_all(chunks, 'snp', 0, 0, tiled=True), axis=0)]
    all_to_all x2 -> x0, starting transfers between devices: 8.81 us -> none  [the longest x1 5.32 us: local(): complete = jnp.sum(lax.all_to_all(chunks, 'snp', 0, 0, tiled=True), axis=0)]
    add x1 -> x0, other arithmetic: 0.72 us -> none  [local(): weights_all = alpha1[:, None] * beta_all + alpha2[:, None] * direction]
    dot_general x1, matrix products: 1.47 us -> 0.76 us  [local(): lax.dot_general(rounded, genotypes, (((1,), (1,)), ((), ())), preferred_e...]
  transfers between devices with their start and end apart: 5 -> 3, of which waited for: 4 -> 2; matrix products, arithmetic and copies ran while one was open for 1% -> 0% of each run, Pallas kernels for 0% -> 0%
where the time goes in v11:
time: 67.5 us; the launch traced here: 67.1 us
  blocking collectives  32.7 us (48%)
  starting transfers between devices  12 us (18%)
  other arithmetic  6.99 us (10%)
  matrix products  6.03 us (9%)
  waiting for transfers between devices  4.86 us (7%)
  local copies, waits for them, and re-layouts  3.55 us (5%)
  between operations  0.99 us (1%)
    all_to_all x1, blocking collectives, local(): complete = jnp.sum(lax.all_to_all(chunks, 'snp', 0, 0, tiled=True), axis=0)  14.6 us
    all_to_all x1, blocking collectives, local(): every = lax.all_to_all(sent, ('ind', 'snp'), 0, 0, tiled=True)  10.4 us
    all_gather x1, blocking collectives, local(): lax.all_gather(jnp.stack([beta_hat, image]), 'ind', axis=1, tiled=True)  7.67 us
    all_to_all x1, starting transfers between devices, all_sum(): return jnp.sum(lax.all_to_all(sent, axes, 0, 0, tiled=True), axis=0)  5.84 us
    ppermute x1, starting transfers between devices, spread_operator(): from_left = lax.ppermute(own[:, rows:], 'snp', forward)  4.9 us
    ppermute x1, waiting for transfers between devices, spread_operator(): from_right = lax.ppermute(own[:, :2 * halo], 'snp', backward)  4.27 us
    dot_general x1, matrix products, spread_operator(): jnp.einsum('tbr,brk->btk', vector.reshape(traits, blocks_here, BLK), bloc...  3.38 us
    unnamed x19, local copies, waits for them, and re-layouts  2.1 us
  transfers between devices with their start and end apart: 3, of which 2 were waited for; matrix products, arithmetic and copies ran while one was open for 0% of the time, Pallas kernels for 0%

profile of v11, /device:TPU:0, one launch (start us, length us, event | category | flops | bytes accessed | tf_op | source)
XLA Modules:
  0.0 67.1 jit_solution(626376015054250110)
XLA Ops:
  0.6 0.0 copy-start
  0.7 0.8 %and_compare_fusion.6 = (pred[8]{0:T(512)(128)(4,1)S(1)}, s32[8]{0:T(128)S(1)}) fusion(s32[8]{0:T(128)} %param.7, s32[]{:T(128)S(6)} %mul.154), kind=kLoop, calls=%fused_computation.100 | loop fusion | flops 56 | bytes 76 | tf_op jit(solution)/shard_map/eq | solution.py:53
  1.5 3.4 %fusion.25 = f32[8,16,1024]{2,1,0:T(8,128)S(1)} fusion(f32[8,128,1024]{2,1,0:T(8,128)} %bitcast.143, f32[16,1024]{1,0:T(8,128)} %param.5), kind=kOutput, calls=%fused_computation.69 | convolution fusion | flops 100663296 | bytes 4784128 | tf_op jit(solution)/shard_map/tbr,brk->btk/dot_general | solution.py:46
  4.9 0.2 slice_select_fusion.6
  5.1 0.0 copy-start.3
  5.1 0.0 copy-start.2
  5.2 0.2 fusion
  5.4 0.2 fusion.1
  5.6 0.2 fusion.2
  5.8 0.2 fusion.3
  6.1 0.2 fusion.4
  6.3 0.2 fusion.5
  6.6 0.0 copy-done.2
  6.6 0.1 broadcast_multiply_fusion
  6.7 0.1 fusion.13
  6.8 4.9 %collective-permute-start = (f32[16,960]{1,0:T(8,128)S(1)}, f32[16,960]{1,0:T(8,128)S(1)}, u32[]{:S(2)}, u32[]{:S(2)}) collective-permute-start(f32[16,960]{1,0:T(8,128)S(1)} %get-tuple-element.28), channel_id=1, source_target_pairs={{0,4},{4,8},{8,12},{12,16},{16,20},{20,24},{24,28},{1,5},{5,9},{9,... | collective-permute-start | bytes 184328 | tf_op jit(solution)/shard_map/ppermute | solution.py:64
  11.7 1.3 %collective-permute-start.1 = (f32[16,960]{1,0:T(8,128)S(1)}, f32[16,960]{1,0:T(8,128)S(1)}, u32[]{:S(2)}, u32[]{:S(2)}) collective-permute-start(f32[16,960]{1,0:T(8,128)S(1)} %get-tuple-element.29), channel_id=1, source_target_pairs={{4,0},{8,4},{12,8},{16,12},{20,16},{24,20},{28,24},{5,1},{9,5},{13... | collective-permute-start | bytes 184328 | tf_op jit(solution)/shard_map/ppermute | solution.py:65
  13.0 0.6 collective-permute-done
  13.6 4.3 %collective-permute-done.1 = f32[16,960]{1,0:T(8,128)S(1)} collective-permute-done((f32[16,960]{1,0:T(8,128)S(1)}, f32[16,960]{1,0:T(8,128)S(1)}, u32[]{:S(2)}, u32[]{:S(2)}) %collective-permute-start.1) | collective-permute-done | bytes 61472 | tf_op jit(solution)/shard_map/ppermute | solution.py:65
  18.0 0.2 slice_select_fusion.5
  18.3 0.0 copy-start.1
  18.3 0.2 slice_select_fusion.4
  18.5 0.2 slice_select_fusion.3
  18.7 0.2 slice_select_fusion.2
  19.0 0.2 slice_select_fusion.1
  19.2 0.2 slice_select_fusion
  19.4 1.0 %copy-done.1 = f32[1024,1024]{1,0:T(8,128)S(1)} copy-done((f32[1024,1024]{1,0:T(8,128)S(1)}, f32[1024,1024]{1,0:T(8,128)}, u32[]{:S(2)}) %copy-start.1) | copy-done | bytes 4194328
  20.5 1.9 %convolution_bitcast_fusion.1 = f32[8,2,8,128]{3,2,1,0:T(8,128)S(1)} fusion(f32[8,128,1024]{2,1,0:T(8,128)S(1)} %bitcast.144, f32[8,16,1088]{2,1,0:T(8,128)S(1)} %slice_select_fusion, pred[8]{0:T(512)(128)(4,1)S(1)} %get-tuple-element.17), kind=kOutput, calls=%fused_computation.1 | convolution fusion | flops 100794368 | bytes 5308928 | tf_op jit(solution)/shard_map/btk,brk->tbr/dot_general | solution.py:36
  22.4 0.2 multiply_reduce_fusion.1
  22.6 0.1 dynamic_update_slice.5
  22.8 0.7 %reshape.124 = f32[32,1,256]{2,1,0:T(1,128)} reshape(f32[32,4,64]{2,1,0:T(4,128)S(1)} %broadcast_in_dim.148) | data formatting | bytes 65536
  23.5 5.8 %all-to-all-start = ((f32[32,1,256]{2,1,0:T(1,128)}), f32[32,1,256]{2,1,0:T(1,128)S(1)}, u32[]{:S(2)}, u32[]{:S(2)}) async-start(f32[32,1,256]{2,1,0:T(1,128)} %reshape.124), calls=%async_computation | async-start | bytes 65536 | tf_op jit(solution)/shard_map/all_to_all | solution.py:16
  29.4 7.7 %all_gather.3 = f32[2,64,1024]{2,1,0:T(8,128)S(1)} all-gather(f32[2,16,1024]{2,1,0:T(8,128)S(1)} %pad_maximum_fusion), channel_id=1, replica_groups=mesh['snp'=8,'ind'=4] {'ind'}, dimensions={1}, use_global_device_ids=true | all-gather | bytes 655360 | tf_op jit(solution)/shard_map/all_gather | solution.py:96
  37.1 0.0 all-to-all-done
  37.1 0.5 broadcast.171
  37.6 0.7 %reduce.3 = f32[32,256]{1,0:T(8,128)S(1)} reduce(f32[32,1,256]{2,1,0:T(1,128)S(1)} %all-to-all-done, f32[]{:T(128)} %broadcast.171), dimensions={1}, to_apply=%all_to_all.9.reduce_sub_computation | reduce | bytes 65540 | tf_op jit(solution)/shard_map/all_to_all | solution.py:16
  38.3 0.1 reshape.125
  38.5 0.2 fusion.33
  38.6 0.6 constant_dynamic-slice_fusion
  39.3 0.8 %convolution_bitcast_fusion = f32[8,8,8,128]{3,2,1,0:T(8,128)S(1)} fusion(bf16[64,1024]{1,0:T(8,128)(2,1)S(1)} %get-tuple-element.5, bf16[1024,1024]{1,0:T(8,128)(2,1)S(1)} %copy-done), kind=kOutput, calls=%fused_computation | convolution fusion | flops 134217728 | bytes 2490368 | tf_op jit(solution)/shard_map/dot_general | solution.py:112
  40.1 14.6 %all_to_all.15 = f32[8,64,128]{2,1,0:T(8,128)S(1)} all-to-all(f32[8,64,128]{2,1,0:T(8,128)S(1)} %bitcast.146), channel_id=1, replica_groups=mesh['snp'=8,'ind'=4] {'snp'}, dimensions={0} | all-to-all | bytes 524288 | tf_op jit(solution)/shard_map/all_to_all | solution.py:118
  54.6 0.1 fusion.32
  54.7 0.2 multiply_reduce_fusion.3
  55.0 0.1 reshape.126
  55.1 10.4 %all_to_all.16 = f32[32,1,128]{2,1,0:T(1,128)S(1)} all-to-all(f32[32,1,128]{2,1,0:T(1,128)S(1)} %reshape.126), channel_id=1, replica_groups=mesh['snp'=8,'ind'=4] {'ind','snp'}, dimensions={0} | all-to-all | bytes 32768 | tf_op jit(solution)/shard_map/all_to_all | solution.py:125
  65.5 0.7 %reduce.4 = f32[32,128]{1,0:T(8,128)S(1)} reduce(f32[32,1,128]{2,1,0:T(1,128)S(1)} %all_to_all.16, f32[]{:T(128)} %broadcast.171), dimensions={1}, to_apply=%all_to_all.11.reduce_sub_computation | reduce | bytes 32772 | tf_op jit(solution)/shard_map/all_to_all | solution.py:125
  66.2 0.1 reshape.127
  66.4 0.7 %subtract_multiply_fusion = f32[64,128]{1,0:T(8,128)} fusion(f32[64,128]{1,0:T(8,128)S(1)} %get-tuple-element.7, f32[64]{0:T(128)S(1)} %add_rsqrt_fusion, f32[64]{0:T(128)S(1)} %broadcast_multiply_fusion.2), kind=kLoop, calls=%fused_computation.76 | loop fusion | flops 16384 | bytes 66048 | tf_op jit(solution)/shard_map/mul | solution.py:131
  (32 shorter events, 0.5 us)
Async XLA Ops:
  0.6 38.6 %copy-start = (bf16[1024,1024]{1,0:T(8,128)(2,1)S(1)}, bf16[1024,1024]{1,0:T(8,128)(2,1)}, u32[]{:S(2)}) copy-start(bf16[1024,1024]{1,0:T(8,128)(2,1)} %param.9) | copy-start | bytes 6291460
  5.1 1.5 %copy-start.3 = (f32[16]{0:T(128)S(1)}, f32[16]{0:T(128)}, u32[]{:S(2)}) copy-start(f32[16]{0:T(128)} %param.8) | copy-start | bytes 196
  5.1 1.5 %copy-start.2 = (f32[16,1024]{1,0:T(8,128)S(1)}, f32[16,1024]{1,0:T(8,128)}, u32[]{:S(2)}) copy-start(f32[16,1024]{1,0:T(8,128)} %param.5) | copy-start | bytes 196612
  6.8 6.8 %collective-permute-start = (f32[16,960]{1,0:T(8,128)S(1)}, f32[16,960]{1,0:T(8,128)S(1)}, u32[]{:S(2)}, u32[]{:S(2)}) collective-permute-start(f32[16,960]{1,0:T(8,128)S(1)} %get-tuple-element.28), channel_id=1, source_target_pairs={{0,4},{4,8},{8,12},{12,16},{16,20},{20,24},{24,28},{1,5},{5,9},{9,... | collective-permute-start | bytes 184328 | tf_op jit(solution)/shard_map/ppermute | solution.py:64
  11.7 6.2 %collective-permute-start.1 = (f32[16,960]{1,0:T(8,128)S(1)}, f32[16,960]{1,0:T(8,128)S(1)}, u32[]{:S(2)}, u32[]{:S(2)}) collective-permute-start(f32[16,960]{1,0:T(8,128)S(1)} %get-tuple-element.29), channel_id=1, source_target_pairs={{4,0},{8,4},{12,8},{16,12},{20,16},{24,20},{28,24},{5,1},{9,5},{13... | collective-permute-start | bytes 184328 | tf_op jit(solution)/shard_map/ppermute | solution.py:65
  18.3 2.2 %copy-start.1 = (f32[1024,1024]{1,0:T(8,128)S(1)}, f32[1024,1024]{1,0:T(8,128)}, u32[]{:S(2)}) copy-start(f32[1024,1024]{1,0:T(8,128)} %param.6) | copy-start | bytes 12582916
  23.5 13.5 %all-to-all-start = ((f32[32,1,256]{2,1,0:T(1,128)}), f32[32,1,256]{2,1,0:T(1,128)S(1)}, u32[]{:S(2)}, u32[]{:S(2)}) async-start(f32[32,1,256]{2,1,0:T(1,128)} %reshape.124), calls=%async_computation | async-start | bytes 65536 | tf_op jit(solution)/shard_map/all_to_all | solution.py:16

commit v12 on v5

--- a/solution.py
+++ b/solution.py
@@ -34,7 +34,7 @@
     windows = windows_of(extended, shifts, band_cols, blocks_here)
     blocks = ld_band.reshape(blocks_here, BLK, band_cols)
     product = jnp.einsum("btk,brk->tbr", windows, blocks, precision=lax.Precision.HIGH)
-    return product.reshape(vector.shape) + ridge_shift[:, None] * vector
+    return product.reshape(vector.shape)
 
 
 def spread_operator(vector, ld_band, shifts, ridge_shift, halo):
@@ -63,7 +63,7 @@
     backward = [(target, source) for source, target in forward]
     from_left = lax.ppermute(own[:, rows:], "snp", forward)
     from_right = lax.ppermute(own[:, : 2 * halo], "snp", backward)
-    return own + jnp.pad(from_left, ((0, 0), (0, rows))) + jnp.pad(from_right, ((0, 0), (rows, 0)))
+    return own, jnp.pad(from_left, ((0, 0), (0, rows))), jnp.pad(from_right, ((0, 0), (rows, 0)))
 
 
 def local(beta_hat, ld_band, band_start, heritability, genotypes):
@@ -77,9 +77,13 @@
     shifts = offsets - jnp.arange(band_start.shape[0], dtype=jnp.int32) * BLK
 
     ridge_shift = M_GENOME / N_GWAS / heritability
-    extended = spread_operator(beta_hat, ld_band, shifts, ridge_shift, halo)
-    image = extended[:, halo : halo + rows_here]
-    image2 = apply_operator(extended, image, ld_band, shifts, ridge_shift)
+    own, left, right = spread_operator(beta_hat, ld_band, shifts, ridge_shift, halo)
+    early = own + left
+    image = (early + right)[:, halo : halo + rows_here]
+    image2 = (
+        apply_operator(early, image, ld_band, shifts, ridge_shift)
+        + apply_operator(right, image, ld_band, shifts, ridge_shift)
+    ) + ridge_shift[:, None] * image
 
     moments = jnp.stack(
         [

time: 67.3 us -> 70.6 us (1.049)
  matrix products: 6.03 us -> 7.96 us
  other arithmetic: 6.82 us -> 7.92 us
    dot_general x1 -> x2, matrix products: 1.9 us -> 3.82 us  [apply_operator(): jnp.einsum('btk,brk->tbr', windows, blocks, precision=lax.Precision.HIGH)]
    select_n x6, other arithmetic: 1.36 us -> 2.47 us  [windows_of(): wide = jnp.where(take, wide[:, :, step:], wide[:, :, :-step])]
    unnamed x17 -> x24, local copies, waits for them, and re-layouts: 1.29 us -> 1.65 us
where the time goes in v12:
time: 70.6 us; the launch traced here: 70.3 us
  blocking collectives  40.2 us (57%)
  matrix products  7.96 us (11%)
  other arithmetic  7.92 us (11%)
  starting transfers between devices  6.19 us (9%)
  waiting for transfers between devices  4.72 us (7%)
  local copies, waits for them, and re-layouts  2.32 us (3%)
  between operations  1.01 us (1%)
    all_to_all x1, blocking collectives, local(): complete = jnp.sum(lax.all_to_all(chunks, 'snp', 0, 0, tiled=True), axis=0)  12.1 us
    all_to_all x1, blocking collectives, all_sum(): return jnp.sum(lax.all_to_all(sent, axes, 0, 0, tiled=True), axis=0)  12.1 us
    all_to_all x1, blocking collectives, local(): every = lax.all_to_all(sent, ('ind', 'snp'), 0, 0, tiled=True)  10.5 us
    all_gather x1, blocking collectives, local(): lax.all_gather(weights.astype(jnp.bfloat16), 'ind', axis=0, tiled=True)  5.4 us
    ppermute x1, starting transfers between devices, spread_operator(): from_left = lax.ppermute(own[:, rows:], 'snp', forward)  4.9 us
    ppermute x1, waiting for transfers between devices, spread_operator(): from_right = lax.ppermute(own[:, :2 * halo], 'snp', backward)  4.13 us
    dot_general x2, matrix products, apply_operator(): jnp.einsum('btk,brk->tbr', windows, blocks, precision=lax.Precision.HIGH)  3.82 us
    dot_general x1, matrix products, spread_operator(): jnp.einsum('tbr,brk->btk', vector.reshape(traits, blocks_here, BLK), bloc...  3.38 us
  transfers between devices with their start and end apart: 2, of which 2 were waited for; matrix products, arithmetic and copies ran while one was open for 0% of the time, Pallas kernels for 0%

profile of v12, /device:TPU:0, one launch (start us, length us, event | category | flops | bytes accessed | tf_op | source)
XLA Modules:
  0.0 70.3 jit_solution(1063446668058222016)
XLA Ops:
  0.6 0.0 copy-start
  0.6 0.8 %and_compare_fusion.6 = (pred[8]{0:T(512)(128)(4,1)S(1)}, s32[8]{0:T(128)S(1)}) fusion(s32[8]{0:T(128)} %param.7, s32[]{:T(128)S(6)} %mul.147), kind=kLoop, calls=%fused_computation.128 | loop fusion | flops 56 | bytes 76 | tf_op jit(solution)/shard_map/eq | solution.py:53
  1.5 3.4 %fusion.40 = f32[8,16,1024]{2,1,0:T(8,128)S(1)} fusion(f32[8,128,1024]{2,1,0:T(8,128)} %bitcast.155, f32[16,1024]{1,0:T(8,128)} %param.5), kind=kOutput, calls=%fused_computation.96 | convolution fusion | flops 100663296 | bytes 4784128 | tf_op jit(solution)/shard_map/tbr,brk->btk/dot_general | solution.py:46
  4.9 0.2 slice_select_fusion.12
  5.1 0.0 copy-start.3
  5.1 0.0 copy-start.2
  5.2 0.2 fusion.1
  5.4 0.2 fusion.2
  5.6 0.2 fusion.3
  5.8 0.2 fusion.4
  6.1 0.2 fusion.5
  6.3 0.2 fusion.6
  6.6 0.0 copy-done.3
  6.6 0.0 copy-done.2
  6.6 0.1 broadcast_multiply_fusion
  6.7 0.1 fusion.12
  6.8 4.9 %collective-permute-start = (f32[16,960]{1,0:T(8,128)S(1)}, f32[16,960]{1,0:T(8,128)S(1)}, u32[]{:S(2)}, u32[]{:S(2)}) collective-permute-start(f32[16,960]{1,0:T(8,128)S(1)} %get-tuple-element.25), channel_id=1, source_target_pairs={{0,4},{4,8},{8,12},{12,16},{16,20},{20,24},{24,28},{1,5},{5,9},{9,... | collective-permute-start | bytes 184328 | tf_op jit(solution)/shard_map/ppermute | solution.py:64
  11.7 1.3 %collective-permute-start.1 = (f32[16,960]{1,0:T(8,128)S(1)}, f32[16,960]{1,0:T(8,128)S(1)}, u32[]{:S(2)}, u32[]{:S(2)}) collective-permute-start(f32[16,960]{1,0:T(8,128)S(1)} %get-tuple-element.24), channel_id=1, source_target_pairs={{4,0},{8,4},{12,8},{16,12},{20,16},{24,20},{28,24},{5,1},{9,5},{13... | collective-permute-start | bytes 184328 | tf_op jit(solution)/shard_map/ppermute | solution.py:65
  13.0 0.6 collective-permute-done
  13.8 4.1 %collective-permute-done.1 = f32[16,960]{1,0:T(8,128)S(1)} collective-permute-done((f32[16,960]{1,0:T(8,128)S(1)}, f32[16,960]{1,0:T(8,128)S(1)}, u32[]{:S(2)}, u32[]{:S(2)}) %collective-permute-start.1) | collective-permute-done | bytes 61472 | tf_op jit(solution)/shard_map/ppermute | solution.py:65
  18.0 0.4 slice_select_fusion.5
  18.4 0.4 slice_select_fusion.4
  18.8 0.4 slice_select_fusion.3
  19.3 0.4 slice_select_fusion.2
  19.7 0.0 copy-start.1
  19.7 0.4 slice_select_fusion.1
  20.1 0.4 slice_select_fusion
  20.5 1.3 %copy-done.1 = f32[1024,1024]{1,0:T(8,128)S(1)} copy-done((f32[1024,1024]{1,0:T(8,128)S(1)}, f32[1024,1024]{1,0:T(8,128)}, u32[]{:S(2)}) %copy-start.1) | copy-done | bytes 4194328
  21.9 1.9 %fusion.8 = f32[8,16,128]{2,1,0:T(8,128)S(1)} fusion(f32[8,128,1024]{2,1,0:T(8,128)S(1)} %bitcast.156, f32[8,16,1088]{2,1,0:T(8,128)S(1)} %get-tuple-element.30, pred[8]{0:T(512)(128)(4,1)S(1)} %get-tuple-element.14), kind=kOutput, calls=%fused_computation.31 | convolution fusion | flops 100794368 | bytes 5308928 | tf_op jit(solution)/shard_map/btk,brk->tbr/dot_general | solution.py:36
  23.8 1.9 %fusion = f32[8,2,8,128]{3,2,1,0:T(8,128)S(1)} fusion(f32[8,16,128]{2,1,0:T(8,128)S(1)} %fusion.8, f32[8,128,1024]{2,1,0:T(8,128)S(1)} %bitcast.157, f32[8,16,1088]{2,1,0:T(8,128)S(1)} %get-tuple-element.29, pred[8]{0:T(512)(128)(4,1)S(1)} %get-tuple-element.14), kind=kOutput, calls=%fused_computation.2 | convolution fusion | flops 100810752 | bytes 5374464 | tf_op jit(solution)/shard_map/btk,brk->tbr/dot_general | solution.py:36
  25.7 0.3 multiply_reduce_fusion.2
  26.0 12.1 %all_to_all.15 = f32[8,4,16]{2,1,0:T(4,128)S(1)} all-to-all(f32[8,4,16]{2,1,0:T(4,128)S(1)} %broadcast_in_dim.172), channel_id=1, replica_groups=mesh['snp'=8,'ind'=4] {'snp'}, dimensions={0} | all-to-all | bytes 4096 | tf_op jit(solution)/shard_map/all_to_all | solution.py:16
  38.1 0.7 %fusion.48 = (bf16[16,1024]{1,0:T(8,128)(2,1)S(1)}, f32[16,1024]{1,0:T(8,128)}) fusion(f32[16,1024]{1,0:T(8,128)S(1)} %copy-done.2, f32[16]{0:T(128)S(1)} %get-tuple-element.11, f32[16,1024]{1,0:T(8,128)S(1)} %get-tuple-element.13, f32[16]{0:T(128)S(1)} %get-tuple-element.10, f32[16]{0:T(128)S(1)} %get-tuple-element.12), kind=kLoop, calls=%fused_computation.134 | loop fusion | flops 131072 | bytes 229568 | tf_op jit(solution)/shard_map/convert_element_type | solution.py:108
  38.9 5.4 %all_gather.3 = bf16[64,1024]{1,0:T(8,128)(2,1)S(1)} all-gather(bf16[16,1024]{1,0:T(8,128)(2,1)S(1)} %get-tuple-element.8), channel_id=1, replica_groups=mesh['snp'=8,'ind'=4] {'ind'}, dimensions={0}, use_global_device_ids=true | all-gather | bytes 163840 | tf_op jit(solution)/shard_map/all_gather | solution.py:108
  44.3 0.0 copy-done
  44.3 0.8 %convolution_bitcast_fusion = f32[8,8,8,128]{3,2,1,0:T(8,128)S(1)} fusion(bf16[64,1024]{1,0:T(8,128)(2,1)S(1)} %all_gather.3, bf16[1024,1024]{1,0:T(8,128)(2,1)S(1)} %copy-done), kind=kOutput, calls=%fused_computation | convolution fusion | flops 134217728 | bytes 2490368 | tf_op jit(solution)/shard_map/dot_general | solution.py:109
  45.0 12.1 %all_to_all.16 = f32[8,64,128]{2,1,0:T(8,128)S(1)} all-to-all(f32[8,64,128]{2,1,0:T(8,128)S(1)} %bitcast.158), channel_id=1, replica_groups=mesh['snp'=8,'ind'=4] {'snp'}, dimensions={0} | all-to-all | bytes 524288 | tf_op jit(solution)/shard_map/all_to_all | solution.py:115
  57.2 0.1 fusion.47
  57.3 0.2 multiply_reduce_fusion.3
  57.5 0.1 reshape.120
  57.6 10.5 %all_to_all.17 = f32[32,1,128]{2,1,0:T(1,128)S(1)} all-to-all(f32[32,1,128]{2,1,0:T(1,128)S(1)} %reshape.120), channel_id=1, replica_groups=mesh['snp'=8,'ind'=4] {'ind','snp'}, dimensions={0} | all-to-all | bytes 32768 | tf_op jit(solution)/shard_map/all_to_all | solution.py:122
  68.2 0.5 broadcast.181
  68.7 0.7 reduce.3
  69.4 0.1 reshape.121
  69.6 0.7 %subtract_multiply_fusion = f32[64,128]{1,0:T(8,128)} fusion(f32[64,128]{1,0:T(8,128)S(1)} %get-tuple-element.3, f32[64]{0:T(128)S(1)} %add_rsqrt_fusion, f32[64]{0:T(128)S(1)} %broadcast_multiply_fusion.2), kind=kLoop, calls=%fused_computation.104 | loop fusion | flops 16384 | bytes 66048 | tf_op jit(solution)/shard_map/mul | solution.py:128
  (37 shorter events, 0.5 us)
Async XLA Ops:
  0.6 43.6 %copy-start = (bf16[1024,1024]{1,0:T(8,128)(2,1)S(1)}, bf16[1024,1024]{1,0:T(8,128)(2,1)}, u32[]{:S(2)}) copy-start(bf16[1024,1024]{1,0:T(8,128)(2,1)} %param.9) | copy-start | bytes 6291460
  5.1 1.5 %copy-start.3 = (f32[16]{0:T(128)S(1)}, f32[16]{0:T(128)}, u32[]{:S(2)}) copy-start(f32[16]{0:T(128)} %param.8) | copy-start | bytes 196
  5.1 1.5 %copy-start.2 = (f32[16,1024]{1,0:T(8,128)S(1)}, f32[16,1024]{1,0:T(8,128)}, u32[]{:S(2)}) copy-start(f32[16,1024]{1,0:T(8,128)} %param.5) | copy-start | bytes 196612
  6.8 6.8 %collective-permute-start = (f32[16,960]{1,0:T(8,128)S(1)}, f32[16,960]{1,0:T(8,128)S(1)}, u32[]{:S(2)}, u32[]{:S(2)}) collective-permute-start(f32[16,960]{1,0:T(8,128)S(1)} %get-tuple-element.25), channel_id=1, source_target_pairs={{0,4},{4,8},{8,12},{12,16},{16,20},{20,24},{24,28},{1,5},{5,9},{9,... | collective-permute-start | bytes 184328 | tf_op jit(solution)/shard_map/ppermute | solution.py:64
  11.7 6.2 %collective-permute-start.1 = (f32[16,960]{1,0:T(8,128)S(1)}, f32[16,960]{1,0:T(8,128)S(1)}, u32[]{:S(2)}, u32[]{:S(2)}) collective-permute-start(f32[16,960]{1,0:T(8,128)S(1)} %get-tuple-element.24), channel_id=1, source_target_pairs={{4,0},{8,4},{12,8},{16,12},{20,16},{24,20},{28,24},{5,1},{9,5},{13... | collective-permute-start | bytes 184328 | tf_op jit(solution)/shard_map/ppermute | solution.py:65
  19.7 2.2 %copy-start.1 = (f32[1024,1024]{1,0:T(8,128)S(1)}, f32[1024,1024]{1,0:T(8,128)}, u32[]{:S(2)}) copy-start(f32[1024,1024]{1,0:T(8,128)} %param.6) | copy-start | bytes 12582916

commit v13 on v5

--- a/solution.py
+++ b/solution.py
@@ -89,7 +89,7 @@
             jnp.sum(image * image2, axis=1),
         ]
     )
-    m0, m1, m2, m3 = all_sum(moments, "snp", n_snp)
+    m0, m1, m2, m3 = all_sum(moments.reshape(-1), "snp", n_snp).reshape(moments.shape)
 
     alpha1 = m0 / m1
     norm1 = alpha1 * alpha1 * m2 - m0

time: 67.3 us -> 67.3 us (level)
  no operation moved by 1% of the time
where the time goes in v13:
time: 67.3 us; the launch traced here: 67 us
  blocking collectives  40.1 us (60%)
  other arithmetic  6.88 us (10%)
  starting transfers between devices  6.19 us (9%)
  matrix products  6.03 us (9%)
  waiting for transfers between devices  4.86 us (7%)
  local copies, waits for them, and re-layouts  2.02 us (3%)
  between operations  0.93 us (1%)
    all_to_all x1, blocking collectives, local(): complete = jnp.sum(lax.all_to_all(chunks, 'snp', 0, 0, tiled=True), axis=0)  12.1 us
    all_to_all x1, blocking collectives, all_sum(): return jnp.sum(lax.all_to_all(sent, axes, 0, 0, tiled=True), axis=0)  12 us
    all_to_all x1, blocking collectives, local(): every = lax.all_to_all(sent, ('ind', 'snp'), 0, 0, tiled=True)  10.5 us
    all_gather x1, blocking collectives, local(): lax.all_gather(weights.astype(jnp.bfloat16), 'ind', axis=0, tiled=True)  5.4 us
    ppermute x1, starting transfers between devices, spread_operator(): from_left = lax.ppermute(own[:, rows:], 'snp', forward)  4.9 us
    ppermute x1, waiting for transfers between devices, spread_operator(): from_right = lax.ppermute(own[:, :2 * halo], 'snp', backward)  4.27 us
    dot_general x1, matrix products, spread_operator(): jnp.einsum('tbr,brk->btk', vector.reshape(traits, blocks_here, BLK), bloc...  3.38 us
    dot_general x1, matrix products, apply_operator(): jnp.einsum('btk,brk->tbr', windows, blocks, precision=lax.Precision.HIGH)  1.9 us
  transfers between devices with their start and end apart: 2, of which 2 were waited for; matrix products, arithmetic and copies ran while one was open for 0% of the time, Pallas kernels for 0%

profile of v13, /device:TPU:0, one launch (start us, length us, event | category | flops | bytes accessed | tf_op | source)
XLA Modules:
  0.0 67.0 jit_solution(1355774872934363092)
XLA Ops:
  0.6 0.0 copy-start
  0.6 0.8 %and_compare_fusion.6 = (pred[8]{0:T(512)(128)(4,1)S(1)}, s32[8]{0:T(128)S(1)}) fusion(s32[8]{0:T(128)} %param.7, s32[]{:T(128)S(6)} %mul.109), kind=kLoop, calls=%fused_computation.84 | loop fusion | flops 56 | bytes 76 | tf_op jit(solution)/shard_map/eq | solution.py:53
  1.5 3.4 %fusion.20 = f32[8,16,1024]{2,1,0:T(8,128)S(1)} fusion(f32[8,128,1024]{2,1,0:T(8,128)} %bitcast.87, f32[16,1024]{1,0:T(8,128)} %param.5), kind=kOutput, calls=%fused_computation.61 | convolution fusion | flops 100663296 | bytes 4784128 | tf_op jit(solution)/shard_map/tbr,brk->btk/dot_general | solution.py:46
  4.9 0.2 slice_select_fusion.6
  5.1 0.0 copy-start.3
  5.1 0.0 copy-start.2
  5.2 0.2 fusion
  5.4 0.2 fusion.1
  5.6 0.2 fusion.2
  5.8 0.2 fusion.3
  6.1 0.2 fusion.4
  6.3 0.2 fusion.5
  6.6 0.0 copy-done.3
  6.6 0.0 copy-done.2
  6.6 0.1 broadcast_multiply_fusion
  6.7 0.1 fusion.8
  6.8 4.9 %collective-permute-start = (f32[16,960]{1,0:T(8,128)S(1)}, f32[16,960]{1,0:T(8,128)S(1)}, u32[]{:S(2)}, u32[]{:S(2)}) collective-permute-start(f32[16,960]{1,0:T(8,128)S(1)} %get-tuple-element.23), channel_id=1, source_target_pairs={{0,4},{4,8},{8,12},{12,16},{16,20},{20,24},{24,28},{1,5},{5,9},{9,... | collective-permute-start | bytes 184328 | tf_op jit(solution)/shard_map/ppermute | solution.py:64
  11.7 1.3 %collective-permute-start.1 = (f32[16,960]{1,0:T(8,128)S(1)}, f32[16,960]{1,0:T(8,128)S(1)}, u32[]{:S(2)}, u32[]{:S(2)}) collective-permute-start(f32[16,960]{1,0:T(8,128)S(1)} %get-tuple-element.24), channel_id=1, source_target_pairs={{4,0},{8,4},{12,8},{16,12},{20,16},{24,20},{28,24},{5,1},{9,5},{13... | collective-permute-start | bytes 184328 | tf_op jit(solution)/shard_map/ppermute | solution.py:65
  13.0 0.6 collective-permute-done
  13.6 4.3 %collective-permute-done.1 = f32[16,960]{1,0:T(8,128)S(1)} collective-permute-done((f32[16,960]{1,0:T(8,128)S(1)}, f32[16,960]{1,0:T(8,128)S(1)}, u32[]{:S(2)}, u32[]{:S(2)}) %collective-permute-start.1) | collective-permute-done | bytes 61472 | tf_op jit(solution)/shard_map/ppermute | solution.py:65
  18.0 0.2 slice_select_fusion.5
  18.3 0.0 copy-start.1
  18.3 0.2 slice_select_fusion.4
  18.5 0.2 slice_select_fusion.3
  18.7 0.2 slice_select_fusion.2
  19.0 0.2 slice_select_fusion.1
  19.2 0.2 slice_select_fusion
  19.4 1.0 %copy-done.1 = f32[1024,1024]{1,0:T(8,128)S(1)} copy-done((f32[1024,1024]{1,0:T(8,128)S(1)}, f32[1024,1024]{1,0:T(8,128)}, u32[]{:S(2)}) %copy-start.1) | copy-done | bytes 4194328
  20.5 1.9 %convolution_bitcast_fusion.1 = f32[8,2,8,128]{3,2,1,0:T(8,128)S(1)} fusion(f32[8,128,1024]{2,1,0:T(8,128)S(1)} %bitcast.88, f32[8,16,1088]{2,1,0:T(8,128)S(1)} %slice_select_fusion, pred[8]{0:T(512)(128)(4,1)S(1)} %get-tuple-element.13), kind=kOutput, calls=%fused_computation.1 | convolution fusion | flops 100794368 | bytes 5308928 | tf_op jit(solution)/shard_map/btk,brk->tbr/dot_general | solution.py:36
  22.4 0.2 multiply_reduce_fusion.1
  22.6 0.1 broadcast_in_dim.145
  22.7 12.0 %all_to_all.16 = f32[8,1,64]{2,1,0:T(1,128)S(1)} all-to-all(f32[8,1,64]{2,1,0:T(1,128)S(1)} %broadcast_in_dim.146), channel_id=1, replica_groups=mesh['snp'=8,'ind'=4] {'snp'}, dimensions={0} | all-to-all | bytes 4096 | tf_op jit(solution)/shard_map/all_to_all | solution.py:16
  34.7 0.1 add_divide_fusion
  34.8 0.7 %fusion.25 = (bf16[16,1024]{1,0:T(8,128)(2,1)S(1)}, f32[16,1024]{1,0:T(8,128)}) fusion(f32[16,1024]{1,0:T(8,128)S(1)} %copy-done.2, f32[16]{0:T(128)S(1)} %get-tuple-element.11, f32[16,1984]{1,0:T(8,128)S(1)} %pad_add_fusion.6, f32[16]{0:T(128)S(1)} %get-tuple-element.10, f32[16]{0:T(128)S(1)} %get-tuple-element.12), kind=kLoop, calls=%fused_computation.92 | loop fusion | flops 131072 | bytes 229568 | tf_op jit(solution)/shard_map/convert_element_type | solution.py:104
  35.6 5.4 %all_gather.3 = bf16[64,1024]{1,0:T(8,128)(2,1)S(1)} all-gather(bf16[16,1024]{1,0:T(8,128)(2,1)S(1)} %get-tuple-element.8), channel_id=1, replica_groups=mesh['snp'=8,'ind'=4] {'ind'}, dimensions={0}, use_global_device_ids=true | all-gather | bytes 163840 | tf_op jit(solution)/shard_map/all_gather | solution.py:104
  41.0 0.0 copy-done
  41.0 0.8 %convolution_bitcast_fusion = f32[8,8,8,128]{3,2,1,0:T(8,128)S(1)} fusion(bf16[64,1024]{1,0:T(8,128)(2,1)S(1)} %all_gather.3, bf16[1024,1024]{1,0:T(8,128)(2,1)S(1)} %copy-done), kind=kOutput, calls=%fused_computation | convolution fusion | flops 134217728 | bytes 2490368 | tf_op jit(solution)/shard_map/dot_general | solution.py:105
  41.8 12.1 %all_to_all.17 = f32[8,64,128]{2,1,0:T(8,128)S(1)} all-to-all(f32[8,64,128]{2,1,0:T(8,128)S(1)} %bitcast.89), channel_id=1, replica_groups=mesh['snp'=8,'ind'=4] {'snp'}, dimensions={0} | all-to-all | bytes 524288 | tf_op jit(solution)/shard_map/all_to_all | solution.py:111
  53.9 0.1 fusion.24
  54.0 0.2 multiply_reduce_fusion.3
  54.2 0.1 reshape.77
  54.3 10.5 %all_to_all.18 = f32[32,1,128]{2,1,0:T(1,128)S(1)} all-to-all(f32[32,1,128]{2,1,0:T(1,128)S(1)} %reshape.77), channel_id=1, replica_groups=mesh['snp'=8,'ind'=4] {'ind','snp'}, dimensions={0} | all-to-all | bytes 32768 | tf_op jit(solution)/shard_map/all_to_all | solution.py:118
  64.9 0.5 broadcast.176
  65.4 0.7 %reduce.4 = f32[32,128]{1,0:T(8,128)S(1)} reduce(f32[32,1,128]{2,1,0:T(1,128)S(1)} %all_to_all.18, f32[]{:T(128)} %broadcast.176), dimensions={1}, to_apply=%all_to_all.12.reduce_sub_computation | reduce | bytes 32772 | tf_op jit(solution)/shard_map/all_to_all | solution.py:118
  66.1 0.1 reshape.78
  66.3 0.7 %subtract_multiply_fusion = f32[64,128]{1,0:T(8,128)} fusion(f32[64,128]{1,0:T(8,128)S(1)} %get-tuple-element.3, f32[64]{0:T(128)S(1)} %add_rsqrt_fusion, f32[64]{0:T(128)S(1)} %broadcast_multiply_fusion.2), kind=kLoop, calls=%fused_computation.68 | loop fusion | flops 16384 | bytes 66048 | tf_op jit(solution)/shard_map/mul | solution.py:124
  (27 shorter events, 0.4 us)
Async XLA Ops:
  0.6 40.3 %copy-start = (bf16[1024,1024]{1,0:T(8,128)(2,1)S(1)}, bf16[1024,1024]{1,0:T(8,128)(2,1)}, u32[]{:S(2)}) copy-start(bf16[1024,1024]{1,0:T(8,128)(2,1)} %param.9) | copy-start | bytes 6291460
  5.1 1.5 %copy-start.3 = (f32[16]{0:T(128)S(1)}, f32[16]{0:T(128)}, u32[]{:S(2)}) copy-start(f32[16]{0:T(128)} %param.8) | copy-start | bytes 196
  5.1 1.5 %copy-start.2 = (f32[16,1024]{1,0:T(8,128)S(1)}, f32[16,1024]{1,0:T(8,128)}, u32[]{:S(2)}) copy-start(f32[16,1024]{1,0:T(8,128)} %param.5) | copy-start | bytes 196612
  6.8 6.8 %collective-permute-start = (f32[16,960]{1,0:T(8,128)S(1)}, f32[16,960]{1,0:T(8,128)S(1)}, u32[]{:S(2)}, u32[]{:S(2)}) collective-permute-start(f32[16,960]{1,0:T(8,128)S(1)} %get-tuple-element.23), channel_id=1, source_target_pairs={{0,4},{4,8},{8,12},{12,16},{16,20},{20,24},{24,28},{1,5},{5,9},{9,... | collective-permute-start | bytes 184328 | tf_op jit(solution)/shard_map/ppermute | solution.py:64
  11.7 6.2 %collective-permute-start.1 = (f32[16,960]{1,0:T(8,128)S(1)}, f32[16,960]{1,0:T(8,128)S(1)}, u32[]{:S(2)}, u32[]{:S(2)}) collective-permute-start(f32[16,960]{1,0:T(8,128)S(1)} %get-tuple-element.24), channel_id=1, source_target_pairs={{4,0},{8,4},{12,8},{16,12},{20,16},{24,20},{28,24},{5,1},{9,5},{13... | collective-permute-start | bytes 184328 | tf_op jit(solution)/shard_map/ppermute | solution.py:65
  18.3 2.2 %copy-start.1 = (f32[1024,1024]{1,0:T(8,128)S(1)}, f32[1024,1024]{1,0:T(8,128)}, u32[]{:S(2)}) copy-start(f32[1024,1024]{1,0:T(8,128)} %param.6) | copy-start | bytes 12582916

commit v14 on v5

--- a/solution.py
+++ b/solution.py
@@ -47,6 +47,7 @@
         "tbr,brk->btk", vector.reshape(traits, blocks_here, BLK), blocks,
         precision=lax.Precision.HIGH,
     )
+    pieces, shifts = lax.optimization_barrier((pieces, shifts))
     wide = jnp.pad(pieces, ((0, 0), (0, 0), (0, span - band_cols)))
     for bit in range(SHIFT_BITS):
         step = 1 << bit
@@ -63,7 +64,8 @@
     backward = [(target, source) for source, target in forward]
     from_left = lax.ppermute(own[:, rows:], "snp", forward)
     from_right = lax.ppermute(own[:, : 2 * halo], "snp", backward)
-    return own + jnp.pad(from_left, ((0, 0), (0, rows))) + jnp.pad(from_right, ((0, 0), (rows, 0)))
+    total = own + jnp.pad(from_left, ((0, 0), (0, rows))) + jnp.pad(from_right, ((0, 0), (rows, 0)))
+    return total, shifts
 
 
 def local(beta_hat, ld_band, band_start, heritability, genotypes):
@@ -77,7 +79,7 @@
     shifts = offsets - jnp.arange(band_start.shape[0], dtype=jnp.int32) * BLK
 
     ridge_shift = M_GENOME / N_GWAS / heritability
-    extended = spread_operator(beta_hat, ld_band, shifts, ridge_shift, halo)
+    extended, shifts = spread_operator(beta_hat, ld_band, shifts, ridge_shift, halo)
     image = extended[:, halo : halo + rows_here]
     image2 = apply_operator(extended, image, ld_band, shifts, ridge_shift)
 

time: 67.3 us -> 66.6 us (0.990)
  other arithmetic: 6.82 us -> 6.01 us
    eq x2 -> x1, other arithmetic: 0.82 us -> 0.01 us  [spread_operator(): take = (shifts >> bit & 1)[:, None, None] == 1]
where the time goes in v14:
time: 66.6 us; the launch traced here: 66.3 us
  blocking collectives  40.2 us (60%)
  starting transfers between devices  6.19 us (9%)
  matrix products  6.17 us (9%)
  other arithmetic  6.01 us (9%)
  waiting for transfers between devices  4.86 us (7%)
  local copies, waits for them, and re-layouts  1.94 us (3%)
  between operations  0.96 us (1%)
    all_to_all x1, blocking collectives, local(): complete = jnp.sum(lax.all_to_all(chunks, 'snp', 0, 0, tiled=True), axis=0)  12.1 us
    all_to_all x1, blocking collectives, all_sum(): return jnp.sum(lax.all_to_all(sent, axes, 0, 0, tiled=True), axis=0)  12.1 us
    all_to_all x1, blocking collectives, local(): every = lax.all_to_all(sent, ('ind', 'snp'), 0, 0, tiled=True)  10.5 us
    all_gather x1, blocking collectives, local(): lax.all_gather(weights.astype(jnp.bfloat16), 'ind', axis=0, tiled=True)  5.4 us
    ppermute x1, starting transfers between devices, spread_operator(): from_left = lax.ppermute(own[:, rows:], 'snp', forward)  4.9 us
    ppermute x1, waiting for transfers between devices, spread_operator(): from_right = lax.ppermute(own[:, :2 * halo], 'snp', backward)  4.27 us
    dot_general x1, matrix products, spread_operator(): jnp.einsum('tbr,brk->btk', vector.reshape(traits, blocks_here, BLK), bloc...  3.51 us
    dot_general x1, matrix products, apply_operator(): jnp.einsum('btk,brk->tbr', windows, blocks, precision=lax.Precision.HIGH)  1.9 us
  transfers between devices with their start and end apart: 2, of which 2 were waited for; matrix products, arithmetic and copies ran while one was open for 0% of the time, Pallas kernels for 0%

profile of v14, /device:TPU:0, one launch (start us, length us, event | category | flops | bytes accessed | tf_op | source)
XLA Modules:
  0.0 66.3 jit_solution(17013956815867235051)
XLA Ops:
  0.6 0.0 copy-start
  0.6 0.0 copy-start.3
  0.7 3.5 %fusion.20 = f32[8,16,1024]{2,1,0:T(8,128)S(1)} fusion(f32[8,128,1024]{2,1,0:T(8,128)} %bitcast.122, f32[16,1024]{1,0:T(8,128)} %param.5), kind=kOutput, calls=%fused_computation.61 | convolution fusion | flops 100663296 | bytes 4784128 | tf_op jit(solution)/shard_map/tbr,brk->btk/dot_general | solution.py:46
  4.2 0.0 copy-done.3
  4.3 0.2 slice_select_fusion.6
  4.5 0.0 copy-start.4
  4.5 0.0 copy-start.2
  4.5 0.2 fusion
  4.7 0.2 fusion.1
  5.0 0.2 fusion.2
  5.2 0.2 fusion.3
  5.4 0.2 fusion.4
  5.7 0.2 fusion.5
  5.9 0.0 copy-done.4
  6.0 0.0 copy-done.2
  6.0 0.1 broadcast_multiply_fusion
  6.1 0.1 fusion.8
  6.2 4.9 %collective-permute-start = (f32[16,960]{1,0:T(8,128)S(1)}, f32[16,960]{1,0:T(8,128)S(1)}, u32[]{:S(2)}, u32[]{:S(2)}) collective-permute-start(f32[16,960]{1,0:T(8,128)S(1)} %get-tuple-element.25), channel_id=1, source_target_pairs={{0,4},{4,8},{8,12},{12,16},{16,20},{20,24},{24,28},{1,5},{5,9},{9,... | collective-permute-start | bytes 184328 | tf_op jit(solution)/shard_map/ppermute | solution.py:65
  11.1 1.3 %collective-permute-start.1 = (f32[16,960]{1,0:T(8,128)S(1)}, f32[16,960]{1,0:T(8,128)S(1)}, u32[]{:S(2)}, u32[]{:S(2)}) collective-permute-start(f32[16,960]{1,0:T(8,128)S(1)} %get-tuple-element.26), channel_id=1, source_target_pairs={{4,0},{8,4},{12,8},{16,12},{20,16},{24,20},{28,24},{5,1},{9,5},{13... | collective-permute-start | bytes 184328 | tf_op jit(solution)/shard_map/ppermute | solution.py:66
  12.4 0.6 collective-permute-done
  13.0 4.3 %collective-permute-done.1 = f32[16,960]{1,0:T(8,128)S(1)} collective-permute-done((f32[16,960]{1,0:T(8,128)S(1)}, f32[16,960]{1,0:T(8,128)S(1)}, u32[]{:S(2)}, u32[]{:S(2)}) %collective-permute-start.1) | collective-permute-done | bytes 61472 | tf_op jit(solution)/shard_map/ppermute | solution.py:66
  17.4 0.2 slice_select_fusion.5
  17.6 0.0 copy-start.1
  17.6 0.2 slice_select_fusion.4
  17.9 0.2 slice_select_fusion.3
  18.1 0.2 slice_select_fusion.2
  18.3 0.2 slice_select_fusion.1
  18.6 0.2 slice_select_fusion
  18.8 1.0 %copy-done.1 = f32[1024,1024]{1,0:T(8,128)S(1)} copy-done((f32[1024,1024]{1,0:T(8,128)S(1)}, f32[1024,1024]{1,0:T(8,128)}, u32[]{:S(2)}) %copy-start.1) | copy-done | bytes 4194328
  19.8 1.9 %convolution_bitcast_fusion.1 = f32[8,2,8,128]{3,2,1,0:T(8,128)S(1)} fusion(f32[8,128,1024]{2,1,0:T(8,128)S(1)} %bitcast.123, f32[8,16,1088]{2,1,0:T(8,128)S(1)} %slice_select_fusion, pred[8]{0:T(512)(128)(4,1)S(1)} %get-tuple-element.30), kind=kOutput, calls=%fused_computation.1 | convolution fusion | flops 100794368 | bytes 5308928 | tf_op jit(solution)/shard_map/btk,brk->tbr/dot_general | solution.py:36
  21.7 0.2 multiply_reduce_fusion.1
  22.0 12.1 %all_to_all.15 = f32[8,4,16]{2,1,0:T(4,128)S(1)} all-to-all(f32[8,4,16]{2,1,0:T(4,128)S(1)} %broadcast_in_dim.144), channel_id=1, replica_groups=mesh['snp'=8,'ind'=4] {'snp'}, dimensions={0} | all-to-all | bytes 4096 | tf_op jit(solution)/shard_map/all_to_all | solution.py:16
  34.1 0.7 %fusion.28 = (bf16[16,1024]{1,0:T(8,128)(2,1)S(1)}, f32[16,1024]{1,0:T(8,128)}) fusion(f32[16,1024]{1,0:T(8,128)S(1)} %copy-done.2, f32[16]{0:T(128)S(1)} %get-tuple-element.15, f32[16,1984]{1,0:T(8,128)S(1)} %pad_add_fusion.6, f32[16]{0:T(128)S(1)} %get-tuple-element.14, f32[16]{0:T(128)S(1)} %get-tuple-element.16), kind=kLoop, calls=%fused_computation.98 | loop fusion | flops 131072 | bytes 229568 | tf_op jit(solution)/shard_map/convert_element_type | solution.py:106
  34.9 5.4 %all_gather.3 = bf16[64,1024]{1,0:T(8,128)(2,1)S(1)} all-gather(bf16[16,1024]{1,0:T(8,128)(2,1)S(1)} %get-tuple-element.12), channel_id=1, replica_groups=mesh['snp'=8,'ind'=4] {'ind'}, dimensions={0}, use_global_device_ids=true | all-gather | bytes 163840 | tf_op jit(solution)/shard_map/all_gather | solution.py:106
  40.3 0.0 copy-done
  40.3 0.8 %convolution_bitcast_fusion = f32[8,8,8,128]{3,2,1,0:T(8,128)S(1)} fusion(bf16[64,1024]{1,0:T(8,128)(2,1)S(1)} %all_gather.3, bf16[1024,1024]{1,0:T(8,128)(2,1)S(1)} %copy-done), kind=kOutput, calls=%fused_computation | convolution fusion | flops 134217728 | bytes 2490368 | tf_op jit(solution)/shard_map/dot_general | solution.py:107
  41.1 12.1 %all_to_all.16 = f32[8,64,128]{2,1,0:T(8,128)S(1)} all-to-all(f32[8,64,128]{2,1,0:T(8,128)S(1)} %bitcast.124), channel_id=1, replica_groups=mesh['snp'=8,'ind'=4] {'snp'}, dimensions={0} | all-to-all | bytes 524288 | tf_op jit(solution)/shard_map/all_to_all | solution.py:113
  53.2 0.1 fusion.27
  53.3 0.2 multiply_reduce_fusion.3
  53.5 0.1 reshape.120
  53.6 10.5 %all_to_all.17 = f32[32,1,128]{2,1,0:T(1,128)S(1)} all-to-all(f32[32,1,128]{2,1,0:T(1,128)S(1)} %reshape.120), channel_id=1, replica_groups=mesh['snp'=8,'ind'=4] {'ind','snp'}, dimensions={0} | all-to-all | bytes 32768 | tf_op jit(solution)/shard_map/all_to_all | solution.py:120
  64.2 0.5 broadcast.177
  64.7 0.7 %reduce.3 = f32[32,128]{1,0:T(8,128)S(1)} reduce(f32[32,1,128]{2,1,0:T(1,128)S(1)} %all_to_all.17, f32[]{:T(128)} %broadcast.177), dimensions={1}, to_apply=%all_to_all.11.reduce_sub_computation | reduce | bytes 32772 | tf_op jit(solution)/shard_map/all_to_all | solution.py:120
  65.4 0.1 reshape.121
  65.6 0.7 %subtract_multiply_fusion = f32[64,128]{1,0:T(8,128)} fusion(f32[64,128]{1,0:T(8,128)S(1)} %get-tuple-element.7, f32[64]{0:T(128)S(1)} %add_rsqrt_fusion, f32[64]{0:T(128)S(1)} %broadcast_multiply_fusion.2), kind=kLoop, calls=%fused_computation.68 | loop fusion | flops 16384 | bytes 66048 | tf_op jit(solution)/shard_map/mul | solution.py:126
  (29 shorter events, 0.4 us)
Async XLA Ops:
  0.6 39.6 %copy-start = (bf16[1024,1024]{1,0:T(8,128)(2,1)S(1)}, bf16[1024,1024]{1,0:T(8,128)(2,1)}, u32[]{:S(2)}) copy-start(bf16[1024,1024]{1,0:T(8,128)(2,1)} %param.9) | copy-start | bytes 6291460
  0.6 3.5 %copy-start.3 = (s32[8]{0:T(128)S(1)}, s32[8]{0:T(128)}, u32[]{:S(2)}) copy-start(s32[8]{0:T(128)} %param.7) | copy-start | bytes 100
  4.5 1.5 %copy-start.4 = (f32[16]{0:T(128)S(1)}, f32[16]{0:T(128)}, u32[]{:S(2)}) copy-start(f32[16]{0:T(128)} %param.8) | copy-start | bytes 196
  4.5 1.5 %copy-start.2 = (f32[16,1024]{1,0:T(8,128)S(1)}, f32[16,1024]{1,0:T(8,128)}, u32[]{:S(2)}) copy-start(f32[16,1024]{1,0:T(8,128)} %param.5) | copy-start | bytes 196612
  6.2 6.8 %collective-permute-start = (f32[16,960]{1,0:T(8,128)S(1)}, f32[16,960]{1,0:T(8,128)S(1)}, u32[]{:S(2)}, u32[]{:S(2)}) collective-permute-start(f32[16,960]{1,0:T(8,128)S(1)} %get-tuple-element.25), channel_id=1, source_target_pairs={{0,4},{4,8},{8,12},{12,16},{16,20},{20,24},{24,28},{1,5},{5,9},{9,... | collective-permute-start | bytes 184328 | tf_op jit(solution)/shard_map/ppermute | solution.py:65
  11.1 6.2 %collective-permute-start.1 = (f32[16,960]{1,0:T(8,128)S(1)}, f32[16,960]{1,0:T(8,128)S(1)}, u32[]{:S(2)}, u32[]{:S(2)}) collective-permute-start(f32[16,960]{1,0:T(8,128)S(1)} %get-tuple-element.26), channel_id=1, source_target_pairs={{4,0},{8,4},{12,8},{16,12},{20,16},{24,20},{28,24},{5,1},{9,5},{13... | collective-permute-start | bytes 184328 | tf_op jit(solution)/shard_map/ppermute | solution.py:66
  17.6 2.2 %copy-start.1 = (f32[1024,1024]{1,0:T(8,128)S(1)}, f32[1024,1024]{1,0:T(8,128)}, u32[]{:S(2)}) copy-start(f32[1024,1024]{1,0:T(8,128)} %param.6) | copy-start | bytes 12582916
